TPU v7x, 512 devices: a whole 4x4x16 slice. The times are simulated.
512 devices in a mesh: dp: 4 (over x), seq: 8 (over z_lo), tensor: 16 (over z_hi, y, core).
Axes of the slice: x: 4, y: 4, z: 16 (z_hi: 2, z_lo: 8; z = z_hi * 8 + z_lo), core: 2. Of those that a mesh axis runs over, the one named last changes fastest.
Arguments:
- features: bfloat16 [4096, 4096], P(('dp', 'seq'), 'tensor'), parts along dimension 0, may hold values from -6 to 6
- in_weight: bfloat16 [4096, 3, 4096], P('seq', None, 'tensor'), may hold values from -0.09375 to 0.09375
- short_taps: float32 [3, 7, 4096], P(None, None, 'tensor'), may hold values from -2.5 to 2.5
- decay_rates: float32 [16, 4096], P(None, 'tensor'), may hold values from 0.00048828125 to 0.1
- residues: float32 [16, 4096], P(None, 'tensor'), may hold values from -1.5 to 1.5
- skip_gain: float32 [4096], P('tensor'), may hold values from 0.5 to 1.5
- out_weight: bfloat16 [4096, 4096], P(None, 'tensor'), may hold values from -0.09375 to 0.09375
Outputs:
- mixed: bfloat16 [4096, 4096], P(('dp', 'seq'), 'tensor'), parts along dimension 0
There are 4 independent parts, one for each index of `dp`. A program takes and returns all parts, laid end to end along the dimension named above; an argument that names none is the same for every part. Nothing has to cross between parts.
All inputs are finite; a program needn't handle non-finite values.
Results may differ from a plain program's by a relative error of at most 0.007.
Values may be sent and summed in bfloat16 or wider, within the bound.
No kernel may reach another device: no remote copies, remote signals or barrier semaphores. Data moves between devices by JAX's collectives and lax.ppermute only.
A program may use at most 64 MiB of HBM per device.

v0:
```python
import jax
import jax.numpy as jnp
from jax import lax
from jax.sharding import PartitionSpec as P

precise = lax.Precision.HIGHEST
block_len = 64


def passed_along(value, axis, steps):
    count = lax.axis_size(axis)
    leading, last = (max(0, -steps), min(count, count - steps))
    return lax.ppermute(value, axis, [(source, source + steps) for source in range(leading, last)])


def prefix_2(part, axis, combine, identity):
    place = lax.axis_index(axis)
    gathered = jax.tree.map(lambda a: lax.all_gather(a, axis), part)
    state = jax.tree.map(lambda a, e: jnp.zeros_like(a) + jnp.asarray(e, a.dtype), part, identity)

    def one(turn, state):
        return combine(
            state, jax.tree.map(lambda a: lax.dynamic_index_in_dim(a, turn, 0, False), gathered)
        )

    return lax.fori_loop(0, place, one, state)


def body(features, in_weight, short_taps, decay_rates, residues, skip_gain, out_weight):
    tok_rows = features.shape[0]
    channels = in_weight.shape[2]
    taps_count = short_taps.shape[1]
    whole_feats = lax.all_gather(features, "tensor", axis=1, tiled=True)
    piece = lax.all_gather(in_weight, "seq", axis=0, tiled=True)
    count = piece.shape[0]
    projected = jnp.dot(
        whole_feats, piece.reshape(count, 3 * channels), preferred_element_type=jnp.float32
    )
    projected = projected.astype(jnp.bfloat16).reshape(tok_rows, 3, channels)
    rim_rows = taps_count - 1
    earlier = passed_along(projected[tok_rows - rim_rows :], "seq", 1)
    extended = jnp.concatenate([earlier, projected], axis=0).astype(jnp.float32)
    short = jnp.zeros((tok_rows, 3, channels), jnp.float32)
    for offset_lag in range(taps_count):
        short = (
            short
            + short_taps[:, offset_lag, :][None]
            * extended[rim_rows - offset_lag : rim_rows - offset_lag + tok_rows]
        )
    product = short[:, 1, :] * short[:, 2, :]
    blocks = tok_rows // block_len
    pieces = product.reshape(blocks, block_len, channels)
    amplitude = residues * jnp.sqrt(2.0 * decay_rates)
    offsets = jnp.arange(block_len).astype(jnp.float32)
    falloff = jnp.exp(-decay_rates[:, None, :] * offsets[None, :, None])
    kernel = jnp.einsum("mc,mtc->tc", amplitude, falloff, precision=precise)
    lag_grid = jnp.arange(block_len)[:, None] - jnp.arange(block_len)[None, :]
    select = (lag_grid[:, :, None] == jnp.arange(block_len)[None, None, :]).astype(jnp.float32)
    toeplitz = jnp.einsum("tsk,kc->tsc", select, kernel, precision=precise)
    inner = jnp.einsum("tsc,bsc->btc", toeplitz, pieces, precision=precise)
    toward_end = jnp.exp(-decay_rates[:, None, :] * (block_len - offsets)[None, :, None])
    block_sums = jnp.einsum("msc,bsc->bmc", toward_end, pieces, precision=precise)
    block_index = jnp.arange(blocks).astype(jnp.float32)
    carry_over = jnp.exp(
        -decay_rates[None] * (block_len * (blocks - 1 - block_index))[:, None, None]
    )
    device_sum = jnp.sum(carry_over * block_sums, axis=0)
    device_decay = jnp.exp(-decay_rates * float(tok_rows))

    def combine(earlier_pair, later_pair):
        return (earlier_pair[0] * later_pair[0], later_pair[0] * earlier_pair[1] + later_pair[1])

    prefix = prefix_2(
        (device_decay, device_sum),
        "seq",
        combine,
        (jnp.ones_like(device_decay), jnp.zeros_like(device_sum)),
    )
    entering = prefix[1]
    step_decay = jnp.exp(-decay_rates * float(block_len))

    def advance(state, block_sum):
        return (step_decay * state + block_sum, state)

    final_state, starts = lax.scan(advance, entering, block_sums)
    outer = jnp.einsum("mic,bmc->bic", amplitude[:, None, :] * falloff, starts, precision=precise)
    conv = (inner + outer).reshape(tok_rows, channels)
    gated = (short[:, 0, :] * (conv + skip_gain[None, :] * product)).astype(jnp.bfloat16)
    mixed = jnp.dot(
        lax.all_gather(gated, "tensor", axis=1, tiled=True),
        out_weight,
        preferred_element_type=jnp.float32,
    )
    return mixed.astype(jnp.bfloat16)


def solution(mesh):
    in_specs = (
        P(("dp", "seq"), "tensor"),
        P("seq", None, "tensor"),
        P(None, None, "tensor"),
        P(None, "tensor"),
        P(None, "tensor"),
        P("tensor"),
        P(None, "tensor"),
    )
    out_specs = P(("dp", "seq"), "tensor")
    return jax.shard_map(body, mesh=mesh, in_specs=in_specs, out_specs=out_specs, check_vma=False)
```

profile of v0, /device:TPU:1, one launch (start us, length us, event | category | flops | bytes accessed | tf_op | source)
XLA Modules:
  0.0 453.0 jit_solution(18063631675276910231)
XLA Ops:
  6.5 0.0 copy-start
  6.5 0.0 all-gather.6.cloned.1.call-start
  6.6 0.7 all-gather.6.cloned.1.call-update
  7.3 0.0 all-gather.8.cloned.1.call-start
  7.3 2.3 copy.59
  9.7 0.0 all-gather.8.cloned.1.call-update
  9.7 0.0 all-gather.10.cloned.1.call-start
  9.7 0.0 copy-done.4
  9.7 0.0 copy-done.5
  9.8 0.1 copy.90
  9.9 0.1 copy.63
  10.0 0.0 copy-start.7
  10.0 0.5 subtract_multiply_fusion
  10.5 0.5 broadcast_subtract_fusion
  11.1 1.6 multiply_reduce_fusion
  12.7 0.0 copy-done.3
  12.8 3.8 fusion.5
  16.6 76.7 %all-gather.6.cloned.1.call-done = bf16[128,4096]{1,0:T(8,128)(2,1)} async-done(((bf16[128,256]{1,0:T(8,128)(2,1)}), bf16[128,4096]{1,0:T(8,128)(2,1)}) %all-gather.6.cloned.1.call-update) | async-done | bytes 1048592 | tf_op jit(solution)/shard_map/all_gather | solution.py:33
  93.3 135.5 %all-gather.8.cloned.1.call-done = bf16[4096,3,256]{0,2,1:T(8,128)(2,1)} async-done(((bf16[512,3,256]{0,2,1:T(8,128)(2,1)}), bf16[4096,3,256]{0,2,1:T(8,128)(2,1)}) %all-gather.8.cloned.1.call-update) | async-done | bytes 6291472 | tf_op jit(solution)/shard_map/all_gather | solution.py:34
  228.8 5.3 %convolution_convert_fusion = bf16[128,768]{1,0:T(8,128)(2,1)S(1)} fusion(bf16[128,4096]{1,0:T(8,128)(2,1)} %all-gather.6.cloned.1.call-done, bf16[4096,768]{0,1:T(8,128)(2,1)} %bitcast.70), kind=kOutput, calls=%fused_computation.13 | convolution fusion | flops 805404672 | bytes 7536640 | tf_op jit(solution)/shard_map/dot_general | solution.py:36
  234.2 0.2 copy.81
  234.4 1.3 collective-permute-start
  235.7 40.2 %all-gather = f32[128,256]{1,0:T(8,128)S(1)} all-gather(f32[16,256]{1,0:T(8,128)S(1)} %get-tuple-element.136), channel_id=2, replica_groups=mesh['dp'=4,'seq'=8,'tensor'=16] {'seq'}, dimensions={0}, use_global_device_ids=true | all-gather | bytes 147456 | tf_op jit(solution)/shard_map/all_gather | solution.py:18
  275.8 0.8 copy.70
  276.6 9.2 %copy.65 = f32[64,64,256]{1,0,2:T(8,128)} copy(f32[64,64,256]{2,1,0:T(8,128)} %fusion.5) | data formatting | bytes 8388608 | tf_op jit(solution)/shard_map/tsk,kc->tsc/dot_general | solution.py:59
  285.8 0.2 copy.61
  285.9 0.0 collective-permute-done
  285.9 0.2 maximum_convert_fusion
  286.1 1.5 fusion.21
  287.6 0.1 copy.62
  287.8 0.1 copy.64
  287.9 15.4 %fusion.32 = f32[256,2,64]{2,1,0:T(2,128)S(1)} fusion(f32[2,64,256]{1,0,2:T(2,128)S(1)} %copy.64, f32[64,64,256]{1,0,2:T(8,128)} %copy.65), kind=kOutput, calls=%fused_computation.61 | convolution fusion | flops 25165824 | bytes 4456448 | tf_op jit(solution)/shard_map/tsc,bsc->btc/dot_general | solution.py:60
  303.4 4.2 multiply_reduce_fusion.1
  307.6 1.0 copy.68
  308.6 39.9 %all-gather.1 = f32[128,256]{1,0:T(8,128)S(1)} all-gather(f32[16,256]{1,0:T(8,128)S(1)} %copy.68), channel_id=3, replica_groups=mesh['dp'=4,'seq'=8,'tensor'=16] {'seq'}, dimensions={0}, use_global_device_ids=true | all-gather | bytes 147456 | tf_op jit(solution)/shard_map/all_gather | solution.py:18
  348.5 0.1 copy.69
  348.6 1.2 while.25
  348.6 0.6 bitcast_dynamic-update-slice_fusion.2
  349.2 0.6 bitcast_dynamic-update-slice_fusion.2
  349.8 0.9 copy.71
  350.7 0.0 copy-start.6
  350.7 3.7 fusion.12
  354.5 0.1 copy.72
  354.6 0.1 copy.73
  354.7 0.7 fusion.28
  355.5 0.0 all-gather.10.cloned.1.call-update
  355.5 88.6 %all-gather.10.cloned.1.call-done = bf16[128,4096]{0,1:T(8,128)(2,1)} async-done(((bf16[128,256]{0,1:T(8,128)(2,1)}), bf16[128,4096]{0,1:T(8,128)(2,1)}) %all-gather.10.cloned.1.call-update) | async-done | bytes 1048592 | tf_op jit(solution)/shard_map/all_gather | solution.py:90
  444.1 2.4 convolution_convert_fusion.1
  (29 shorter events, 0.1 us)
Async XLA Ops:
  6.5 437.5 %copy-start = (bf16[4096,256]{1,0:T(8,128)(2,1)S(1)}, bf16[4096,256]{1,0:T(8,128)(2,1)}, u32[]{:S(2)}) copy-start(bf16[4096,256]{1,0:T(8,128)(2,1)} %param.17) | copy-start | bytes 6291460
  6.5 3.2 copy-start.4
  6.5 3.2 copy-start.5
  6.5 6.2 %copy-start.3 = (f32[3,7,256]{2,1,0:T(8,128)S(1)}, f32[3,7,256]{2,1,0:T(8,128)}, u32[]{:S(2)}) copy-start(f32[3,7,256]{2,1,0:T(8,128)} %param.13) | copy-start | bytes 64516
  6.5 86.7 %all-gather.6.cloned.1.call-start = ((), (), s32[]{:S(2)}) async-start(), calls=%async_computation | async-start | bytes 1114112 | tf_op jit(solution)/shard_map/all_gather | solution.py:33
  7.3 221.5 %all-gather.8.cloned.1.call-start = ((), (), s32[]{:S(2)}) async-start(), calls=%async_computation.1 | async-start | bytes 7077888 | tf_op jit(solution)/shard_map/all_gather | solution.py:34
  9.7 434.4 %all-gather.10.cloned.1.call-start = ((), (), s32[]{:S(2)}) async-start(), calls=%async_computation.2 | async-start | bytes 1114112 | tf_op jit(solution)/shard_map/all_gather | solution.py:90
  10.0 6.6 %copy-start.1 = (f32[16,256]{0,1:T(8,128)}, f32[16,256]{0,1:T(8,128)S(1)}, u32[]{:S(2)}) copy-start(f32[16,256]{0,1:T(8,128)S(1)} %copy.63) | copy-start | bytes 49156
  10.0 6.6 %copy-start.7 = (f32[64]{0:T(128)}, f32[64]{0:T(128)S(1)}, u32[]{:S(2)}) copy-start(f32[64]{0:T(128)S(1)} %iota_convert_fusion) | copy-start | bytes 772
  234.4 51.6 %collective-permute-start = (bf16[6,3,256]{0,2,1:T(8,128)(2,1)S(1)}, bf16[6,3,256]{0,2,1:T(8,128)(2,1)S(1)}, u32[]{:S(2)}, u32[]{:S(2)}) collective-permute-start(bf16[6,3,256]{0,2,1:T(8,128)(2,1)S(1)} %bitcast.76), channel_id=1, source_target_pairs={{0,16},{16,32},{32,48},{48,64},{64,80},{80,96},{96,112},{1,17},{17... | collective-permute-start | bytes 27656 | tf_op jit(solution)/shard_map/ppermute | solution.py:13
  287.9 15.5 %copy-start.2 = (f32[16,256]{0,1:T(8,128)S(1)}, f32[16,256]{0,1:T(8,128)}, u32[]{:S(2)}) copy-start(f32[16,256]{0,1:T(8,128)} %copy-done.1) | copy-start | bytes 49156
  287.9 15.4 %copy-start.8 = (f32[2]{0:T(128)S(1)}, f32[2]{0:T(128)}, u32[]{:S(2)}) copy-start(f32[2]{0:T(128)} %subtract_multiply_fusion) | copy-start | bytes 28
  287.9 15.4 %copy-start.9 = (f32[64]{0:T(128)S(1)}, f32[64]{0:T(128)}, u32[]{:S(2)}) copy-start(f32[64]{0:T(128)} %broadcast_subtract_fusion) | copy-start | bytes 772
  350.7 4.0 copy-start.6
Sparse Core Ops, SparseCore 0:
  10.5 82.7 all-gather.5
  95.4 133.4 all-gather.7
  355.6 88.4 all-gather.9
where the time goes:
time: 453 us
  waiting for transfers between devices  301 us (66%)
  blocking collectives  80.1 us (18%)
  matrix products  35 us (8%)
  local copies, waits for them, and re-layouts  16.5 us (4%)
  between operations  13.4 us (3%)
  other arithmetic  5.16 us (1%)
    all_gather x1, waiting for transfers between devices, body(): piece = lax.all_gather(in_weight, 'seq', axis=0, tiled=True)  136 us
    all_gather x1, waiting for transfers between devices, body(): lax.all_gather(gated, 'tensor', axis=1, tiled=True)  88.6 us
    all_gather x2, blocking collectives, prefix_2(): gathered = jax.tree.map(lambda a: lax.all_gather(a, axis), part)  80.1 us
    all_gather x1, waiting for transfers between devices, body(): whole_feats = lax.all_gather(features, 'tensor', axis=1, tiled=True)  76.7 us
    dot_general x1, matrix products, body(): inner = jnp.einsum('tsc,bsc->btc', toeplitz, pieces, precision=precise)  15.4 us
    dot_general x1, local copies, waits for them, and re-layouts, body(): toeplitz = jnp.einsum('tsk,kc->tsc', select, kernel, precision=precise)  9.17 us
  transfers between devices with their start and end apart: 4, of which 3 were waited for; matrix products, arithmetic and copies ran while one was open for 4% of the time, Pallas kernels for 0%

commit v1 on v0

--- a/solution.py
+++ b/solution.py
@@ -11,19 +11,6 @@
     count = lax.axis_size(axis)
     leading, last = (max(0, -steps), min(count, count - steps))
     return lax.ppermute(value, axis, [(source, source + steps) for source in range(leading, last)])
-
-
-def prefix_2(part, axis, combine, identity):
-    place = lax.axis_index(axis)
-    gathered = jax.tree.map(lambda a: lax.all_gather(a, axis), part)
-    state = jax.tree.map(lambda a, e: jnp.zeros_like(a) + jnp.asarray(e, a.dtype), part, identity)
-
-    def one(turn, state):
-        return combine(
-            state, jax.tree.map(lambda a: lax.dynamic_index_in_dim(a, turn, 0, False), gathered)
-        )
-
-    return lax.fori_loop(0, place, one, state)
 
 
 def body(features, in_weight, short_taps, decay_rates, residues, skip_gain, out_weight):
@@ -65,18 +52,16 @@
         -decay_rates[None] * (block_len * (blocks - 1 - block_index))[:, None, None]
     )
     device_sum = jnp.sum(carry_over * block_sums, axis=0)
-    device_decay = jnp.exp(-decay_rates * float(tok_rows))
-
-    def combine(earlier_pair, later_pair):
-        return (earlier_pair[0] * later_pair[0], later_pair[0] * earlier_pair[1] + later_pair[1])
-
-    prefix = prefix_2(
-        (device_decay, device_sum),
-        "seq",
-        combine,
-        (jnp.ones_like(device_decay), jnp.zeros_like(device_sum)),
+    place = lax.axis_index("seq")
+    gathered_sums = lax.all_gather(device_sum, "seq")
+    earlier_count = jnp.arange(gathered_sums.shape[0])
+    distance = (place - 1 - earlier_count).astype(jnp.float32)
+    weight = jnp.where(
+        (earlier_count < place)[:, None, None],
+        jnp.exp(-decay_rates[None] * (float(tok_rows) * jnp.maximum(distance, 0.0))[:, None, None]),
+        0.0,
     )
-    entering = prefix[1]
+    entering = jnp.sum(weight * gathered_sums, axis=0)
     step_decay = jnp.exp(-decay_rates * float(block_len))
 
     def advance(state, block_sum):

time: 453 us -> 405 us (0.89)
  blocking collectives: 80.1 us -> 40.2 us
  waiting for transfers between devices: 301 us -> 296 us
    all_gather x2 -> x1, blocking collectives: 80.1 us -> 40.2 us  [body(): gathered_sums = lax.all_gather(device_sum, 'seq')]
    all_gather x1, waiting for transfers between devices: 88.6 us -> 82.1 us  [body(): lax.all_gather(gated, 'tensor', axis=1, tiled=True)]
where the time goes in v1:
time: 405 us
  waiting for transfers between devices  296 us (73%)
  blocking collectives  40.2 us (10%)
  matrix products  34.9 us (9%)
  local copies, waits for them, and re-layouts  14.5 us (4%)
  between operations  13.4 us (3%)
  other arithmetic  4.23 us (1%)
    all_gather x1, waiting for transfers between devices, body(): piece = lax.all_gather(in_weight, 'seq', axis=0, tiled=True)  136 us
    all_gather x1, waiting for transfers between devices, body(): lax.all_gather(gated, 'tensor', axis=1, tiled=True)  82.1 us
    all_gather x1, waiting for transfers between devices, body(): whole_feats = lax.all_gather(features, 'tensor', axis=1, tiled=True)  77.7 us
    all_gather x1, blocking collectives, body(): gathered_sums = lax.all_gather(device_sum, 'seq')  40.2 us
    dot_general x1, matrix products, body(): inner = jnp.einsum('tsc,bsc->btc', toeplitz, pieces, precision=precise)  15.4 us
    dot_general x1, local copies, waits for them, and re-layouts, body(): toeplitz = jnp.einsum('tsk,kc->tsc', select, kernel, precision=precise)  9.15 us
  transfers between devices with their start and end apart: 4, of which 3 were waited for; matrix products, arithmetic and copies ran while one was open for 4% of the time, Pallas kernels for 0%

profile of v1, /device:TPU:1, one launch (start us, length us, event | category | flops | bytes accessed | tf_op | source)
XLA Modules:
  0.0 405.0 jit_solution(2613455563154956939)
XLA Ops:
  6.5 0.0 copy-start
  6.5 0.0 copy-start.2
  6.5 0.0 copy-start.3
  6.5 0.0 copy-start.1
  6.5 0.0 all-gather.5.cloned.1.call-start
  6.6 0.7 all-gather.5.cloned.1.call-update
  7.3 0.0 all-gather.7.cloned.1.call-start
  7.3 2.3 copy.59
  9.6 0.0 all-gather.7.cloned.1.call-update
  9.7 0.0 all-gather.9.cloned.1.call-start
  9.7 0.0 copy-done.2
  9.7 0.0 copy-done.3
  9.7 0.1 copy.63
  9.8 0.1 copy.90
  10.0 1.6 multiply_reduce_fusion
  11.6 0.0 copy-done.1
  11.7 3.8 fusion.5
  15.6 77.7 %all-gather.5.cloned.1.call-done = bf16[128,4096]{1,0:T(8,128)(2,1)} async-done(((bf16[128,256]{1,0:T(8,128)(2,1)}), bf16[128,4096]{1,0:T(8,128)(2,1)}) %all-gather.5.cloned.1.call-update) | async-done | bytes 1048592 | tf_op jit(solution)/shard_map/all_gather | solution.py:20
  93.3 135.5 %all-gather.7.cloned.1.call-done = bf16[4096,3,256]{0,2,1:T(8,128)(2,1)} async-done(((bf16[512,3,256]{0,2,1:T(8,128)(2,1)}), bf16[4096,3,256]{0,2,1:T(8,128)(2,1)}) %all-gather.7.cloned.1.call-update) | async-done | bytes 6291472 | tf_op jit(solution)/shard_map/all_gather | solution.py:21
  228.8 5.3 %convolution_convert_fusion = bf16[128,768]{1,0:T(8,128)(2,1)S(1)} fusion(bf16[128,4096]{1,0:T(8,128)(2,1)} %all-gather.5.cloned.1.call-done, bf16[4096,768]{0,1:T(8,128)(2,1)} %bitcast.59), kind=kOutput, calls=%fused_computation.11 | convolution fusion | flops 805404672 | bytes 7536640 | tf_op jit(solution)/shard_map/dot_general | solution.py:23
  234.2 0.2 copy.81
  234.4 1.5 collective-permute-start
  235.9 0.7 copy.70
  236.6 9.2 %copy.65 = f32[64,64,256]{1,0,2:T(8,128)} copy(f32[64,64,256]{2,1,0:T(8,128)} %fusion.5) | data formatting | bytes 8388608 | tf_op jit(solution)/shard_map/tsk,kc->tsc/dot_general | solution.py:46
  245.8 0.2 copy.61
  245.9 0.0 collective-permute-done
  246.0 0.2 maximum_convert_fusion
  246.1 1.5 fusion.21
  247.7 0.1 copy.62
  247.8 0.1 copy.64
  247.9 15.4 %fusion.32 = f32[256,2,64]{2,1,0:T(2,128)S(1)} fusion(f32[2,64,256]{1,0,2:T(2,128)S(1)} %copy.64, f32[64,64,256]{1,0,2:T(8,128)} %copy.65), kind=kOutput, calls=%fused_computation.61 | convolution fusion | flops 25165824 | bytes 4456448 | tf_op jit(solution)/shard_map/tsc,bsc->btc/dot_general | solution.py:47
  263.3 4.2 %multiply_reduce_fusion.1 = (f32[16,256]{0,1:T(8,128)}, f32[2,16,256]{1,0,2:T(2,128)S(1)}) fusion(f32[16,256]{0,1:T(8,128)S(1)} %copy.63, f32[2]{0:T(128)S(1)} %subtract_multiply_fusion, f32[2,64,256]{1,0,2:T(2,128)S(1)} %copy.64, f32[64]{0:T(128)S(1)} %broadcast_subtract_fusion), kind=kOutput, calls=%fused_computation.36 | convolution fusion | flops 6574080 | bytes 196872 | tf_op jit(solution)/shard_map/msc,bsc->bmc/dot_general | solution.py:49
  267.5 1.0 copy.68
  268.5 40.2 %all-gather = f32[128,256]{1,0:T(8,128)S(1)} all-gather(f32[16,256]{1,0:T(8,128)S(1)} %copy.68), channel_id=2, replica_groups=mesh['dp'=4,'seq'=8,'tensor'=16] {'seq'}, dimensions={0}, use_global_device_ids=true | all-gather | bytes 147456 | tf_op jit(solution)/shard_map/all_gather | solution.py:56
  308.7 0.1 copy.69
  308.8 0.1 multiply_reduce_fusion.2
  308.9 0.1 while.12
  309.0 0.1 copy.71
  309.2 0.0 copy-start.4
  309.2 3.7 fusion.12
  312.9 0.1 copy.72
  313.0 0.1 copy.73
  313.1 0.0 copy-done.4
  313.1 0.7 fusion.28
  313.9 0.0 all-gather.9.cloned.1.call-update
  313.9 82.1 %all-gather.9.cloned.1.call-done = bf16[128,4096]{0,1:T(8,128)(2,1)} async-done(((bf16[128,256]{0,1:T(8,128)(2,1)}), bf16[128,4096]{0,1:T(8,128)(2,1)}) %all-gather.9.cloned.1.call-update) | async-done | bytes 1048592 | tf_op jit(solution)/shard_map/all_gather | solution.py:75
  396.0 0.0 copy-done
  396.0 2.4 convolution_convert_fusion.1
  (19 shorter events, 0.1 us)
Async XLA Ops:
  6.5 389.5 %copy-start = (bf16[4096,256]{1,0:T(8,128)(2,1)S(1)}, bf16[4096,256]{1,0:T(8,128)(2,1)}, u32[]{:S(2)}) copy-start(bf16[4096,256]{1,0:T(8,128)(2,1)} %param.15) | copy-start | bytes 6291460
  6.5 3.2 copy-start.2
  6.5 3.2 copy-start.3
  6.5 5.1 %copy-start.1 = (f32[3,7,256]{2,1,0:T(8,128)S(1)}, f32[3,7,256]{2,1,0:T(8,128)}, u32[]{:S(2)}) copy-start(f32[3,7,256]{2,1,0:T(8,128)} %param.11) | copy-start | bytes 64516
  6.5 86.7 %all-gather.5.cloned.1.call-start = ((), (), s32[]{:S(2)}) async-start(), calls=%async_computation | async-start | bytes 1114112 | tf_op jit(solution)/shard_map/all_gather | solution.py:20
  7.3 221.6 %all-gather.7.cloned.1.call-start = ((), (), s32[]{:S(2)}) async-start(), calls=%async_computation.1 | async-start | bytes 7077888 | tf_op jit(solution)/shard_map/all_gather | solution.py:21
  9.7 386.4 %all-gather.9.cloned.1.call-start = ((), (), s32[]{:S(2)}) async-start(), calls=%async_computation.2 | async-start | bytes 1114112 | tf_op jit(solution)/shard_map/all_gather | solution.py:75
  234.4 11.6 %collective-permute-start = (bf16[6,3,256]{0,2,1:T(8,128)(2,1)S(1)}, bf16[6,3,256]{0,2,1:T(8,128)(2,1)S(1)}, u32[]{:S(2)}, u32[]{:S(2)}) collective-permute-start(bf16[6,3,256]{0,2,1:T(8,128)(2,1)S(1)} %bitcast.64), channel_id=1, source_target_pairs={{0,16},{16,32},{32,48},{48,64},{64,80},{80,96},{96,112},{1,17},{17... | collective-permute-start | bytes 27656 | tf_op jit(solution)/shard_map/ppermute | solution.py:13
  309.2 3.9 copy-start.4
Sparse Core Ops, SparseCore 0:
  10.5 82.7 all-gather.4
  95.4 133.4 all-gather.6
  314.0 81.9 all-gather.8

commit v2 on v1

v2 whole, which is shorter than its diff:
```python
import jax
import jax.numpy as jnp
from jax import lax
from jax.sharding import PartitionSpec as P

precise = lax.Precision.HIGHEST
block_len = 64


def gather_weight_rows(features, seq_n, ten_n, halves):
    rounds = []
    for j in range(seq_n * halves):
        i, h = j % seq_n, j // seq_n
        perm = []
        for s in range(seq_n):
            for a in range(seq_n):
                for b in range(halves):
                    src = ((a + i) % seq_n) * ten_n + s * halves + (b + h) % halves
                    perm.append((src, s * ten_n + a * halves + b))
        rounds.append(lax.ppermute(features, ("seq", "tensor"), perm))
    columns = [
        jnp.concatenate(rounds[h * seq_n : (h + 1) * seq_n], axis=0) for h in range(halves)
    ]
    return jnp.concatenate(columns, axis=1)


def body(features, in_weight, short_taps, decay_rates, residues, skip_gain, out_weight):
    seq_n = lax.axis_size("seq")
    ten_n = lax.axis_size("tensor")
    place = lax.axis_index("seq")
    lane = lax.axis_index("tensor")
    tok_rows, fcols = features.shape
    rows_here, branches, channels = in_weight.shape
    halves = rows_here // fcols
    sub = channels // seq_n
    length = tok_rows * seq_n
    taps_count = short_taps.shape[1]
    rotation = lane // halves
    half_of = lane % halves

    rows_of_feats = gather_weight_rows(features, seq_n, ten_n, halves)
    doubled = jnp.concatenate([in_weight, in_weight], axis=0)
    weight_rows = lax.dynamic_slice_in_dim(doubled, half_of * fcols, rows_here, axis=0)
    weight_rows = weight_rows.reshape(rows_here, branches, seq_n, sub)
    partial = jnp.einsum(
        "td,djgc->gtjc", rows_of_feats, weight_rows, preferred_element_type=jnp.float32
    )
    summed = lax.psum_scatter(partial.reshape(seq_n * length, -1), "seq", scatter_dimension=0, tiled=True)
    summed = jnp.roll(summed.reshape(length, branches, sub), rotation * tok_rows, axis=0)
    projected = lax.reduce_precision(summed, exponent_bits=8, mantissa_bits=7)

    taps = lax.dynamic_slice_in_dim(short_taps, place * sub, sub, axis=2)
    decay = lax.dynamic_slice_in_dim(decay_rates, place * sub, sub, axis=1)
    resid = lax.dynamic_slice_in_dim(residues, place * sub, sub, axis=1)
    skip = lax.dynamic_slice_in_dim(skip_gain, place * sub, sub, axis=0)

    rim_rows = taps_count - 1
    extended = jnp.concatenate(
        [jnp.zeros((rim_rows, branches, sub), jnp.float32), projected], axis=0
    )
    short = jnp.zeros((length, branches, sub), jnp.float32)
    for offset_lag in range(taps_count):
        short = (
            short
            + taps[:, offset_lag, :][None]
            * extended[rim_rows - offset_lag : rim_rows - offset_lag + length]
        )
    product = short[:, 1, :] * short[:, 2, :]
    blocks = length // block_len
    pieces = product.reshape(blocks, block_len, sub)
    amplitude = resid * jnp.sqrt(2.0 * decay)
    offsets = jnp.arange(block_len).astype(jnp.float32)
    falloff = jnp.exp(-decay[:, None, :] * offsets[None, :, None])
    kernel = jnp.einsum("mc,mtc->tc", amplitude, falloff, precision=precise)
    lag_grid = jnp.arange(block_len)[:, None] - jnp.arange(block_len)[None, :]
    select = (lag_grid[:, :, None] == jnp.arange(block_len)[None, None, :]).astype(jnp.float32)
    toeplitz = jnp.einsum("tsk,kc->tsc", select, kernel, precision=precise)
    inner = jnp.einsum("tsc,bsc->btc", toeplitz, pieces, precision=precise)
    toward_end = jnp.exp(-decay[:, None, :] * (block_len - offsets)[None, :, None])
    block_sums = jnp.einsum("msc,bsc->bmc", toward_end, pieces, precision=precise)
    later = jnp.arange(blocks)[:, None]
    earlier = jnp.arange(blocks)[None, :]
    distance = jnp.maximum(later - 1 - earlier, 0).astype(jnp.float32)
    carry = jnp.where(
        (earlier < later)[:, :, None, None],
        jnp.exp(-decay[None, None] * (block_len * distance)[:, :, None, None]),
        0.0,
    )
    starts = jnp.sum(carry * block_sums[None], axis=1)
    outer = jnp.einsum("mic,bmc->bic", amplitude[:, None, :] * falloff, starts, precision=precise)
    conv = (inner + outer).reshape(length, sub)
    gated = (short[:, 0, :] * (conv + skip[None, :] * product)).astype(jnp.bfloat16)
    gated = lax.all_to_all(gated, "seq", 0, 1, tiled=True)
    mixed = jnp.dot(
        lax.all_gather(gated, "tensor", axis=1, tiled=True),
        out_weight,
        preferred_element_type=jnp.float32,
    )
    return mixed.astype(jnp.bfloat16)


def solution(mesh):
    in_specs = (
        P(("dp", "seq"), "tensor"),
        P("seq", None, "tensor"),
        P(None, None, "tensor"),
        P(None, "tensor"),
        P(None, "tensor"),
        P("tensor"),
        P(None, "tensor"),
    )
    out_specs = P(("dp", "seq"), "tensor")
    return jax.shard_map(body, mesh=mesh, in_specs=in_specs, out_specs=out_specs, check_vma=False)
```

time: 405 us -> 348 us (0.86)
  waiting for transfers between devices: 296 us -> 180 us
  starting transfers between devices: 1.6 us -> 108 us
  blocking collectives: 40.2 us -> 13 us
  matrix products: 34.9 us -> 13.2 us
  other arithmetic: 4.23 us -> 8.46 us
  local copies, waits for them, and re-layouts: 14.5 us -> 10.3 us
    all_gather x2 -> x0, waiting for transfers between devices: 213 us -> none  [the longest x1 136 us: body(): piece = lax.all_gather(in_weight, 'seq', axis=0, tiled=True)]
    ppermute x1 -> x16, starting transfers between devices: 1.48 us -> 108 us  [gather_weight_rows(): rounds.append(lax.ppermute(features, ('seq', 'tensor'), perm))]
    reduce_scatter x0 -> x1, waiting for transfers between devices: none -> 87.4 us  [body(): lax.psum_scatter(partial.reshape(seq_n * length, -1), 'seq', scatter_dime...]
    all_gather x1 -> x0, blocking collectives: 40.2 us -> none  [body(): gathered_sums = lax.all_gather(device_sum, 'seq')]
    ppermute x1 -> x16, waiting for transfers between devices: 0.01 us -> 13.1 us  [gather_weight_rows(): rounds.append(lax.ppermute(features, ('seq', 'tensor'), perm))]
    all_to_all x0 -> x1, blocking collectives: none -> 13 us  [body(): gated = lax.all_to_all(gated, 'seq', 0, 1, tiled=True)]
    dot_general x1, matrix products: 15.4 us -> 2.92 us  [body(): inner = jnp.einsum('tsc,bsc->btc', toeplitz, pieces, precision=precise)]
    dot_general x1 -> x0, local copies, waits for them, and re-layouts: 9.15 us -> none  [body(): toeplitz = jnp.einsum('tsk,kc->tsc', select, kernel, precision=precise)]
  transfers between devices with their start and end apart: 4 -> 18, of which waited for: 3 -> 3; matrix products, arithmetic and copies ran while one was open for 4% -> 4% of each run, Pallas kernels for 0% -> 0%
where the time goes in v2:
time: 348 us; the launch traced here: 347 us
  waiting for transfers between devices  180 us (52%)
  starting transfers between devices  108 us (31%)
  between operations  14 us (4%)
  matrix products  13.2 us (4%)
  blocking collectives  13 us (4%)
  local copies, waits for them, and re-layouts  10.3 us (3%)
  other arithmetic  8.46 us (2%)
    ppermute x16, starting transfers between devices, gather_weight_rows(): rounds.append(lax.ppermute(features, ('seq', 'tensor'), perm))  108 us
    reduce_scatter x1, waiting for transfers between devices, body(): lax.psum_scatter(partial.reshape(seq_n * length, -1), 'seq', scatter_dime...  87.4 us
    all_gather x1, waiting for transfers between devices, body(): lax.all_gather(gated, 'tensor', axis=1, tiled=True)  79.7 us
    ppermute x16, waiting for transfers between devices, gather_weight_rows(): rounds.append(lax.ppermute(features, ('seq', 'tensor'), perm))  13.1 us
    all_to_all x1, blocking collectives, body(): gated = lax.all_to_all(gated, 'seq', 0, 1, tiled=True)  13 us
  transfers between devices with their start and end apart: 18, of which 3 were waited for; matrix products, arithmetic and copies ran while one was open for 4% of the time, Pallas kernels for 0%

profile of v2, /device:TPU:1, one launch (start us, length us, event | category | flops | bytes accessed | tf_op | source)
XLA Modules:
  0.0 347.0 jit_solution(18220900289405770104)
XLA Ops:
  6.5 8.9 %collective-permute-start.8 = (bf16[128,256]{1,0:T(8,128)(2,1)}, bf16[128,256]{1,0:T(8,128)(2,1)S(1)}, u32[]{:S(2)}, u32[]{:S(2)}) collective-permute-start(bf16[128,256]{1,0:T(8,128)(2,1)} %param.7), channel_id=1, source_target_pairs={{1,0},{0,1},{17,2},{16,3},{33,4},{32,5},{49,6},{48,7},{65,8},{64,9... | collective-permute-start | bytes 196616 | tf_op jit(solution)/shard_map/ppermute | solution.py:20
  15.5 12.4 %collective-permute-start.9 = (bf16[128,256]{1,0:T(8,128)(2,1)}, bf16[128,256]{1,0:T(8,128)(2,1)S(1)}, u32[]{:S(2)}, u32[]{:S(2)}) collective-permute-start(bf16[128,256]{1,0:T(8,128)(2,1)} %param.7), channel_id=1, source_target_pairs={{17,0},{16,1},{33,2},{32,3},{49,4},{48,5},{65,6},{64,7},{81,8},{80... | collective-permute-start | bytes 196616 | tf_op jit(solution)/shard_map/ppermute | solution.py:20
  27.9 7.0 %collective-permute-start.10 = (bf16[128,256]{1,0:T(8,128)(2,1)}, bf16[128,256]{1,0:T(8,128)(2,1)S(1)}, u32[]{:S(2)}, u32[]{:S(2)}) collective-permute-start(bf16[128,256]{1,0:T(8,128)(2,1)} %param.7), channel_id=1, source_target_pairs={{33,0},{32,1},{49,2},{48,3},{65,4},{64,5},{81,6},{80,7},{97,8},{96... | collective-permute-start | bytes 196616 | tf_op jit(solution)/shard_map/ppermute | solution.py:20
  34.9 3.2 collective-permute-start.11
  38.1 7.8 %collective-permute-start.12 = (bf16[128,256]{1,0:T(8,128)(2,1)}, bf16[128,256]{1,0:T(8,128)(2,1)S(1)}, u32[]{:S(2)}, u32[]{:S(2)}) collective-permute-start(bf16[128,256]{1,0:T(8,128)(2,1)} %param.7), channel_id=1, source_target_pairs={{65,0},{64,1},{81,2},{80,3},{97,4},{96,5},{113,6},{112,7},{1,8},{0... | collective-permute-start | bytes 196616 | tf_op jit(solution)/shard_map/ppermute | solution.py:20
  46.0 2.4 fusion.7
  48.4 1.4 copy.30
  49.8 0.7 collective-permute-start
  50.5 13.4 %collective-permute-start.13 = (bf16[128,256]{1,0:T(8,128)(2,1)S(1)}, bf16[128,256]{1,0:T(8,128)(2,1)S(1)}, u32[]{:S(2)}, u32[]{:S(2)}) collective-permute-start(bf16[128,256]{1,0:T(8,128)(2,1)S(1)} %copy-done.7), channel_id=1, source_target_pairs={{81,0},{80,1},{97,2},{96,3},{113,4},{112,5},{1,6},{0,7},{17,8},{16... | collective-permute-start | bytes 196616 | tf_op jit(solution)/shard_map/ppermute | solution.py:20
  63.9 1.9 collective-permute-start.14
  65.9 9.0 %collective-permute-start.15 = (bf16[128,256]{1,0:T(8,128)(2,1)S(1)}, bf16[128,256]{1,0:T(8,128)(2,1)S(1)}, u32[]{:S(2)}, u32[]{:S(2)}) collective-permute-start(bf16[128,256]{1,0:T(8,128)(2,1)S(1)} %copy-done.7), channel_id=1, source_target_pairs={{113,0},{112,1},{1,2},{0,3},{17,4},{16,5},{33,6},{32,7},{49,8},{48... | collective-permute-start | bytes 196616 | tf_op jit(solution)/shard_map/ppermute | solution.py:20
  74.9 8.7 %collective-permute-start.1 = (bf16[128,256]{1,0:T(8,128)(2,1)S(1)}, bf16[128,256]{1,0:T(8,128)(2,1)S(1)}, u32[]{:S(2)}, u32[]{:S(2)}) collective-permute-start(bf16[128,256]{1,0:T(8,128)(2,1)S(1)} %copy-done.7), channel_id=1, source_target_pairs={{16,0},{17,1},{32,2},{33,3},{48,4},{49,5},{64,6},{65,7},{80,8},{81... | collective-permute-start | bytes 196616 | tf_op jit(solution)/shard_map/ppermute | solution.py:20
  83.7 9.3 %collective-permute-start.2 = (bf16[128,256]{1,0:T(8,128)(2,1)S(1)}, bf16[128,256]{1,0:T(8,128)(2,1)S(1)}, u32[]{:S(2)}, u32[]{:S(2)}) collective-permute-start(bf16[128,256]{1,0:T(8,128)(2,1)S(1)} %copy-done.7), channel_id=1, source_target_pairs={{32,0},{33,1},{48,2},{49,3},{64,4},{65,5},{80,6},{81,7},{96,8},{97... | collective-permute-start | bytes 196616 | tf_op jit(solution)/shard_map/ppermute | solution.py:20
  93.0 7.3 %collective-permute-start.3 = (bf16[128,256]{1,0:T(8,128)(2,1)S(1)}, bf16[128,256]{1,0:T(8,128)(2,1)S(1)}, u32[]{:S(2)}, u32[]{:S(2)}) collective-permute-start(bf16[128,256]{1,0:T(8,128)(2,1)S(1)} %copy-done.7), channel_id=1, source_target_pairs={{48,0},{49,1},{64,2},{65,3},{80,4},{81,5},{96,6},{97,7},{112,8},{1... | collective-permute-start | bytes 196616 | tf_op jit(solution)/shard_map/ppermute | solution.py:20
  100.3 4.2 %collective-permute-start.4 = (bf16[128,256]{1,0:T(8,128)(2,1)S(1)}, bf16[128,256]{1,0:T(8,128)(2,1)S(1)}, u32[]{:S(2)}, u32[]{:S(2)}) collective-permute-start(bf16[128,256]{1,0:T(8,128)(2,1)S(1)} %copy-done.7), channel_id=1, source_target_pairs={{64,0},{65,1},{80,2},{81,3},{96,4},{97,5},{112,6},{113,7},{0,8},{1... | collective-permute-start | bytes 196616 | tf_op jit(solution)/shard_map/ppermute | solution.py:20
  104.5 1.9 collective-permute-start.5
  106.5 7.7 %collective-permute-start.6 = (bf16[128,256]{1,0:T(8,128)(2,1)S(1)}, bf16[128,256]{1,0:T(8,128)(2,1)S(1)}, u32[]{:S(2)}, u32[]{:S(2)}) collective-permute-start(bf16[128,256]{1,0:T(8,128)(2,1)S(1)} %copy-done.7), channel_id=1, source_target_pairs={{96,0},{97,1},{112,2},{113,3},{0,4},{1,5},{16,6},{17,7},{32,8},{33... | collective-permute-start | bytes 196616 | tf_op jit(solution)/shard_map/ppermute | solution.py:20
  114.2 4.1 %collective-permute-start.7 = (bf16[128,256]{1,0:T(8,128)(2,1)S(1)}, bf16[128,256]{1,0:T(8,128)(2,1)S(1)}, u32[]{:S(2)}, u32[]{:S(2)}) collective-permute-start(bf16[128,256]{1,0:T(8,128)(2,1)S(1)} %copy-done.7), channel_id=1, source_target_pairs={{112,0},{113,1},{0,2},{1,3},{16,4},{17,5},{32,6},{33,7},{48,8},{49... | collective-permute-start | bytes 196616 | tf_op jit(solution)/shard_map/ppermute | solution.py:20
  118.4 13.1 %collective-permute-done.7 = bf16[128,256]{1,0:T(8,128)(2,1)S(1)} collective-permute-done((bf16[128,256]{1,0:T(8,128)(2,1)S(1)}, bf16[128,256]{1,0:T(8,128)(2,1)S(1)}, u32[]{:S(2)}, u32[]{:S(2)}) %collective-permute-start.7) | collective-permute-done | bytes 65568 | tf_op jit(solution)/shard_map/ppermute | solution.py:20
  131.5 1.0 convolution_bitcast_fusion
  132.5 1.8 copy.31
  134.4 3.8 %copy.48 = f32[12,8,8,1024]{3,1,2,0:T(8,128)} copy(f32[12,8,8,1024]{3,2,1,0:T(8,128)S(1)} %bitcast.72) | data formatting | bytes 6291456
  138.2 0.2 all-gather.2.cloned.1.call-start
  138.5 1.1 constant_dynamic-slice_fusion.4
  139.6 0.1 dynamic-slice_negate_fusion
  139.7 0.7 copy.35
  140.5 0.6 dynamic_slice.24
  141.2 0.6 broadcast_subtract_fusion
  141.7 0.6 iota_compare_fusion.2
  142.4 0.7 convert_multiply_fusion
  143.0 0.4 fusion.25
  143.5 3.6 %fusion = f32[64,64,32]{1,2,0:T(8,128)S(1)} fusion(f32[32,64,1]{1,0,2:T(8,128)S(1)} %bitcast.78, s32[64,64]{1,0:T(8,128)S(1)} %iota_subtract_fusion), kind=kOutput, calls=%fused_computation.2 | convolution fusion | flops 100925440 | bytes 548864 | tf_op jit(solution)/shard_map/tsk,kc->tsc/dot_general | solution.py:77
  147.1 87.4 %reduce-scatter.2.cloned.1.call-done = f32[1024,96]{0,1:T(8,128)} async-done(((f32[8192,96]{0,1:T(8,128)}), f32[1024,96]{0,1:T(8,128)}) %reduce-scatter.2.cloned.1.call-update) | async-done | bytes 393232 | tf_op jit(solution)/shard_map/reduce_scatter | solution.py:48
  234.5 1.1 fusion.21
  235.6 0.8 fusion.14
  236.4 0.7 slice_bitcast_fusion
  237.1 0.1 mul.203
  237.2 2.9 fusion.4
  240.1 1.3 convolution_bitcast_fusion.1
  241.4 0.2 copy.34
  241.6 1.5 multiply_reduce_fusion
  243.1 0.2 copy.36
  243.2 1.5 fusion.1
  244.7 0.1 reshape.105
  244.9 0.1 fusion.28
  245.0 13.0 %all_to_all.16 = bf16[8,128,32]{1,2,0:T(8,128)(2,1)} all-to-all(bf16[8,128,32]{1,2,0:T(8,128)(2,1)S(1)} %copy.37), channel_id=1, replica_groups=mesh['dp'=4,'seq'=8,'tensor'=16] {'seq'}, dimensions={0} | all-to-all | bytes 131072 | tf_op jit(solution)/shard_map/all_to_all | solution.py:93
  258.0 79.7 %all-gather.2.cloned.1.call-done = bf16[128,4096]{0,1:T(8,128)(2,1)} async-done(((bf16[128,256]{0,1:T(8,128)(2,1)}), bf16[128,4096]{0,1:T(8,128)(2,1)}) %all-gather.2.cloned.1.call-update) | async-done | bytes 1048592 | tf_op jit(solution)/shard_map/all_gather | solution.py:95
  337.7 2.4 convolution_convert_fusion
  (64 shorter events, 0.5 us)
Async XLA Ops:
  6.5 331.2 %copy-start = (bf16[4096,256]{1,0:T(8,128)(2,1)S(1)}, bf16[4096,256]{1,0:T(8,128)(2,1)}, u32[]{:S(2)}) copy-start(bf16[4096,256]{1,0:T(8,128)(2,1)} %param.13) | copy-start | bytes 6291460
  6.5 43.3 %copy-start.7 = (bf16[128,256]{1,0:T(8,128)(2,1)S(1)}, bf16[128,256]{1,0:T(8,128)(2,1)}, u32[]{:S(2)}) copy-start(bf16[128,256]{1,0:T(8,128)(2,1)} %param.7) | copy-start | bytes 196612
  6.5 228.0 %reduce-scatter.2.cloned.1.call-start = ((), (), s32[]{:S(2)}) async-start(), calls=%async_computation.2 | async-start | bytes 3538944 | tf_op jit(solution)/shard_map/reduce_scatter | solution.py:48
  6.5 43.3 %collective-permute-start.8 = (bf16[128,256]{1,0:T(8,128)(2,1)}, bf16[128,256]{1,0:T(8,128)(2,1)S(1)}, u32[]{:S(2)}, u32[]{:S(2)}) collective-permute-start(bf16[128,256]{1,0:T(8,128)(2,1)} %param.7), channel_id=1, source_target_pairs={{1,0},{0,1},{17,2},{16,3},{33,4},{32,5},{49,6},{48,7},{65,8},{64,9... | collective-permute-start | bytes 196616 | tf_op jit(solution)/shard_map/ppermute | solution.py:20
  15.5 48.4 %collective-permute-start.9 = (bf16[128,256]{1,0:T(8,128)(2,1)}, bf16[128,256]{1,0:T(8,128)(2,1)S(1)}, u32[]{:S(2)}, u32[]{:S(2)}) collective-permute-start(bf16[128,256]{1,0:T(8,128)(2,1)} %param.7), channel_id=1, source_target_pairs={{17,0},{16,1},{33,2},{32,3},{49,4},{48,5},{65,6},{64,7},{81,8},{80... | collective-permute-start | bytes 196616 | tf_op jit(solution)/shard_map/ppermute | solution.py:20
  27.9 38.0 %collective-permute-start.10 = (bf16[128,256]{1,0:T(8,128)(2,1)}, bf16[128,256]{1,0:T(8,128)(2,1)S(1)}, u32[]{:S(2)}, u32[]{:S(2)}) collective-permute-start(bf16[128,256]{1,0:T(8,128)(2,1)} %param.7), channel_id=1, source_target_pairs={{33,0},{32,1},{49,2},{48,3},{65,4},{64,5},{81,6},{80,7},{97,8},{96... | collective-permute-start | bytes 196616 | tf_op jit(solution)/shard_map/ppermute | solution.py:20
  34.9 40.0 %collective-permute-start.11 = (bf16[128,256]{1,0:T(8,128)(2,1)}, bf16[128,256]{1,0:T(8,128)(2,1)S(1)}, u32[]{:S(2)}, u32[]{:S(2)}) collective-permute-start(bf16[128,256]{1,0:T(8,128)(2,1)} %param.7), channel_id=1, source_target_pairs={{49,0},{48,1},{65,2},{64,3},{81,4},{80,5},{97,6},{96,7},{113,8},{1... | collective-permute-start | bytes 196616 | tf_op jit(solution)/shard_map/ppermute | solution.py:20
  38.1 45.5 %collective-permute-start.12 = (bf16[128,256]{1,0:T(8,128)(2,1)}, bf16[128,256]{1,0:T(8,128)(2,1)S(1)}, u32[]{:S(2)}, u32[]{:S(2)}) collective-permute-start(bf16[128,256]{1,0:T(8,128)(2,1)} %param.7), channel_id=1, source_target_pairs={{65,0},{64,1},{81,2},{80,3},{97,4},{96,5},{113,6},{112,7},{1,8},{0... | collective-permute-start | bytes 196616 | tf_op jit(solution)/shard_map/ppermute | solution.py:20
  49.8 0.7 collective-permute-start
  50.5 42.5 %collective-permute-start.13 = (bf16[128,256]{1,0:T(8,128)(2,1)S(1)}, bf16[128,256]{1,0:T(8,128)(2,1)S(1)}, u32[]{:S(2)}, u32[]{:S(2)}) collective-permute-start(bf16[128,256]{1,0:T(8,128)(2,1)S(1)} %copy-done.7), channel_id=1, source_target_pairs={{81,0},{80,1},{97,2},{96,3},{113,4},{112,5},{1,6},{0,7},{17,8},{16... | collective-permute-start | bytes 196616 | tf_op jit(solution)/shard_map/ppermute | solution.py:20
  63.9 36.4 %collective-permute-start.14 = (bf16[128,256]{1,0:T(8,128)(2,1)S(1)}, bf16[128,256]{1,0:T(8,128)(2,1)S(1)}, u32[]{:S(2)}, u32[]{:S(2)}) collective-permute-start(bf16[128,256]{1,0:T(8,128)(2,1)S(1)} %copy-done.7), channel_id=1, source_target_pairs={{97,0},{96,1},{113,2},{112,3},{1,4},{0,5},{17,6},{16,7},{33,8},{32... | collective-permute-start | bytes 196616 | tf_op jit(solution)/shard_map/ppermute | solution.py:20
  65.9 38.7 %collective-permute-start.15 = (bf16[128,256]{1,0:T(8,128)(2,1)S(1)}, bf16[128,256]{1,0:T(8,128)(2,1)S(1)}, u32[]{:S(2)}, u32[]{:S(2)}) collective-permute-start(bf16[128,256]{1,0:T(8,128)(2,1)S(1)} %copy-done.7), channel_id=1, source_target_pairs={{113,0},{112,1},{1,2},{0,3},{17,4},{16,5},{33,6},{32,7},{49,8},{48... | collective-permute-start | bytes 196616 | tf_op jit(solution)/shard_map/ppermute | solution.py:20
  74.9 31.6 %collective-permute-start.1 = (bf16[128,256]{1,0:T(8,128)(2,1)S(1)}, bf16[128,256]{1,0:T(8,128)(2,1)S(1)}, u32[]{:S(2)}, u32[]{:S(2)}) collective-permute-start(bf16[128,256]{1,0:T(8,128)(2,1)S(1)} %copy-done.7), channel_id=1, source_target_pairs={{16,0},{17,1},{32,2},{33,3},{48,4},{49,5},{64,6},{65,7},{80,8},{81... | collective-permute-start | bytes 196616 | tf_op jit(solution)/shard_map/ppermute | solution.py:20
  83.7 30.6 %collective-permute-start.2 = (bf16[128,256]{1,0:T(8,128)(2,1)S(1)}, bf16[128,256]{1,0:T(8,128)(2,1)S(1)}, u32[]{:S(2)}, u32[]{:S(2)}) collective-permute-start(bf16[128,256]{1,0:T(8,128)(2,1)S(1)} %copy-done.7), channel_id=1, source_target_pairs={{32,0},{33,1},{48,2},{49,3},{64,4},{65,5},{80,6},{81,7},{96,8},{97... | collective-permute-start | bytes 196616 | tf_op jit(solution)/shard_map/ppermute | solution.py:20
  93.0 25.3 %collective-permute-start.3 = (bf16[128,256]{1,0:T(8,128)(2,1)S(1)}, bf16[128,256]{1,0:T(8,128)(2,1)S(1)}, u32[]{:S(2)}, u32[]{:S(2)}) collective-permute-start(bf16[128,256]{1,0:T(8,128)(2,1)S(1)} %copy-done.7), channel_id=1, source_target_pairs={{48,0},{49,1},{64,2},{65,3},{80,4},{81,5},{96,6},{97,7},{112,8},{1... | collective-permute-start | bytes 196616 | tf_op jit(solution)/shard_map/ppermute | solution.py:20
  100.3 18.0 %collective-permute-start.4 = (bf16[128,256]{1,0:T(8,128)(2,1)S(1)}, bf16[128,256]{1,0:T(8,128)(2,1)S(1)}, u32[]{:S(2)}, u32[]{:S(2)}) collective-permute-start(bf16[128,256]{1,0:T(8,128)(2,1)S(1)} %copy-done.7), channel_id=1, source_target_pairs={{64,0},{65,1},{80,2},{81,3},{96,4},{97,5},{112,6},{113,7},{0,8},{1... | collective-permute-start | bytes 196616 | tf_op jit(solution)/shard_map/ppermute | solution.py:20
  104.5 13.8 %collective-permute-start.5 = (bf16[128,256]{1,0:T(8,128)(2,1)S(1)}, bf16[128,256]{1,0:T(8,128)(2,1)S(1)}, u32[]{:S(2)}, u32[]{:S(2)}) collective-permute-start(bf16[128,256]{1,0:T(8,128)(2,1)S(1)} %copy-done.7), channel_id=1, source_target_pairs={{80,0},{81,1},{96,2},{97,3},{112,4},{113,5},{0,6},{1,7},{16,8},{17... | collective-permute-start | bytes 196616 | tf_op jit(solution)/shard_map/ppermute | solution.py:20
  106.5 11.9 %collective-permute-start.6 = (bf16[128,256]{1,0:T(8,128)(2,1)S(1)}, bf16[128,256]{1,0:T(8,128)(2,1)S(1)}, u32[]{:S(2)}, u32[]{:S(2)}) collective-permute-start(bf16[128,256]{1,0:T(8,128)(2,1)S(1)} %copy-done.7), channel_id=1, source_target_pairs={{96,0},{97,1},{112,2},{113,3},{0,4},{1,5},{16,6},{17,7},{32,8},{33... | collective-permute-start | bytes 196616 | tf_op jit(solution)/shard_map/ppermute | solution.py:20
  114.2 17.3 %collective-permute-start.7 = (bf16[128,256]{1,0:T(8,128)(2,1)S(1)}, bf16[128,256]{1,0:T(8,128)(2,1)S(1)}, u32[]{:S(2)}, u32[]{:S(2)}) collective-permute-start(bf16[128,256]{1,0:T(8,128)(2,1)S(1)} %copy-done.7), channel_id=1, source_target_pairs={{112,0},{113,1},{0,2},{1,3},{16,4},{17,5},{32,6},{33,7},{48,8},{49... | collective-permute-start | bytes 196616 | tf_op jit(solution)/shard_map/ppermute | solution.py:20
  138.2 1.4 copy-start.3
  138.2 1.4 copy-start.4
  138.2 2.3 copy-start.8
  138.2 199.5 %all-gather.2.cloned.1.call-start = ((), (), s32[]{:S(2)}) async-start(), calls=%async_computation.3 | async-start | bytes 1114112 | tf_op jit(solution)/shard_map/all_gather | solution.py:95
  139.7 3.8 %copy-start.2 = (f32[16,32]{1,0:T(8,128)}, f32[16,32]{1,0:T(8,128)S(1)}, u32[]{:S(2)}) copy-start(f32[16,32]{1,0:T(8,128)S(1)} %get-tuple-element.14) | copy-start | bytes 6148
  141.1 2.4 copy-start.6
  240.1 4.8 %copy-start.1 = (f32[4,8,8,128]{3,1,2,0:T(8,128)S(1)}, f32[4,8,8,128]{3,1,2,0:T(8,128)}, u32[]{:S(2)}) copy-start(f32[4,8,8,128]{3,1,2,0:T(8,128)} %get-tuple-element.5) | copy-start | bytes 393220
  240.1 4.8 %copy-start.5 = (f32[32]{0:T(128)S(1)}, f32[32]{0:T(128)}, u32[]{:S(2)}) copy-start(f32[32]{0:T(128)} %dynamic_slice.24) | copy-start | bytes 388
Sparse Core Ops, SparseCore 0:
  138.3 96.1 reduce-scatter.1
  258.1 79.5 all-gather.1

commit v3 on v2

--- a/solution.py
+++ b/solution.py
@@ -5,23 +5,6 @@
 
 precise = lax.Precision.HIGHEST
 block_len = 64
-
-
-def gather_weight_rows(features, seq_n, ten_n, halves):
-    rounds = []
-    for j in range(seq_n * halves):
-        i, h = j % seq_n, j // seq_n
-        perm = []
-        for s in range(seq_n):
-            for a in range(seq_n):
-                for b in range(halves):
-                    src = ((a + i) % seq_n) * ten_n + s * halves + (b + h) % halves
-                    perm.append((src, s * ten_n + a * halves + b))
-        rounds.append(lax.ppermute(features, ("seq", "tensor"), perm))
-    columns = [
-        jnp.concatenate(rounds[h * seq_n : (h + 1) * seq_n], axis=0) for h in range(halves)
-    ]
-    return jnp.concatenate(columns, axis=1)
 
 
 def body(features, in_weight, short_taps, decay_rates, residues, skip_gain, out_weight):
@@ -35,18 +18,15 @@
     sub = channels // seq_n
     length = tok_rows * seq_n
     taps_count = short_taps.shape[1]
-    rotation = lane // halves
-    half_of = lane % halves
-
-    rows_of_feats = gather_weight_rows(features, seq_n, ten_n, halves)
-    doubled = jnp.concatenate([in_weight, in_weight], axis=0)
-    weight_rows = lax.dynamic_slice_in_dim(doubled, half_of * fcols, rows_here, axis=0)
-    weight_rows = weight_rows.reshape(rows_here, branches, seq_n, sub)
+    copies = jnp.tile(features, (ten_n, 1))
+    own_tokens = lax.all_to_all(copies, "tensor", 0, 1, tiled=True)
+    rows_of_feats = lax.all_to_all(own_tokens, "seq", 1, 0, tiled=True)
+    weight_rows = in_weight.reshape(rows_here, branches, seq_n, sub)
     partial = jnp.einsum(
         "td,djgc->gtjc", rows_of_feats, weight_rows, preferred_element_type=jnp.float32
     )
     summed = lax.psum_scatter(partial.reshape(seq_n * length, -1), "seq", scatter_dimension=0, tiled=True)
-    summed = jnp.roll(summed.reshape(length, branches, sub), rotation * tok_rows, axis=0)
+    summed = summed.reshape(length, branches, sub)
     projected = lax.reduce_precision(summed, exponent_bits=8, mantissa_bits=7)
 
     taps = lax.dynamic_slice_in_dim(short_taps, place * sub, sub, axis=2)
@@ -90,9 +70,13 @@
     outer = jnp.einsum("mic,bmc->bic", amplitude[:, None, :] * falloff, starts, precision=precise)
     conv = (inner + outer).reshape(length, sub)
     gated = (short[:, 0, :] * (conv + skip[None, :] * product)).astype(jnp.bfloat16)
-    gated = lax.all_to_all(gated, "seq", 0, 1, tiled=True)
+    outgoing = jnp.broadcast_to(
+        gated.reshape(seq_n, 1, tok_rows, sub), (seq_n, ten_n, tok_rows, sub)
+    ).reshape(seq_n * ten_n * tok_rows, sub)
+    incoming = lax.all_to_all(outgoing, ("seq", "tensor"), 0, 0, tiled=True)
+    incoming = incoming.reshape(seq_n, ten_n, tok_rows, sub).transpose(2, 1, 0, 3)
     mixed = jnp.dot(
-        lax.all_gather(gated, "tensor", axis=1, tiled=True),
+        incoming.reshape(tok_rows, ten_n * seq_n * sub),
         out_weight,
         preferred_element_type=jnp.float32,
     )

time: 348 us -> 314 us (0.902)
  blocking collectives: 13 us -> 113 us
  starting transfers between devices: 108 us -> 32.7 us
  waiting for transfers between devices: 180 us -> 118 us
  local copies, waits for them, and re-layouts: 10.3 us -> 15.2 us
    ppermute x16 -> x0, starting transfers between devices: 108 us -> none  [gather_weight_rows(): rounds.append(lax.ppermute(features, ('seq', 'tensor'), perm))]
    all_to_all x1 -> x2, blocking collectives: 13 us -> 113 us  [the longest x1 64 us: body(): incoming = lax.all_to_all(outgoing, ('seq', 'tensor'), 0, 0, tiled=True)]
    all_gather x1 -> x0, waiting for transfers between devices: 79.7 us -> none  [body(): lax.all_gather(gated, 'tensor', axis=1, tiled=True)]
    all_to_all x0 -> x1, waiting for transfers between devices: none -> 33.3 us  [body(): rows_of_feats = lax.all_to_all(own_tokens, 'seq', 1, 0, tiled=True)]
    all_to_all x0 -> x1, starting transfers between devices: none -> 32.6 us  [body(): rows_of_feats = lax.all_to_all(own_tokens, 'seq', 1, 0, tiled=True)]
    ppermute x16 -> x0, waiting for transfers between devices: 13.1 us -> none  [gather_weight_rows(): rounds.append(lax.ppermute(features, ('seq', 'tensor'), perm))]
    unnamed x39 -> x27, local copies, waits for them, and re-layouts: 4.01 us -> 8.34 us
  transfers between devices with their start and end apart: 18 -> 2, of which waited for: 3 -> 2; matrix products, arithmetic and copies ran while one was open for 4% -> 3% of each run, Pallas kernels for 0% -> 0%
where the time goes in v3:
time: 314 us; the launch traced here: 311 us
  waiting for transfers between devices  118 us (38%)
  blocking collectives  113 us (36%)
  starting transfers between devices  32.7 us (10%)
  local copies, waits for them, and re-layouts  15.2 us (5%)
  between operations  13.6 us (4%)
  matrix products  13.1 us (4%)
  other arithmetic  5.98 us (2%)
    reduce_scatter x1, waiting for transfers between devices, body(): lax.psum_scatter(partial.reshape(seq_n * length, -1), 'seq', scatter_dime...  84.1 us
    all_to_all x1, blocking collectives, body(): incoming = lax.all_to_all(outgoing, ('seq', 'tensor'), 0, 0, tiled=True)  64 us
    all_to_all x1, blocking collectives, body(): own_tokens = lax.all_to_all(copies, 'tensor', 0, 1, tiled=True)  48.7 us
    all_to_all x1, waiting for transfers between devices, body(): rows_of_feats = lax.all_to_all(own_tokens, 'seq', 1, 0, tiled=True)  33.3 us
    all_to_all x1, starting transfers between devices, body(): rows_of_feats = lax.all_to_all(own_tokens, 'seq', 1, 0, tiled=True)  32.6 us
    unnamed x27, local copies, waits for them, and re-layouts  8.34 us
  transfers between devices with their start and end apart: 2, of which 2 were waited for; matrix products, arithmetic and copies ran while one was open for 3% of the time, Pallas kernels for 0%

profile of v3, /device:TPU:1, one launch (start us, length us, event | category | flops | bytes accessed | tf_op | source)
XLA Modules:
  0.0 310.8 jit_solution(8027920702149134036)
XLA Ops:
  6.5 0.0 copy-start
  6.5 1.1 copy.30
  7.6 0.2 tile.2
  7.8 48.7 %all_to_all.41 = bf16[16,128,256]{1,2,0:T(8,128)(2,1)} all-to-all(bf16[16,128,256]{1,2,0:T(8,128)(2,1)S(1)} %tile.2), channel_id=1, replica_groups=mesh['dp'=4,'seq'=8,'tensor'=16] {'tensor'}, dimensions={0} | all-to-all | bytes 2097152 | tf_op jit(solution)/shard_map/all_to_all | solution.py:22
  56.5 32.6 %all-to-all-start.1 = ((bf16[128,8,512]{0,2,1:T(8,128)(2,1)}), bf16[128,8,512]{0,2,1:T(8,128)(2,1)S(1)}, u32[]{:S(2)}, u32[]{:S(2)}) async-start(bf16[128,8,512]{0,2,1:T(8,128)(2,1)} %bitcast.83), calls=%async_computation.1 | async-start | bytes 2097152 | tf_op jit(solution)/shard_map/all_to_all | solution.py:23
  89.2 0.0 reduce-scatter.2.cloned.1.call-start
  89.2 2.4 copy.29
  91.6 33.3 %all-to-all-done.1 = bf16[128,8,512]{0,2,1:T(8,128)(2,1)S(1)} async-done(((bf16[128,8,512]{0,2,1:T(8,128)(2,1)}), bf16[128,8,512]{0,2,1:T(8,128)(2,1)S(1)}, u32[]{:S(2)}, u32[]{:S(2)}) %all-to-all-start.1) | async-done | bytes 1048608 | tf_op jit(solution)/shard_map/all_to_all | solution.py:23
  124.9 1.0 copy-done.1
  125.9 1.5 copy.31
  127.4 2.1 convolution_bitcast_fusion
  129.5 1.8 copy.32
  131.3 3.8 %copy.50 = f32[12,8,8,1024]{3,1,2,0:T(8,128)} copy(f32[12,8,8,1024]{3,2,1,0:T(8,128)S(1)} %bitcast.79) | data formatting | bytes 6291456
  135.2 0.0 reduce-scatter.2.cloned.1.call-update
  135.2 1.1 constant_dynamic-slice_fusion.5
  136.3 0.0 copy-done.4
  136.3 0.0 copy-done.5
  136.3 0.1 dynamic-slice_negate_fusion
  136.4 0.7 copy.36
  137.1 0.1 copy.41
  137.1 0.1 copy.33
  137.2 0.0 copy-done.8
  137.2 0.7 dynamic_slice.15
  137.9 0.5 broadcast_subtract_fusion
  138.4 0.6 iota_compare_fusion.2
  139.1 0.7 convert_multiply_fusion
  139.7 0.4 fusion.20
  140.2 3.6 %fusion = f32[64,64,32]{1,2,0:T(8,128)S(1)} fusion(f32[32,64,1]{1,0,2:T(8,128)S(1)} %bitcast.90, s32[64,64]{1,0:T(8,128)S(1)} %iota_subtract_fusion), kind=kOutput, calls=%fused_computation.2 | convolution fusion | flops 100925440 | bytes 548864 | tf_op jit(solution)/shard_map/tsk,kc->tsc/dot_general | solution.py:57
  143.8 84.1 %reduce-scatter.2.cloned.1.call-done = f32[1024,96]{0,1:T(8,128)} async-done(((f32[8192,96]{0,1:T(8,128)}), f32[1024,96]{0,1:T(8,128)}) %reduce-scatter.2.cloned.1.call-update) | async-done | bytes 393232 | tf_op jit(solution)/shard_map/reduce_scatter | solution.py:28
  227.9 1.0 reduce_precision.6
  228.9 0.0 copy-done.3
  229.0 0.0 copy-done.7
  229.0 0.8 fusion.11
  229.8 0.7 slice_bitcast_fusion
  230.5 0.1 mul.204
  230.6 2.9 fusion.2
  233.5 1.3 convolution_bitcast_fusion.1
  234.8 0.2 copy.35
  234.9 1.5 multiply_reduce_fusion
  236.4 0.2 copy.37
  236.6 1.5 fusion.1
  238.1 0.1 reshape.141
  238.2 0.0 copy-done.2
  238.2 0.1 fusion.23
  238.4 0.2 broadcast_in_dim.12
  238.5 64.0 %all_to_all.42 = bf16[128,128,32]{1,2,0:T(8,128)(2,1)S(1)} all-to-all(bf16[128,128,32]{1,2,0:T(8,128)(2,1)S(1)} %bitcast.84), channel_id=1, replica_groups=mesh['dp'=4,'seq'=8,'tensor'=16] {'seq','tensor'}, dimensions={0} | all-to-all | bytes 2097152 | tf_op jit(solution)/shard_map/all_to_all | solution.py:76
  302.6 0.1 copy.39
  302.7 1.2 convolution_convert_fusion
  (20 shorter events, 0.1 us)
Async XLA Ops:
  6.5 296.2 %copy-start = (bf16[4096,256]{1,0:T(8,128)(2,1)S(1)}, bf16[4096,256]{1,0:T(8,128)(2,1)}, u32[]{:S(2)}) copy-start(bf16[4096,256]{1,0:T(8,128)(2,1)} %param.13) | copy-start | bytes 6291460
  56.5 68.4 %all-to-all-start.1 = ((bf16[128,8,512]{0,2,1:T(8,128)(2,1)}), bf16[128,8,512]{0,2,1:T(8,128)(2,1)S(1)}, u32[]{:S(2)}, u32[]{:S(2)}) async-start(bf16[128,8,512]{0,2,1:T(8,128)(2,1)} %bitcast.83), calls=%async_computation.1 | async-start | bytes 2097152 | tf_op jit(solution)/shard_map/all_to_all | solution.py:23
  89.2 138.8 %reduce-scatter.2.cloned.1.call-start = ((), (), s32[]{:S(2)}) async-start(), calls=%async_computation.4 | async-start | bytes 3538944 | tf_op jit(solution)/shard_map/reduce_scatter | solution.py:28
  124.9 1.0 copy-start.1
  135.2 1.1 copy-start.4
  135.2 1.1 copy-start.5
  135.2 2.1 copy-start.8
  136.4 92.6 %copy-start.3 = (f32[16,32]{1,0:T(8,128)}, f32[16,32]{1,0:T(8,128)S(1)}, u32[]{:S(2)}) copy-start(f32[16,32]{1,0:T(8,128)S(1)} %get-tuple-element.14) | copy-start | bytes 6148
  137.9 91.1 %copy-start.7 = (f32[64]{0:T(128)}, f32[64]{0:T(128)S(1)}, u32[]{:S(2)}) copy-start(f32[64]{0:T(128)S(1)} %iota_convert_fusion) | copy-start | bytes 772
  233.5 4.7 %copy-start.2 = (f32[4,8,8,128]{3,1,2,0:T(8,128)S(1)}, f32[4,8,8,128]{3,1,2,0:T(8,128)}, u32[]{:S(2)}) copy-start(f32[4,8,8,128]{3,1,2,0:T(8,128)} %get-tuple-element.5) | copy-start | bytes 393220
  233.5 4.8 %copy-start.6 = (f32[32]{0:T(128)S(1)}, f32[32]{0:T(128)}, u32[]{:S(2)}) copy-start(f32[32]{0:T(128)} %dynamic_slice.15) | copy-start | bytes 388
Sparse Core Ops, SparseCore 0:
  135.3 92.5 reduce-scatter.1

commit v4 on v3

--- a/solution.py
+++ b/solution.py
@@ -18,10 +18,21 @@
     sub = channels // seq_n
     length = tok_rows * seq_n
     taps_count = short_taps.shape[1]
-    copies = jnp.tile(features, (ten_n, 1))
-    own_tokens = lax.all_to_all(copies, "tensor", 0, 1, tiled=True)
-    rows_of_feats = lax.all_to_all(own_tokens, "seq", 1, 0, tiled=True)
-    weight_rows = in_weight.reshape(rows_here, branches, seq_n, sub)
+    copies = jnp.tile(features, (seq_n, 1))
+    my_columns = lax.all_to_all(copies, "seq", 0, 0, tiled=True)
+    across = []
+    for s in range(seq_n):
+        for a in range(seq_n):
+            for b in range(halves):
+                across.append((a * ten_n + s * halves + b, s * ten_n + a * halves + b))
+    first = lax.ppermute(my_columns, ("seq", "tensor"), across)
+    swap = [(k, k + 1 - 2 * (k % 2)) for k in range(ten_n)]
+    second = lax.ppermute(first, "tensor", swap)
+    rows_of_feats = jnp.concatenate([first, second], axis=1)
+    half_of = lane % halves
+    doubled = jnp.concatenate([in_weight, in_weight], axis=0)
+    weight_rows = lax.dynamic_slice_in_dim(doubled, half_of * fcols, rows_here, axis=0)
+    weight_rows = weight_rows.reshape(rows_here, branches, seq_n, sub)
     partial = jnp.einsum(
         "td,djgc->gtjc", rows_of_feats, weight_rows, preferred_element_type=jnp.float32
     )

time: 314 us -> 280 us (0.89)
  starting transfers between devices: 32.7 us -> 9.59 us
  blocking collectives: 113 us -> 99.4 us
  waiting for transfers between devices: 118 us -> 123 us
  local copies, waits for them, and re-layouts: 15.2 us -> 11.5 us
    reduce_scatter x1, waiting for transfers between devices: 84.1 us -> 122 us  [body(): lax.psum_scatter(partial.reshape(seq_n * length, -1), 'seq', scatter_dime...]
    all_to_all x1 -> x0, waiting for transfers between devices: 33.3 us -> none  [body(): rows_of_feats = lax.all_to_all(own_tokens, 'seq', 1, 0, tiled=True)]
    all_to_all x1 -> x0, starting transfers between devices: 32.6 us -> none  [body(): rows_of_feats = lax.all_to_all(own_tokens, 'seq', 1, 0, tiled=True)]
    all_to_all x1, blocking collectives: 48.7 us -> 35.6 us  [body(): my_columns = lax.all_to_all(copies, 'seq', 0, 0, tiled=True)]
    ppermute x0 -> x2, starting transfers between devices: none -> 9.59 us  [the longest x1 8.9 us: body(): second = lax.ppermute(first, 'tensor', swap)]
    unnamed x27 -> x25, local copies, waits for them, and re-layouts: 8.34 us -> 3.91 us
  transfers between devices with their start and end apart: 2 -> 3, of which waited for: 2 -> 1; matrix products, arithmetic and copies ran while one was open for 3% -> 4% of each run, Pallas kernels for 0% -> 0%
where the time goes in v4:
time: 280 us; the launch traced here: 277 us
  waiting for transfers between devices  123 us (44%)
  blocking collectives  99.4 us (36%)
  between operations  13.7 us (5%)
  matrix products  13 us (5%)
  local copies, waits for them, and re-layouts  11.5 us (4%)
  starting transfers between devices  9.59 us (3%)
  other arithmetic  7.7 us (3%)
    reduce_scatter x1, waiting for transfers between devices, body(): lax.psum_scatter(partial.reshape(seq_n * length, -1), 'seq', scatter_dime...  122 us
    all_to_all x1, blocking collectives, body(): incoming = lax.all_to_all(outgoing, ('seq', 'tensor'), 0, 0, tiled=True)  63.9 us
    all_to_all x1, blocking collectives, body(): my_columns = lax.all_to_all(copies, 'seq', 0, 0, tiled=True)  35.6 us
    ppermute x1, starting transfers between devices, body(): second = lax.ppermute(first, 'tensor', swap)  8.9 us
  transfers between devices with their start and end apart: 3, of which 1 were waited for; matrix products, arithmetic and copies ran while one was open for 4% of the time, Pallas kernels for 0%

profile of v4, /device:TPU:1, one launch (start us, length us, event | category | flops | bytes accessed | tf_op | source)
XLA Modules:
  0.0 277.4 jit_solution(4013239788591000243)
XLA Ops:
  6.5 0.0 copy-start
  6.5 0.0 reduce-scatter.2.cloned.1.call-start
  6.5 1.0 tile.2
  7.6 35.6 %all_to_all.18 = bf16[8,128,256]{2,1,0:T(8,128)(2,1)S(1)} all-to-all(bf16[8,128,256]{2,1,0:T(8,128)(2,1)S(1)} %tile.2), channel_id=1, replica_groups=mesh['dp'=4,'seq'=8,'tensor'=16] {'seq'}, dimensions={0} | all-to-all | bytes 1048576 | tf_op jit(solution)/shard_map/all_to_all | solution.py:22
  43.1 0.7 collective-permute-start
  43.8 0.0 collective-permute-done
  43.8 8.9 %collective-permute-start.1 = (bf16[1024,256]{1,0:T(8,128)(2,1)S(1)}, bf16[1024,256]{1,0:T(8,128)(2,1)}, u32[]{:S(2)}, u32[]{:S(2)}) collective-permute-start(bf16[1024,256]{1,0:T(8,128)(2,1)S(1)} %collective-permute-done), channel_id=1, source_target_pairs={{0,1},{1,0},{2,3},{3,2},{4,5},{5,4},{6,7},{7,6},{8,9},{9,8},{10,11... | collective-permute-start | bytes 1572872 | tf_op jit(solution)/shard_map/ppermute | solution.py:30
  52.8 0.0 copy-done.1
  52.8 1.7 fusion.7
  54.5 1.4 copy.25
  55.9 0.0 collective-permute-done.1
  55.9 2.1 convolution_bitcast_fusion
  58.0 1.8 copy.26
  59.8 3.8 %copy.44 = f32[12,8,8,1024]{3,1,2,0:T(8,128)} copy(f32[12,8,8,1024]{3,2,1,0:T(8,128)S(1)} %bitcast.75) | data formatting | bytes 6291456
  63.6 0.0 reduce-scatter.2.cloned.1.call-update
  63.7 1.1 constant_dynamic-slice_fusion.5
  64.7 0.0 copy-done.4
  64.7 0.0 copy-done.5
  64.8 0.1 dynamic-slice_negate_fusion
  64.8 0.1 copy.27
  64.9 0.7 copy.30
  65.6 0.1 copy.35
  65.7 0.7 dynamic_slice.19
  66.4 0.5 broadcast_subtract_fusion
  66.9 0.6 iota_compare_fusion.2
  67.5 0.7 convert_multiply_fusion
  68.2 0.4 fusion.23
  68.6 0.0 copy-done.3
  68.7 0.0 copy-done.7
  68.7 3.6 %fusion = f32[64,64,32]{1,2,0:T(8,128)S(1)} fusion(f32[32,64,1]{1,0,2:T(8,128)S(1)} %bitcast.84, s32[64,64]{1,0:T(8,128)S(1)} %iota_subtract_fusion), kind=kOutput, calls=%fused_computation.2 | convolution fusion | flops 100925440 | bytes 548864 | tf_op jit(solution)/shard_map/tsk,kc->tsc/dot_general | solution.py:68
  72.3 122.5 %reduce-scatter.2.cloned.1.call-done = f32[1024,96]{0,1:T(8,128)} async-done(((f32[8192,96]{0,1:T(8,128)}), f32[1024,96]{0,1:T(8,128)}) %reduce-scatter.2.cloned.1.call-update) | async-done | bytes 393232 | tf_op jit(solution)/shard_map/reduce_scatter | solution.py:39
  194.7 1.0 reduce_precision.6
  195.8 0.8 fusion.14
  196.6 0.7 slice_bitcast_fusion
  197.3 0.1 mul.208
  197.4 2.9 %fusion.4 = f32[32,16,64]{2,1,0:T(8,128)} fusion(f32[16,64,32]{1,0,2:T(8,128)S(1)} %mul.208, f32[64,64,32]{1,2,0:T(8,128)S(1)} %fusion), kind=kOutput, calls=%fused_computation.13 | convolution fusion | flops 25165824 | bytes 786432 | tf_op jit(solution)/shard_map/tsc,bsc->btc/dot_general | solution.py:69
  200.3 1.3 convolution_bitcast_fusion.1
  201.6 0.2 copy.29
  201.7 1.5 multiply_reduce_fusion
  203.2 0.2 copy.31
  203.4 1.5 fusion.1
  204.9 0.1 reshape.136
  205.0 0.0 copy-done.6
  205.1 0.1 fusion.26
  205.2 0.2 broadcast_in_dim.12
  205.3 63.9 %all_to_all.19 = bf16[128,128,32]{1,2,0:T(8,128)(2,1)S(1)} all-to-all(bf16[128,128,32]{1,2,0:T(8,128)(2,1)S(1)} %bitcast.78), channel_id=1, replica_groups=mesh['dp'=4,'seq'=8,'tensor'=16] {'seq','tensor'}, dimensions={0} | all-to-all | bytes 2097152 | tf_op jit(solution)/shard_map/all_to_all | solution.py:87
  269.2 0.1 copy.33
  269.3 1.2 convolution_convert_fusion
  (21 shorter events, 0.1 us)
Async XLA Ops:
  6.5 262.8 %copy-start = (bf16[4096,256]{1,0:T(8,128)(2,1)S(1)}, bf16[4096,256]{1,0:T(8,128)(2,1)}, u32[]{:S(2)}) copy-start(bf16[4096,256]{1,0:T(8,128)(2,1)} %param.13) | copy-start | bytes 6291460
  6.5 46.2 %copy-start.1 = (bf16[512,3,256]{2,0,1:T(8,128)(2,1)S(1)}, bf16[512,3,256]{2,0,1:T(8,128)(2,1)}, u32[]{:S(2)}) copy-start(bf16[512,3,256]{2,0,1:T(8,128)(2,1)} %param.8) | copy-start | bytes 2359300
  6.5 188.2 %reduce-scatter.2.cloned.1.call-start = ((), (), s32[]{:S(2)}) async-start(), calls=%async_computation.3 | async-start | bytes 3538944 | tf_op jit(solution)/shard_map/reduce_scatter | solution.py:39
  43.1 0.7 collective-permute-start
  43.8 12.1 %collective-permute-start.1 = (bf16[1024,256]{1,0:T(8,128)(2,1)S(1)}, bf16[1024,256]{1,0:T(8,128)(2,1)}, u32[]{:S(2)}, u32[]{:S(2)}) collective-permute-start(bf16[1024,256]{1,0:T(8,128)(2,1)S(1)} %collective-permute-done), channel_id=1, source_target_pairs={{0,1},{1,0},{2,3},{3,2},{4,5},{5,4},{6,7},{7,6},{8,9},{9,8},{10,11... | collective-permute-start | bytes 1572872 | tf_op jit(solution)/shard_map/ppermute | solution.py:30
  63.6 1.1 copy-start.4
  63.6 1.1 copy-start.5
  63.6 2.1 copy-start.8
  64.8 3.8 %copy-start.3 = (f32[16,32]{1,0:T(8,128)}, f32[16,32]{1,0:T(8,128)S(1)}, u32[]{:S(2)}) copy-start(f32[16,32]{1,0:T(8,128)S(1)} %get-tuple-element.14) | copy-start | bytes 6148
  66.3 2.3 copy-start.7
  200.3 4.7 %copy-start.2 = (f32[4,8,8,128]{3,1,2,0:T(8,128)S(1)}, f32[4,8,8,128]{3,1,2,0:T(8,128)}, u32[]{:S(2)}) copy-start(f32[4,8,8,128]{3,1,2,0:T(8,128)} %get-tuple-element.5) | copy-start | bytes 393220
  200.3 4.8 %copy-start.6 = (f32[32]{0:T(128)S(1)}, f32[32]{0:T(128)}, u32[]{:S(2)}) copy-start(f32[32]{0:T(128)} %dynamic_slice.19) | copy-start | bytes 388
Sparse Core Ops, SparseCore 0:
  63.8 130.9 reduce-scatter.1

commit v5 on v3

--- a/solution.py
+++ b/solution.py
@@ -7,32 +7,9 @@
 block_len = 64
 
 
-def body(features, in_weight, short_taps, decay_rates, residues, skip_gain, out_weight):
-    seq_n = lax.axis_size("seq")
-    ten_n = lax.axis_size("tensor")
-    place = lax.axis_index("seq")
-    lane = lax.axis_index("tensor")
-    tok_rows, fcols = features.shape
-    rows_here, branches, channels = in_weight.shape
-    halves = rows_here // fcols
-    sub = channels // seq_n
-    length = tok_rows * seq_n
-    taps_count = short_taps.shape[1]
-    copies = jnp.tile(features, (ten_n, 1))
-    own_tokens = lax.all_to_all(copies, "tensor", 0, 1, tiled=True)
-    rows_of_feats = lax.all_to_all(own_tokens, "seq", 1, 0, tiled=True)
-    weight_rows = in_weight.reshape(rows_here, branches, seq_n, sub)
-    partial = jnp.einsum(
-        "td,djgc->gtjc", rows_of_feats, weight_rows, preferred_element_type=jnp.float32
-    )
-    summed = lax.psum_scatter(partial.reshape(seq_n * length, -1), "seq", scatter_dimension=0, tiled=True)
-    summed = summed.reshape(length, branches, sub)
-    projected = lax.reduce_precision(summed, exponent_bits=8, mantissa_bits=7)
-
-    taps = lax.dynamic_slice_in_dim(short_taps, place * sub, sub, axis=2)
-    decay = lax.dynamic_slice_in_dim(decay_rates, place * sub, sub, axis=1)
-    resid = lax.dynamic_slice_in_dim(residues, place * sub, sub, axis=1)
-    skip = lax.dynamic_slice_in_dim(skip_gain, place * sub, sub, axis=0)
+def mix_channels(projected, taps, decay, resid, skip):
+    length, branches, sub = projected.shape
+    taps_count = taps.shape[1]
 
     rim_rows = taps_count - 1
     extended = jnp.concatenate(
@@ -70,16 +47,65 @@
     outer = jnp.einsum("mic,bmc->bic", amplitude[:, None, :] * falloff, starts, precision=precise)
     conv = (inner + outer).reshape(length, sub)
     gated = (short[:, 0, :] * (conv + skip[None, :] * product)).astype(jnp.bfloat16)
-    outgoing = jnp.broadcast_to(
-        gated.reshape(seq_n, 1, tok_rows, sub), (seq_n, ten_n, tok_rows, sub)
-    ).reshape(seq_n * ten_n * tok_rows, sub)
-    incoming = lax.all_to_all(outgoing, ("seq", "tensor"), 0, 0, tiled=True)
-    incoming = incoming.reshape(seq_n, ten_n, tok_rows, sub).transpose(2, 1, 0, 3)
-    mixed = jnp.dot(
-        incoming.reshape(tok_rows, ten_n * seq_n * sub),
-        out_weight,
-        preferred_element_type=jnp.float32,
+    return gated
+
+
+def body(features, in_weight, short_taps, decay_rates, residues, skip_gain, out_weight):
+    seq_n = lax.axis_size("seq")
+    ten_n = lax.axis_size("tensor")
+    place = lax.axis_index("seq")
+    lane = lax.axis_index("tensor")
+    tok_rows, fcols = features.shape
+    rows_here, branches, channels = in_weight.shape
+    halves = rows_here // fcols
+    sub = channels // seq_n
+    length = tok_rows * seq_n
+    chunks = 2
+    copies = jnp.tile(features, (seq_n, 1))
+    my_columns = lax.all_to_all(copies, "seq", 0, 0, tiled=True)
+    across = []
+    for s in range(seq_n):
+        for a in range(seq_n):
+            for b in range(halves):
+                across.append((a * ten_n + s * halves + b, s * ten_n + a * halves + b))
+    first = lax.ppermute(my_columns, ("seq", "tensor"), across)
+    swap = [(k, k + 1 - 2 * (k % 2)) for k in range(ten_n)]
+    second = lax.ppermute(first, "tensor", swap)
+    rows_of_feats = jnp.concatenate([first, second], axis=1)
+    half_of = lane % halves
+    doubled = jnp.concatenate([in_weight, in_weight], axis=0)
+    weight_rows = lax.dynamic_slice_in_dim(doubled, half_of * fcols, rows_here, axis=0)
+    weight_rows = weight_rows.reshape(rows_here, branches, seq_n, sub)
+    partial = jnp.einsum(
+        "td,djgc->gtjc", rows_of_feats, weight_rows, preferred_element_type=jnp.float32
     )
+    taps = lax.dynamic_slice_in_dim(short_taps, place * sub, sub, axis=2)
+    decay = lax.dynamic_slice_in_dim(decay_rates, place * sub, sub, axis=1)
+    resid = lax.dynamic_slice_in_dim(residues, place * sub, sub, axis=1)
+    skip = lax.dynamic_slice_in_dim(skip_gain, place * sub, sub, axis=0)
+    weight_out = out_weight.reshape(ten_n, seq_n, chunks, sub // chunks, -1)
+    part_len = sub // chunks
+    mixed = None
+    for q in range(chunks):
+        cut = slice(q * part_len, (q + 1) * part_len)
+        piece = partial[..., cut].reshape(seq_n * length, branches * part_len)
+        summed = lax.psum_scatter(piece, "seq", scatter_dimension=0, tiled=True)
+        projected = lax.reduce_precision(
+            summed.reshape(length, branches, part_len), exponent_bits=8, mantissa_bits=7
+        )
+        gated = mix_channels(projected, taps[..., cut], decay[:, cut], resid[:, cut], skip[cut])
+        outgoing = jnp.broadcast_to(
+            gated.reshape(seq_n, 1, tok_rows, part_len), (seq_n, ten_n, tok_rows, part_len)
+        ).reshape(seq_n * ten_n * tok_rows, part_len)
+        incoming = lax.all_to_all(outgoing, ("seq", "tensor"), 0, 0, tiled=True)
+        incoming = incoming.reshape(seq_n, ten_n, tok_rows, part_len).transpose(2, 1, 0, 3)
+        rows = weight_out[:, :, q].reshape(ten_n * seq_n * part_len, -1)
+        term = jnp.dot(
+            incoming.reshape(tok_rows, ten_n * seq_n * part_len),
+            rows,
+            preferred_element_type=jnp.float32,
+        )
+        mixed = term if mixed is None else mixed + term
     return mixed.astype(jnp.bfloat16)
 
 

time: 314 us -> 342 us (1.089)
  waiting for transfers between devices: 118 us -> 226 us
  blocking collectives: 113 us -> 35.6 us
    reduce_scatter x1 -> x2, waiting for transfers between devices: 84.1 us -> 170 us  [body(): summed = lax.psum_scatter(piece, 'seq', scatter_dimension=0, tiled=True)]
    all_to_all x2 -> x1, blocking collectives: 113 us -> 35.6 us  [body(): my_columns = lax.all_to_all(copies, 'seq', 0, 0, tiled=True)]
    all_to_all x1 -> x2, waiting for transfers between devices: 33.3 us -> 55.5 us  [body(): incoming = lax.all_to_all(outgoing, ('seq', 'tensor'), 0, 0, tiled=True)]
    ppermute x0 -> x2, starting transfers between devices: none -> 9.58 us  [the longest x1 8.9 us: body(): second = lax.ppermute(first, 'tensor', swap)]
    all_to_all x1 -> x2, starting transfers between devices: 32.6 us -> 23.5 us  [body(): incoming = lax.all_to_all(outgoing, ('seq', 'tensor'), 0, 0, tiled=True)]
    unnamed x27 -> x24, local copies, waits for them, and re-layouts: 8.34 us -> 4.22 us
    dot_general x6 -> x12, matrix products: 10.9 us -> 11.9 us  [the longest x2 6.38 us: mix_channels(): toeplitz = jnp.einsum('tsk,kc->tsc', select, kernel, precision=precise)]
  transfers between devices with their start and end apart: 2 -> 6, of which waited for: 2 -> 5; matrix products, arithmetic and copies ran while one was open for 3% -> 5% of each run, Pallas kernels for 0% -> 0%
where the time goes in v5:
time: 342 us; the launch traced here: 340 us
  waiting for transfers between devices  226 us (66%)
  blocking collectives  35.6 us (10%)
  starting transfers between devices  33.1 us (10%)
  between operations  13.9 us (4%)
  local copies, waits for them, and re-layouts  13.7 us (4%)
  matrix products  12.9 us (4%)
  other arithmetic  5.18 us (2%)
    reduce_scatter x2, waiting for transfers between devices, body(): summed = lax.psum_scatter(piece, 'seq', scatter_dimension=0, tiled=True)  170 us
    all_to_all x2, waiting for transfers between devices, body(): incoming = lax.all_to_all(outgoing, ('seq', 'tensor'), 0, 0, tiled=True)  55.5 us
    all_to_all x1, blocking collectives, body(): my_columns = lax.all_to_all(copies, 'seq', 0, 0, tiled=True)  35.6 us
    all_to_all x2, starting transfers between devices, body(): incoming = lax.all_to_all(outgoing, ('seq', 'tensor'), 0, 0, tiled=True)  23.5 us
    ppermute x1, starting transfers between devices, body(): second = lax.ppermute(first, 'tensor', swap)  8.9 us
  transfers between devices with their start and end apart: 6, of which 5 were waited for; matrix products, arithmetic and copies ran while one was open for 5% of the time, Pallas kernels for 0%

profile of v5, /device:TPU:1, one launch (start us, length us, event | category | flops | bytes accessed | tf_op | source)
XLA Modules:
  0.0 340.3 jit_solution(13560674049457215604)
XLA Ops:
  6.5 0.9 tile.2
  7.5 35.6 %all_to_all.27 = bf16[8,128,256]{2,1,0:T(8,128)(2,1)S(1)} all-to-all(bf16[8,128,256]{2,1,0:T(8,128)(2,1)S(1)} %tile.2), channel_id=1, replica_groups=mesh['dp'=4,'seq'=8,'tensor'=16] {'seq'}, dimensions={0} | all-to-all | bytes 1048576 | tf_op jit(solution)/shard_map/all_to_all | solution.py:65
  43.1 0.7 collective-permute-start
  43.8 8.9 %collective-permute-start.1 = (bf16[1024,256]{1,0:T(8,128)(2,1)S(1)}, bf16[1024,256]{1,0:T(8,128)(2,1)S(1)}, u32[]{:S(2)}, u32[]{:S(2)}) collective-permute-start(bf16[1024,256]{1,0:T(8,128)(2,1)S(1)} %collective-permute-done), channel_id=1, source_target_pairs={{0,1},{1,0},{2,3},{3,2},{4,5},{5,4},{6,7},{7,6},{8,9},{9,8},{10,11... | collective-permute-start | bytes 1572872 | tf_op jit(solution)/shard_map/ppermute | solution.py:73
  52.7 0.8 fusion.9
  53.5 0.3 copy.39
  53.8 0.4 collective-permute-done.1
  54.2 1.0 convolution_bitcast_fusion
  55.2 0.3 fusion.67
  55.5 0.9 copy.40
  56.5 2.0 copy.75
  58.6 0.1 constant_dynamic-slice_fusion.11
  58.8 0.1 dynamic-slice_multiply_fusion
  59.2 0.9 copy.48
  60.2 2.1 copy.78
  62.4 0.3 fusion.40
  62.7 3.2 fusion
  65.9 104.6 %reduce-scatter.3.cloned.1.call-done = f32[1024,48]{0,1:T(8,128)} async-done(((f32[8192,48]{0,1:T(8,128)}), f32[1024,48]{0,1:T(8,128)}) %reduce-scatter.3.cloned.1.call-update) | async-done | bytes 196624 | tf_op jit(solution)/shard_map/reduce_scatter | solution.py:92
  170.6 0.9 reduce_precision.12
  171.5 0.4 fusion.18
  172.1 0.4 convolution_bitcast_fusion.2
  172.5 0.1 copy.43
  172.6 65.4 %reduce-scatter.5.cloned.1.call-done = f32[1024,48]{0,1:T(8,128)} async-done(((f32[8192,48]{0,1:T(8,128)}), f32[1024,48]{0,1:T(8,128)}) %reduce-scatter.5.cloned.1.call-update) | async-done | bytes 196624 | tf_op jit(solution)/shard_map/reduce_scatter | solution.py:92
  238.0 0.9 reduce_precision.14
  238.9 0.4 fusion.30
  239.5 0.4 convolution_bitcast_fusion.1
  239.9 0.1 copy.51
  240.0 1.3 multiply_reduce_fusion
  241.3 0.1 copy.53
  241.5 0.3 fusion.36
  241.8 1.0 fusion.2
  243.0 0.1 fusion.48
  243.1 0.9 broadcast_in_dim.25
  243.9 14.4 %all-to-all-start.2 = ((bf16[128,128,16]{1,2,0:T(8,128)(2,1)}), bf16[128,128,16]{1,2,0:T(8,128)(2,1)S(1)}, u32[]{:S(2)}, u32[]{:S(2)}) async-start(bf16[128,128,16]{1,2,0:T(8,128)(2,1)} %bitcast.25), calls=%async_computation.4 | async-start | bytes 1048576 | tf_op jit(solution)/shard_map/all_to_all | solution.py:100
  258.5 0.3 fusion.45
  258.8 3.2 fusion.1
  262.0 0.1 copy.45
  262.1 0.3 fusion.41
  262.5 1.0 fusion.3
  263.6 0.1 fusion.51
  263.8 26.1 %all-to-all-done.2 = bf16[128,128,16]{1,2,0:T(8,128)(2,1)S(1)} async-done(((bf16[128,128,16]{1,2,0:T(8,128)(2,1)}), bf16[128,128,16]{1,2,0:T(8,128)(2,1)S(1)}, u32[]{:S(2)}, u32[]{:S(2)}) %all-to-all-start.2) | async-done | bytes 524320 | tf_op jit(solution)/shard_map/all_to_all | solution.py:100
  289.9 0.9 broadcast_in_dim.24
  290.7 9.1 %all-to-all-start.1 = ((bf16[128,128,16]{1,2,0:T(8,128)(2,1)}), bf16[128,128,16]{1,2,0:T(8,128)(2,1)}, u32[]{:S(2)}, u32[]{:S(2)}) async-start(bf16[128,128,16]{1,2,0:T(8,128)(2,1)} %bitcast.12), calls=%async_computation.2 | async-start | bytes 1048576 | tf_op jit(solution)/shard_map/all_to_all | solution.py:100
  299.8 1.7 fusion.68
  301.6 29.4 %all-to-all-done.1 = bf16[128,128,16]{1,2,0:T(8,128)(2,1)} async-done(((bf16[128,128,16]{1,2,0:T(8,128)(2,1)}), bf16[128,128,16]{1,2,0:T(8,128)(2,1)}, u32[]{:S(2)}, u32[]{:S(2)}) %all-to-all-start.1) | async-done | bytes 524320 | tf_op jit(solution)/shard_map/all_to_all | solution.py:100
  331.0 1.1 copy.47
  332.1 0.4 fusion.70
  332.4 1.0 fusion.4
  (49 shorter events, 1.2 us)
Async XLA Ops:
  6.5 46.1 %copy-start = (bf16[512,3,256]{2,0,1:T(8,128)(2,1)S(1)}, bf16[512,3,256]{2,0,1:T(8,128)(2,1)}, u32[]{:S(2)}) copy-start(bf16[512,3,256]{2,0,1:T(8,128)(2,1)} %param.8) | copy-start | bytes 2359300
  6.5 164.0 %reduce-scatter.3.cloned.1.call-start = ((), (), s32[]{:S(2)}) async-start(), calls=%async_computation.5 | async-start | bytes 1769472 | tf_op jit(solution)/shard_map/reduce_scatter | solution.py:92
  43.1 0.7 collective-permute-start
  43.8 10.4 %collective-permute-start.1 = (bf16[1024,256]{1,0:T(8,128)(2,1)S(1)}, bf16[1024,256]{1,0:T(8,128)(2,1)S(1)}, u32[]{:S(2)}, u32[]{:S(2)}) collective-permute-start(bf16[1024,256]{1,0:T(8,128)(2,1)S(1)} %collective-permute-done), channel_id=1, source_target_pairs={{0,1},{1,0},{2,3},{3,2},{4,5},{5,4},{6,7},{7,6},{8,9},{9,8},{10,11... | collective-permute-start | bytes 1572872 | tf_op jit(solution)/shard_map/ppermute | solution.py:73
  56.4 2.2 copy-start.1
  56.4 2.3 copy-start.2
  56.5 2.3 copy-start.3
  56.5 2.7 copy-start.4
  58.5 179.5 %reduce-scatter.5.cloned.1.call-start = ((), (), s32[]{:S(2)}) async-start(), calls=%async_computation.6 | async-start | bytes 1769472 | tf_op jit(solution)/shard_map/reduce_scatter | solution.py:92
  243.9 45.9 %all-to-all-start.2 = ((bf16[128,128,16]{1,2,0:T(8,128)(2,1)}), bf16[128,128,16]{1,2,0:T(8,128)(2,1)S(1)}, u32[]{:S(2)}, u32[]{:S(2)}) async-start(bf16[128,128,16]{1,2,0:T(8,128)(2,1)} %bitcast.25), calls=%async_computation.4 | async-start | bytes 1048576 | tf_op jit(solution)/shard_map/all_to_all | solution.py:100
  290.7 40.2 %all-to-all-start.1 = ((bf16[128,128,16]{1,2,0:T(8,128)(2,1)}), bf16[128,128,16]{1,2,0:T(8,128)(2,1)}, u32[]{:S(2)}, u32[]{:S(2)}) async-start(bf16[128,128,16]{1,2,0:T(8,128)(2,1)} %bitcast.12), calls=%async_computation.2 | async-start | bytes 1048576 | tf_op jit(solution)/shard_map/all_to_all | solution.py:100
Sparse Core Ops, SparseCore 0:
  58.7 111.8 reduce-scatter.2
  173.4 64.5 reduce-scatter.4

commit v6 on v4

--- a/solution.py
+++ b/solution.py
@@ -9,9 +9,12 @@
 
 def body(features, in_weight, short_taps, decay_rates, residues, skip_gain, out_weight):
     seq_n = lax.axis_size("seq")
-    ten_n = lax.axis_size("tensor")
+    outer_n = lax.axis_size("zhi")
+    inner_n = lax.axis_size("inner")
+    ten_n = outer_n * inner_n
     place = lax.axis_index("seq")
-    lane = lax.axis_index("tensor")
+    far = lax.axis_index("zhi")
+    lane = far * inner_n + lax.axis_index("inner")
     tok_rows, fcols = features.shape
     rows_here, branches, channels = in_weight.shape
     halves = rows_here // fcols
@@ -25,9 +28,9 @@
         for a in range(seq_n):
             for b in range(halves):
                 across.append((a * ten_n + s * halves + b, s * ten_n + a * halves + b))
-    first = lax.ppermute(my_columns, ("seq", "tensor"), across)
-    swap = [(k, k + 1 - 2 * (k % 2)) for k in range(ten_n)]
-    second = lax.ppermute(first, "tensor", swap)
+    first = lax.ppermute(my_columns, ("seq", "zhi", "inner"), across)
+    swap = [(k, k + 1 - 2 * (k % 2)) for k in range(inner_n)]
+    second = lax.ppermute(first, "inner", swap)
     rows_of_feats = jnp.concatenate([first, second], axis=1)
     half_of = lane % halves
     doubled = jnp.concatenate([in_weight, in_weight], axis=0)
@@ -81,13 +84,12 @@
     outer = jnp.einsum("mic,bmc->bic", amplitude[:, None, :] * falloff, starts, precision=precise)
     conv = (inner + outer).reshape(length, sub)
     gated = (short[:, 0, :] * (conv + skip[None, :] * product)).astype(jnp.bfloat16)
-    outgoing = jnp.broadcast_to(
-        gated.reshape(seq_n, 1, tok_rows, sub), (seq_n, ten_n, tok_rows, sub)
-    ).reshape(seq_n * ten_n * tok_rows, sub)
-    incoming = lax.all_to_all(outgoing, ("seq", "tensor"), 0, 0, tiled=True)
-    incoming = incoming.reshape(seq_n, ten_n, tok_rows, sub).transpose(2, 1, 0, 3)
+    gated = lax.all_to_all(gated, "seq", 0, 1, tiled=True)
+    opposite = lax.ppermute(gated, "zhi", [(z, outer_n - 1 - z) for z in range(outer_n)])
+    pair = jnp.where(far == 0, jnp.stack([gated, opposite], 1), jnp.stack([opposite, gated], 1))
+    whole = lax.all_gather(pair, "inner", axis=2, tiled=False)
     mixed = jnp.dot(
-        incoming.reshape(tok_rows, ten_n * seq_n * sub),
+        whole.reshape(tok_rows, ten_n * channels),
         out_weight,
         preferred_element_type=jnp.float32,
     )
@@ -95,14 +97,22 @@
 
 
 def solution(mesh):
+    devices = mesh.devices
+    halves_mesh = jax.sharding.Mesh(
+        devices.reshape(devices.shape[0], devices.shape[1], 2, devices.shape[2] // 2),
+        ("dp", "seq", "zhi", "inner"),
+    )
+    tensor = ("zhi", "inner")
     in_specs = (
-        P(("dp", "seq"), "tensor"),
-        P("seq", None, "tensor"),
-        P(None, None, "tensor"),
-        P(None, "tensor"),
-        P(None, "tensor"),
-        P("tensor"),
-        P(None, "tensor"),
+        P(("dp", "seq"), tensor),
+        P("seq", None, tensor),
+        P(None, None, tensor),
+        P(None, tensor),
+        P(None, tensor),
+        P(tensor),
+        P(None, tensor),
     )
-    out_specs = P(("dp", "seq"), "tensor")
-    return jax.shard_map(body, mesh=mesh, in_specs=in_specs, out_specs=out_specs, check_vma=False)
+    out_specs = P(("dp", "seq"), tensor)
+    return jax.shard_map(
+        body, mesh=halves_mesh, in_specs=in_specs, out_specs=out_specs, check_vma=False
+    )

time: 280 us -> 278 us (level)
  blocking collectives: 99.4 us -> 48.5 us
  waiting for transfers between devices: 123 us -> 161 us
  starting transfers between devices: 9.59 us -> 20.9 us
    all_to_all x1, blocking collectives: 63.9 us -> 12.9 us  [body(): gated = lax.all_to_all(gated, 'seq', 0, 1, tiled=True)]
    all_gather x0 -> x1, waiting for transfers between devices: none -> 35.6 us  [body(): whole = lax.all_gather(pair, 'inner', axis=2, tiled=False)]
    ppermute x2 -> x3, starting transfers between devices: 9.59 us -> 20.7 us  [the longest x1 11.1 us: body(): lax.ppermute(gated, 'zhi', [(z, outer_n - 1 - z) for z in range(outer_n)])]
  transfers between devices with their start and end apart: 3 -> 5, of which waited for: 1 -> 3; matrix products, arithmetic and copies ran while one was open for 4% -> 4% of each run, Pallas kernels for 0% -> 0%
where the time goes in v6:
time: 278 us
  waiting for transfers between devices  161 us (58%)
  blocking collectives  48.5 us (17%)
  starting transfers between devices  20.9 us (8%)
  matrix products  14.2 us (5%)
  between operations  13.7 us (5%)
  local copies, waits for them, and re-layouts  11.5 us (4%)
  other arithmetic  8.35 us (3%)
    reduce_scatter x1, waiting for transfers between devices, body(): lax.psum_scatter(partial.reshape(seq_n * length, -1), 'seq', scatter_dime...  122 us
    all_gather x1, waiting for transfers between devices, body(): whole = lax.all_gather(pair, 'inner', axis=2, tiled=False)  35.6 us
    all_to_all x1, blocking collectives, body(): my_columns = lax.all_to_all(copies, 'seq', 0, 0, tiled=True)  35.6 us
    all_to_all x1, blocking collectives, body(): gated = lax.all_to_all(gated, 'seq', 0, 1, tiled=True)  12.9 us
    ppermute x1, starting transfers between devices, body(): lax.ppermute(gated, 'zhi', [(z, outer_n - 1 - z) for z in range(outer_n)])  11.1 us
    ppermute x1, starting transfers between devices, body(): second = lax.ppermute(first, 'inner', swap)  8.9 us
  transfers between devices with their start and end apart: 5, of which 3 were waited for; matrix products, arithmetic and copies ran while one was open for 4% of the time, Pallas kernels for 0%

profile of v6, /device:TPU:1, one launch (start us, length us, event | category | flops | bytes accessed | tf_op | source)
XLA Modules:
  0.0 277.7 jit_solution(7524622134841934787)
XLA Ops:
  6.5 0.0 copy-start
  6.5 0.0 reduce-scatter.2.cloned.1.call-start
  6.5 1.0 tile.2
  7.6 35.6 %all_to_all.25 = bf16[8,128,256]{2,1,0:T(8,128)(2,1)S(1)} all-to-all(bf16[8,128,256]{2,1,0:T(8,128)(2,1)S(1)} %tile.2), channel_id=1, replica_groups=mesh['dp'=4,'seq'=8,'zhi'=2,'inner'=8] {'seq'}, dimensions={0} | all-to-all | bytes 1048576 | tf_op jit(solution)/shard_map/all_to_all | solution.py:25
  43.1 0.7 collective-permute-start
  43.8 0.0 collective-permute-done
  43.8 8.9 %collective-permute-start.1 = (bf16[1024,256]{1,0:T(8,128)(2,1)S(1)}, bf16[1024,256]{1,0:T(8,128)(2,1)}, u32[]{:S(2)}, u32[]{:S(2)}) collective-permute-start(bf16[1024,256]{1,0:T(8,128)(2,1)S(1)} %collective-permute-done), channel_id=1, source_target_pairs={{0,1},{1,0},{2,3},{3,2},{4,5},{5,4},{6,7},{7,6},{8,9},{9,8},{10,11... | collective-permute-start | bytes 1572872 | tf_op jit(solution)/shard_map/ppermute | solution.py:33
  52.8 1.7 fusion.7
  54.5 1.4 copy.40
  55.9 0.0 collective-permute-done.1
  55.9 2.0 convolution_bitcast_fusion
  58.0 1.8 copy.41
  59.8 3.8 %copy.61 = f32[12,8,8,1024]{3,1,2,0:T(8,128)} copy(f32[12,8,8,1024]{3,2,1,0:T(8,128)S(1)} %bitcast.77) | data formatting | bytes 6291456
  63.6 0.0 reduce-scatter.2.cloned.1.call-update
  63.6 0.2 all-gather.2.cloned.1.call-start
  63.9 1.1 constant_dynamic-slice_fusion.5
  65.0 0.1 dynamic-slice_negate_fusion
  65.1 0.1 copy.42
  65.1 0.7 copy.45
  65.8 0.1 copy.52
  65.9 0.6 dynamic_slice.19
  66.6 0.5 broadcast_subtract_fusion
  67.1 0.6 iota_compare_fusion.2
  67.7 0.7 convert_multiply_fusion
  68.4 0.4 fusion.23
  68.9 3.6 %fusion = f32[64,64,32]{1,2,0:T(8,128)S(1)} fusion(f32[32,64,1]{1,0,2:T(8,128)S(1)} %bitcast.87, s32[64,64]{1,0:T(8,128)S(1)} %iota_subtract_fusion), kind=kOutput, calls=%fused_computation.2 | convolution fusion | flops 100925440 | bytes 548864 | tf_op jit(solution)/shard_map/tsk,kc->tsc/dot_general | solution.py:71
  72.5 122.3 %reduce-scatter.2.cloned.1.call-done = f32[1024,96]{0,1:T(8,128)} async-done(((f32[8192,96]{0,1:T(8,128)}), f32[1024,96]{0,1:T(8,128)}) %reduce-scatter.2.cloned.1.call-update) | async-done | bytes 393232 | tf_op jit(solution)/shard_map/reduce_scatter | solution.py:42
  194.7 1.0 reduce_precision.6
  195.8 0.8 fusion.14
  196.6 0.7 slice_bitcast_fusion
  197.3 0.1 mul.203
  197.4 2.9 %fusion.4 = f32[32,16,64]{2,1,0:T(8,128)} fusion(f32[16,64,32]{1,0,2:T(8,128)S(1)} %mul.203, f32[64,64,32]{1,2,0:T(8,128)S(1)} %fusion), kind=kOutput, calls=%fused_computation.13 | convolution fusion | flops 25165824 | bytes 786432 | tf_op jit(solution)/shard_map/tsc,bsc->btc/dot_general | solution.py:72
  200.3 1.3 convolution_bitcast_fusion.1
  201.6 0.2 copy.44
  201.7 1.5 multiply_reduce_fusion
  203.2 0.2 copy.46
  203.4 1.5 fusion.1
  204.9 0.1 reshape.173
  205.0 0.1 fusion.26
  205.2 12.9 %all_to_all.26 = bf16[8,128,32]{1,2,0:T(8,128)(2,1)S(1)} all-to-all(bf16[8,128,32]{1,2,0:T(8,128)(2,1)S(1)} %copy.47), channel_id=1, replica_groups=mesh['dp'=4,'seq'=8,'zhi'=2,'inner'=8] {'seq'}, dimensions={0} | all-to-all | bytes 131072 | tf_op jit(solution)/shard_map/all_to_all | solution.py:87
  218.1 11.1 %collective-permute-start.2 = (bf16[128,256]{0,1:T(8,128)(2,1)S(1)}, bf16[128,256]{0,1:T(8,128)(2,1)S(1)}, u32[]{:S(2)}, u32[]{:S(2)}) collective-permute-start(bf16[128,256]{0,1:T(8,128)(2,1)S(1)} %bitcast.84), channel_id=1, source_target_pairs={{0,8},{8,0},{1,9},{9,1},{2,10},{10,2},{3,11},{11,3},{4,12},{12,4},... | collective-permute-start | bytes 196616 | tf_op jit(solution)/shard_map/ppermute | solution.py:88
  229.2 2.6 collective-permute-done.2
  231.8 0.1 copy.48
  231.9 0.1 copy.49
  232.1 0.7 maximum_select_fusion
  232.8 0.0 all-gather.2.cloned.1.call-update
  232.8 35.6 %all-gather.2.cloned.1.call-done = bf16[128,2,8,256]{0,3,2,1:T(8,128)(2,1)} async-done(((bf16[128,2,1,256]{0,3,2,1:T(8,128)(2,1)}), bf16[128,2,8,256]{0,3,2,1:T(8,128)(2,1)}) %all-gather.2.cloned.1.call-update) | async-done | bytes 1048592 | tf_op jit(solution)/shard_map/all_gather | solution.py:90
  268.4 2.4 convolution_convert_fusion
  (27 shorter events, 0.1 us)
Async XLA Ops:
  6.5 261.9 %copy-start = (bf16[4096,256]{1,0:T(8,128)(2,1)S(1)}, bf16[4096,256]{1,0:T(8,128)(2,1)}, u32[]{:S(2)}) copy-start(bf16[4096,256]{1,0:T(8,128)(2,1)} %param.13) | copy-start | bytes 6291460
  6.5 46.2 %copy-start.1 = (bf16[512,3,256]{2,0,1:T(8,128)(2,1)S(1)}, bf16[512,3,256]{2,0,1:T(8,128)(2,1)}, u32[]{:S(2)}) copy-start(bf16[512,3,256]{2,0,1:T(8,128)(2,1)} %param.8) | copy-start | bytes 2359300
  6.5 188.2 %reduce-scatter.2.cloned.1.call-start = ((), (), s32[]{:S(2)}) async-start(), calls=%async_computation.3 | async-start | bytes 3538944 | tf_op jit(solution)/shard_map/reduce_scatter | solution.py:42
  43.1 0.7 collective-permute-start
  43.8 12.1 %collective-permute-start.1 = (bf16[1024,256]{1,0:T(8,128)(2,1)S(1)}, bf16[1024,256]{1,0:T(8,128)(2,1)}, u32[]{:S(2)}, u32[]{:S(2)}) collective-permute-start(bf16[1024,256]{1,0:T(8,128)(2,1)S(1)} %collective-permute-done), channel_id=1, source_target_pairs={{0,1},{1,0},{2,3},{3,2},{4,5},{5,4},{6,7},{7,6},{8,9},{9,8},{10,11... | collective-permute-start | bytes 1572872 | tf_op jit(solution)/shard_map/ppermute | solution.py:33
  63.6 1.3 copy-start.4
  63.6 1.4 copy-start.5
  63.6 2.3 copy-start.8
  63.6 204.8 %all-gather.2.cloned.1.call-start = ((), (), s32[]{:S(2)}) async-start(), calls=%async_computation.4 | async-start | bytes 1179648 | tf_op jit(solution)/shard_map/all_gather | solution.py:90
  65.1 3.8 %copy-start.3 = (f32[16,32]{1,0:T(8,128)}, f32[16,32]{1,0:T(8,128)S(1)}, u32[]{:S(2)}) copy-start(f32[16,32]{1,0:T(8,128)S(1)} %get-tuple-element.14) | copy-start | bytes 6148
  66.6 2.3 copy-start.7
  200.3 4.7 %copy-start.2 = (f32[4,8,8,128]{3,1,2,0:T(8,128)S(1)}, f32[4,8,8,128]{3,1,2,0:T(8,128)}, u32[]{:S(2)}) copy-start(f32[4,8,8,128]{3,1,2,0:T(8,128)} %get-tuple-element.5) | copy-start | bytes 393220
  200.3 4.8 %copy-start.6 = (f32[32]{0:T(128)S(1)}, f32[32]{0:T(128)}, u32[]{:S(2)}) copy-start(f32[32]{0:T(128)} %dynamic_slice.19) | copy-start | bytes 388
  218.1 13.7 %collective-permute-start.2 = (bf16[128,256]{0,1:T(8,128)(2,1)S(1)}, bf16[128,256]{0,1:T(8,128)(2,1)S(1)}, u32[]{:S(2)}, u32[]{:S(2)}) collective-permute-start(bf16[128,256]{0,1:T(8,128)(2,1)S(1)} %bitcast.84), channel_id=1, source_target_pairs={{0,8},{8,0},{1,9},{9,1},{2,10},{10,2},{3,11},{11,3},{4,12},{12,4},... | collective-permute-start | bytes 196616 | tf_op jit(solution)/shard_map/ppermute | solution.py:88
Sparse Core Ops, SparseCore 0:
  63.8 130.9 reduce-scatter.1
  232.9 35.4 all-gather.1

commit v7 on v6

--- a/solution.py
+++ b/solution.py
@@ -23,12 +23,39 @@
     taps_count = short_taps.shape[1]
     copies = jnp.tile(features, (seq_n, 1))
     my_columns = lax.all_to_all(copies, "seq", 0, 0, tiled=True)
-    across = []
+    y_n = inner_n // halves
+
+    def spot(s, z, y, b):
+        return (s * outer_n + z) * inner_n + y * halves + b
+
+    def root_of(s, b):
+        k = s * halves + b
+        return k // inner_n, (k % inner_n) // halves
+
+    over = []
     for s in range(seq_n):
-        for a in range(seq_n):
-            for b in range(halves):
-                across.append((a * ten_n + s * halves + b, s * ten_n + a * halves + b))
-    first = lax.ppermute(my_columns, ("seq", "zhi", "inner"), across)
+        for b in range(halves):
+            z_r, y_r = root_of(s, b)
+            over.append((spot(s, z_r, y_r, b), spot(s, outer_n - 1 - z_r, y_r, b)))
+    crossed = lax.ppermute(my_columns, ("seq", "zhi", "inner"), over)
+    inner = lax.axis_index("inner")
+    my_y = inner // halves
+    my_b = inner % halves
+    root_k = place * halves + my_b
+    root_z = root_k // inner_n
+    root_y = (root_k % inner_n) // halves
+    relay = jnp.where(far == root_z, my_columns, crossed)
+    first = jnp.where(far == root_z, my_columns, crossed)
+    shift = (my_y - root_y) % y_n
+    for o in range(1, y_n):
+        along = []
+        for s in range(seq_n):
+            for z in range(outer_n):
+                for b in range(halves):
+                    _, y_r = root_of(s, b)
+                    along.append((spot(s, z, y_r, b), spot(s, z, (y_r + o) % y_n, b)))
+        moved = lax.ppermute(relay, ("seq", "zhi", "inner"), along)
+        first = jnp.where(shift == o, moved, first)
     swap = [(k, k + 1 - 2 * (k % 2)) for k in range(inner_n)]
     second = lax.ppermute(first, "inner", swap)
     rows_of_feats = jnp.concatenate([first, second], axis=1)

time: 278 us -> 287 us (1.032)
  starting transfers between devices: 20.9 us -> 32.8 us
  waiting for transfers between devices: 161 us -> 157 us
    reduce_scatter x1, waiting for transfers between devices: 122 us -> 85.3 us  [body(): lax.psum_scatter(partial.reshape(seq_n * length, -1), 'seq', scatter_dime...]
    ppermute x1 -> x4, waiting for transfers between devices: 0.01 us -> 33.3 us  [the longest x1 18 us: body(): crossed = lax.ppermute(my_columns, ('seq', 'zhi', 'inner'), over)]
    ppermute x1 -> x4, starting transfers between devices: 0.68 us -> 14.2 us  [the longest x1 8.74 us: body(): crossed = lax.ppermute(my_columns, ('seq', 'zhi', 'inner'), over)]
  transfers between devices with their start and end apart: 5 -> 8, of which waited for: 3 -> 7; matrix products, arithmetic and copies ran while one was open for 4% -> 4% of each run, Pallas kernels for 0% -> 0%
where the time goes in v7:
time: 287 us; the launch traced here: 286 us
  waiting for transfers between devices  157 us (55%)
  blocking collectives  48.4 us (17%)
  starting transfers between devices  32.8 us (11%)
  matrix products  14.2 us (5%)
  between operations  13.7 us (5%)
  local copies, waits for them, and re-layouts  11.4 us (4%)
  other arithmetic  9.19 us (3%)
    reduce_scatter x1, waiting for transfers between devices, body(): lax.psum_scatter(partial.reshape(seq_n * length, -1), 'seq', scatter_dime...  85.3 us
    all_gather x1, waiting for transfers between devices, body(): whole = lax.all_gather(pair, 'inner', axis=2, tiled=False)  35.7 us
    all_to_all x1, blocking collectives, body(): my_columns = lax.all_to_all(copies, 'seq', 0, 0, tiled=True)  35.6 us
    ppermute x1, waiting for transfers between devices, body(): crossed = lax.ppermute(my_columns, ('seq', 'zhi', 'inner'), over)  18 us
    ppermute x3, waiting for transfers between devices, body(): moved = lax.ppermute(relay, ('seq', 'zhi', 'inner'), along)  15.3 us
    all_to_all x1, blocking collectives, body(): gated = lax.all_to_all(gated, 'seq', 0, 1, tiled=True)  12.8 us
    ppermute x1, starting transfers between devices, body(): lax.ppermute(gated, 'zhi', [(z, outer_n - 1 - z) for z in range(outer_n)])  11.2 us
    ppermute x1, starting transfers between devices, body(): crossed = lax.ppermute(my_columns, ('seq', 'zhi', 'inner'), over)  8.74 us
  transfers between devices with their start and end apart: 8, of which 7 were waited for; matrix products, arithmetic and copies ran while one was open for 4% of the time, Pallas kernels for 0%

profile of v7, /device:TPU:1, one launch (start us, length us, event | category | flops | bytes accessed | tf_op | source)
XLA Modules:
  0.0 286.5 jit_solution(2397592457525267271)
XLA Ops:
  6.5 1.0 tile.2
  7.6 35.6 %all_to_all.25 = bf16[8,128,256]{2,1,0:T(8,128)(2,1)S(1)} all-to-all(bf16[8,128,256]{2,1,0:T(8,128)(2,1)S(1)} %tile.2), channel_id=1, replica_groups=mesh['dp'=4,'seq'=8,'zhi'=2,'inner'=8] {'seq'}, dimensions={0} | all-to-all | bytes 1048576 | tf_op jit(solution)/shard_map/all_to_all | solution.py:25
  43.1 8.7 %collective-permute-start = (bf16[1024,256]{1,0:T(8,128)(2,1)S(1)}, bf16[1024,256]{1,0:T(8,128)(2,1)}, u32[]{:S(2)}, u32[]{:S(2)}) collective-permute-start(bf16[1024,256]{1,0:T(8,128)(2,1)S(1)} %bitcast.80), channel_id=1, source_target_pairs={{0,8},{1,9},{18,26},{19,27},{36,44},{37,45},{54,62},{55,63},{72,64... | collective-permute-start | bytes 1572872 | tf_op jit(solution)/shard_map/ppermute | solution.py:40
  51.9 18.0 %collective-permute-done = bf16[1024,256]{1,0:T(8,128)(2,1)} collective-permute-done((bf16[1024,256]{1,0:T(8,128)(2,1)S(1)}, bf16[1024,256]{1,0:T(8,128)(2,1)}, u32[]{:S(2)}, u32[]{:S(2)}) %collective-permute-start) | collective-permute-done | bytes 524320 | tf_op jit(solution)/shard_map/ppermute | solution.py:40
  69.9 0.1 broadcast_select_fusion
  70.0 1.3 collective-permute-start.1
  71.3 2.1 collective-permute-start.2
  73.4 2.1 collective-permute-start.3
  75.5 2.7 collective-permute-done.1
  78.2 1.3 collective-permute-done.2
  79.6 11.2 %collective-permute-done.3 = bf16[1024,256]{1,0:T(8,128)(2,1)} collective-permute-done((bf16[1024,256]{1,0:T(8,128)(2,1)S(1)}, bf16[1024,256]{1,0:T(8,128)(2,1)}, u32[]{:S(2)}, u32[]{:S(2)}) %collective-permute-start.3) | collective-permute-done | bytes 524320 | tf_op jit(solution)/shard_map/ppermute | solution.py:57
  90.8 0.1 select_select_fusion
  90.9 7.1 %collective-permute-start.4 = (bf16[1024,256]{1,0:T(8,128)(2,1)S(1)}, bf16[1024,256]{1,0:T(8,128)(2,1)}, u32[]{:S(2)}, u32[]{:S(2)}) collective-permute-start(bf16[1024,256]{1,0:T(8,128)(2,1)S(1)} %select_select_fusion), channel_id=1, source_target_pairs={{0,1},{1,0},{2,3},{3,2},{4,5},{5,4},{6,7},{7,6},{8,9},{9,8},{10,11... | collective-permute-start | bytes 1572872 | tf_op jit(solution)/shard_map/ppermute | solution.py:60
  98.0 2.4 fusion.7
  100.4 1.4 copy.40
  101.8 2.0 convolution_bitcast_fusion
  103.8 1.8 copy.41
  105.7 3.8 %copy.61 = f32[12,8,8,1024]{3,1,2,0:T(8,128)} copy(f32[12,8,8,1024]{3,2,1,0:T(8,128)S(1)} %bitcast.78) | data formatting | bytes 6291456
  109.5 0.2 all-gather.2.cloned.1.call-start
  109.8 1.1 constant_dynamic-slice_fusion.5
  111.0 0.7 copy.45
  111.8 0.6 dynamic_slice.19
  112.4 0.5 broadcast_subtract_fusion
  113.0 0.6 iota_compare_fusion.2
  113.6 0.7 convert_multiply_fusion
  114.2 0.4 fusion.23
  114.7 3.6 %fusion = f32[64,64,32]{1,2,0:T(8,128)S(1)} fusion(f32[32,64,1]{1,0,2:T(8,128)S(1)} %bitcast.88, s32[64,64]{1,0:T(8,128)S(1)} %iota_subtract_fusion), kind=kOutput, calls=%fused_computation.2 | convolution fusion | flops 100925440 | bytes 548864 | tf_op jit(solution)/shard_map/tsk,kc->tsc/dot_general | solution.py:98
  118.3 85.3 %reduce-scatter.2.cloned.1.call-done = f32[1024,96]{0,1:T(8,128)} async-done(((f32[8192,96]{0,1:T(8,128)}), f32[1024,96]{0,1:T(8,128)}) %reduce-scatter.2.cloned.1.call-update) | async-done | bytes 393232 | tf_op jit(solution)/shard_map/reduce_scatter | solution.py:69
  203.6 1.0 reduce_precision.6
  204.6 0.8 fusion.14
  205.4 0.7 slice_bitcast_fusion
  206.1 0.1 mul.207
  206.2 2.9 %fusion.4 = f32[32,16,64]{2,1,0:T(8,128)} fusion(f32[16,64,32]{1,0,2:T(8,128)S(1)} %mul.207, f32[64,64,32]{1,2,0:T(8,128)S(1)} %fusion), kind=kOutput, calls=%fused_computation.13 | convolution fusion | flops 25165824 | bytes 786432 | tf_op jit(solution)/shard_map/tsc,bsc->btc/dot_general | solution.py:99
  209.1 1.3 convolution_bitcast_fusion.1
  210.4 0.2 copy.44
  210.5 1.5 multiply_reduce_fusion
  212.0 0.2 copy.46
  212.2 1.5 fusion.1
  213.7 0.1 reshape.173
  213.9 0.1 fusion.26
  214.0 12.8 %all_to_all.26 = bf16[8,128,32]{1,2,0:T(8,128)(2,1)S(1)} all-to-all(bf16[8,128,32]{1,2,0:T(8,128)(2,1)S(1)} %copy.47), channel_id=1, replica_groups=mesh['dp'=4,'seq'=8,'zhi'=2,'inner'=8] {'seq'}, dimensions={0} | all-to-all | bytes 131072 | tf_op jit(solution)/shard_map/all_to_all | solution.py:114
  226.8 11.2 %collective-permute-start.5 = (bf16[128,256]{0,1:T(8,128)(2,1)S(1)}, bf16[128,256]{0,1:T(8,128)(2,1)S(1)}, u32[]{:S(2)}, u32[]{:S(2)}) collective-permute-start(bf16[128,256]{0,1:T(8,128)(2,1)S(1)} %bitcast.85), channel_id=1, source_target_pairs={{0,8},{8,0},{1,9},{9,1},{2,10},{10,2},{3,11},{11,3},{4,12},{12,4},... | collective-permute-start | bytes 196616 | tf_op jit(solution)/shard_map/ppermute | solution.py:115
  238.1 2.5 collective-permute-done.5
  240.5 0.1 copy.48
  240.7 0.1 copy.49
  240.8 0.7 maximum_select_fusion
  241.5 35.7 %all-gather.2.cloned.1.call-done = bf16[128,2,8,256]{0,3,2,1:T(8,128)(2,1)} async-done(((bf16[128,2,1,256]{0,3,2,1:T(8,128)(2,1)}), bf16[128,2,8,256]{0,3,2,1:T(8,128)(2,1)}) %all-gather.2.cloned.1.call-update) | async-done | bytes 1048592 | tf_op jit(solution)/shard_map/all_gather | solution.py:117
  277.2 2.4 convolution_convert_fusion
  (35 shorter events, 0.4 us)
Async XLA Ops:
  6.5 270.7 %copy-start = (bf16[4096,256]{1,0:T(8,128)(2,1)S(1)}, bf16[4096,256]{1,0:T(8,128)(2,1)}, u32[]{:S(2)}) copy-start(bf16[4096,256]{1,0:T(8,128)(2,1)} %param.13) | copy-start | bytes 6291460
  6.5 197.0 %reduce-scatter.2.cloned.1.call-start = ((), (), s32[]{:S(2)}) async-start(), calls=%async_computation.3 | async-start | bytes 3538944 | tf_op jit(solution)/shard_map/reduce_scatter | solution.py:69
  43.1 26.8 %collective-permute-start = (bf16[1024,256]{1,0:T(8,128)(2,1)S(1)}, bf16[1024,256]{1,0:T(8,128)(2,1)}, u32[]{:S(2)}, u32[]{:S(2)}) collective-permute-start(bf16[1024,256]{1,0:T(8,128)(2,1)S(1)} %bitcast.80), channel_id=1, source_target_pairs={{0,8},{1,9},{18,26},{19,27},{36,44},{37,45},{54,62},{55,63},{72,64... | collective-permute-start | bytes 1572872 | tf_op jit(solution)/shard_map/ppermute | solution.py:40
  70.0 8.2 %collective-permute-start.1 = (bf16[1024,256]{1,0:T(8,128)(2,1)S(1)}, bf16[1024,256]{1,0:T(8,128)(2,1)S(1)}, u32[]{:S(2)}, u32[]{:S(2)}) collective-permute-start(bf16[1024,256]{1,0:T(8,128)(2,1)S(1)} %broadcast_select_fusion), channel_id=1, source_target_pairs={{0,6},{1,7},{8,14},{9,15},{18,16},{19,17},{26,24},{27,25},{36,34},... | collective-permute-start | bytes 1572872 | tf_op jit(solution)/shard_map/ppermute | solution.py:57
  71.3 8.2 %collective-permute-start.2 = (bf16[1024,256]{1,0:T(8,128)(2,1)S(1)}, bf16[1024,256]{1,0:T(8,128)(2,1)}, u32[]{:S(2)}, u32[]{:S(2)}) collective-permute-start(bf16[1024,256]{1,0:T(8,128)(2,1)S(1)} %broadcast_select_fusion), channel_id=1, source_target_pairs={{0,4},{1,5},{8,12},{9,13},{18,22},{19,23},{26,30},{27,31},{36,32},... | collective-permute-start | bytes 1572872 | tf_op jit(solution)/shard_map/ppermute | solution.py:57
  73.4 17.4 %collective-permute-start.3 = (bf16[1024,256]{1,0:T(8,128)(2,1)S(1)}, bf16[1024,256]{1,0:T(8,128)(2,1)}, u32[]{:S(2)}, u32[]{:S(2)}) collective-permute-start(bf16[1024,256]{1,0:T(8,128)(2,1)S(1)} %broadcast_select_fusion), channel_id=1, source_target_pairs={{0,2},{1,3},{8,10},{9,11},{18,20},{19,21},{26,28},{27,29},{36,38},... | collective-permute-start | bytes 1572872 | tf_op jit(solution)/shard_map/ppermute | solution.py:57
  78.2 1.3 copy-start.2
  90.9 10.9 %collective-permute-start.4 = (bf16[1024,256]{1,0:T(8,128)(2,1)S(1)}, bf16[1024,256]{1,0:T(8,128)(2,1)}, u32[]{:S(2)}, u32[]{:S(2)}) collective-permute-start(bf16[1024,256]{1,0:T(8,128)(2,1)S(1)} %select_select_fusion), channel_id=1, source_target_pairs={{0,1},{1,0},{2,3},{3,2},{4,5},{5,4},{6,7},{7,6},{8,9},{9,8},{10,11... | collective-permute-start | bytes 1572872 | tf_op jit(solution)/shard_map/ppermute | solution.py:60
  109.5 1.3 copy-start.4
  109.5 1.4 copy-start.5
  109.5 2.3 copy-start.8
  109.5 167.7 %all-gather.2.cloned.1.call-start = ((), (), s32[]{:S(2)}) async-start(), calls=%async_computation.4 | async-start | bytes 1179648 | tf_op jit(solution)/shard_map/all_gather | solution.py:117
  111.0 3.7 %copy-start.3 = (f32[16,32]{1,0:T(8,128)}, f32[16,32]{1,0:T(8,128)S(1)}, u32[]{:S(2)}) copy-start(f32[16,32]{1,0:T(8,128)S(1)} %get-tuple-element.14) | copy-start | bytes 6148
  112.4 93.7 %copy-start.7 = (f32[64]{0:T(128)}, f32[64]{0:T(128)S(1)}, u32[]{:S(2)}) copy-start(f32[64]{0:T(128)S(1)} %iota_convert_fusion) | copy-start | bytes 772
  209.1 4.7 %copy-start.1 = (f32[4,8,8,128]{3,1,2,0:T(8,128)S(1)}, f32[4,8,8,128]{3,1,2,0:T(8,128)}, u32[]{:S(2)}) copy-start(f32[4,8,8,128]{3,1,2,0:T(8,128)} %get-tuple-element.5) | copy-start | bytes 393220
  209.1 4.8 %copy-start.6 = (f32[32]{0:T(128)S(1)}, f32[32]{0:T(128)}, u32[]{:S(2)}) copy-start(f32[32]{0:T(128)} %dynamic_slice.19) | copy-start | bytes 388
  226.8 13.7 %collective-permute-start.5 = (bf16[128,256]{0,1:T(8,128)(2,1)S(1)}, bf16[128,256]{0,1:T(8,128)(2,1)S(1)}, u32[]{:S(2)}, u32[]{:S(2)}) collective-permute-start(bf16[128,256]{0,1:T(8,128)(2,1)S(1)} %bitcast.85), channel_id=1, source_target_pairs={{0,8},{8,0},{1,9},{9,1},{2,10},{10,2},{3,11},{11,3},{4,12},{12,4},... | collective-permute-start | bytes 196616 | tf_op jit(solution)/shard_map/ppermute | solution.py:115
Sparse Core Ops, SparseCore 0:
  109.7 93.8 reduce-scatter.1
  241.6 35.5 all-gather.1

commit v8 on v6

--- a/solution.py
+++ b/solution.py
@@ -21,27 +21,17 @@
     sub = channels // seq_n
     length = tok_rows * seq_n
     taps_count = short_taps.shape[1]
-    copies = jnp.tile(features, (seq_n, 1))
-    my_columns = lax.all_to_all(copies, "seq", 0, 0, tiled=True)
-    across = []
-    for s in range(seq_n):
-        for a in range(seq_n):
-            for b in range(halves):
-                across.append((a * ten_n + s * halves + b, s * ten_n + a * halves + b))
-    first = lax.ppermute(my_columns, ("seq", "zhi", "inner"), across)
-    swap = [(k, k + 1 - 2 * (k % 2)) for k in range(inner_n)]
-    second = lax.ppermute(first, "inner", swap)
-    rows_of_feats = jnp.concatenate([first, second], axis=1)
-    half_of = lane % halves
-    doubled = jnp.concatenate([in_weight, in_weight], axis=0)
-    weight_rows = lax.dynamic_slice_in_dim(doubled, half_of * fcols, rows_here, axis=0)
-    weight_rows = weight_rows.reshape(rows_here, branches, seq_n, sub)
-    partial = jnp.einsum(
-        "td,djgc->gtjc", rows_of_feats, weight_rows, preferred_element_type=jnp.float32
-    )
-    summed = lax.psum_scatter(partial.reshape(seq_n * length, -1), "seq", scatter_dimension=0, tiled=True)
-    summed = summed.reshape(length, branches, sub)
-    projected = lax.reduce_precision(summed, exponent_bits=8, mantissa_bits=7)
+    copies = jnp.tile(features, (ten_n, 1))
+    own_tokens = lax.all_to_all(copies, ("zhi", "inner"), 0, 1, tiled=True)
+    whole_weight = lax.all_gather(in_weight, "seq", axis=0, tiled=True)
+    local = jnp.dot(
+        own_tokens,
+        whole_weight.reshape(seq_n * rows_here, branches * channels),
+        preferred_element_type=jnp.float32,
+    ).astype(jnp.bfloat16)
+    local = local.reshape(tok_rows, branches, seq_n, sub).transpose(2, 0, 1, 3)
+    projected = lax.all_to_all(local, "seq", 0, 1, tiled=True)
+    projected = projected.reshape(length, branches, sub).astype(jnp.float32)
 
     taps = lax.dynamic_slice_in_dim(short_taps, place * sub, sub, axis=2)
     decay = lax.dynamic_slice_in_dim(decay_rates, place * sub, sub, axis=1)

time: 278 us -> 306 us (1.10)
  waiting for transfers between devices: 161 us -> 208 us
  blocking collectives: 48.5 us -> 17.5 us
  starting transfers between devices: 20.9 us -> 35.1 us
  other arithmetic: 8.35 us -> 5.08 us
    reduce_scatter x1 -> x0, waiting for transfers between devices: 122 us -> none  [body(): lax.psum_scatter(partial.reshape(seq_n * length, -1), 'seq', scatter_dime...]
    all_gather x0 -> x1, waiting for transfers between devices: none -> 117 us  [body(): whole_weight = lax.all_gather(in_weight, 'seq', axis=0, tiled=True)]
    all_to_all x0 -> x2, waiting for transfers between devices: none -> 53.1 us  [the longest x1 46.2 us: body(): own_tokens = lax.all_to_all(copies, ('zhi', 'inner'), 0, 1, tiled=True)]
    all_to_all x1 -> x0, blocking collectives: 35.6 us -> none  [body(): my_columns = lax.all_to_all(copies, 'seq', 0, 0, tiled=True)]
    all_to_all x0 -> x2, starting transfers between devices: none -> 26.5 us  [the longest x1 19.2 us: body(): own_tokens = lax.all_to_all(copies, ('zhi', 'inner'), 0, 1, tiled=True)]
    ppermute x2 -> x0, starting transfers between devices: 9.59 us -> none  [the longest x1 8.9 us: body(): second = lax.ppermute(first, 'inner', swap)]
    all_to_all x1, blocking collectives: 12.9 us -> 17.5 us  [body(): gated = lax.all_to_all(gated, 'seq', 0, 1, tiled=True)]
    all_gather x1, waiting for transfers between devices: 35.6 us -> 32.2 us  [body(): whole = lax.all_gather(pair, 'inner', axis=2, tiled=False)]
  transfers between devices with their start and end apart: 5 -> 5, of which waited for: 3 -> 5; matrix products, arithmetic and copies ran while one was open for 4% -> 3% of each run, Pallas kernels for 0% -> 0%
where the time goes in v8:
time: 306 us; the launch traced here: 305 us
  waiting for transfers between devices  208 us (68%)
  starting transfers between devices  35.1 us (11%)
  blocking collectives  17.5 us (6%)
  matrix products  17.2 us (6%)
  between operations  13.6 us (4%)
  local copies, waits for them, and re-layouts  8.62 us (3%)
  other arithmetic  5.08 us (2%)
    all_gather x1, waiting for transfers between devices, body(): whole_weight = lax.all_gather(in_weight, 'seq', axis=0, tiled=True)  117 us
    all_to_all x1, waiting for transfers between devices, body(): own_tokens = lax.all_to_all(copies, ('zhi', 'inner'), 0, 1, tiled=True)  46.2 us
    all_gather x1, waiting for transfers between devices, body(): whole = lax.all_gather(pair, 'inner', axis=2, tiled=False)  32.2 us
    all_to_all x1, starting transfers between devices, body(): own_tokens = lax.all_to_all(copies, ('zhi', 'inner'), 0, 1, tiled=True)  19.2 us
    all_to_all x1, blocking collectives, body(): gated = lax.all_to_all(gated, 'seq', 0, 1, tiled=True)  17.5 us
    ppermute x1, starting transfers between devices, body(): lax.ppermute(gated, 'zhi', [(z, outer_n - 1 - z) for z in range(outer_n)])  8.56 us
    all_to_all x1, starting transfers between devices, body(): projected = lax.all_to_all(local, 'seq', 0, 1, tiled=True)  7.3 us
    all_to_all x1, waiting for transfers between devices, body(): projected = lax.all_to_all(local, 'seq', 0, 1, tiled=True)  6.88 us
  transfers between devices with their start and end apart: 5, of which 5 were waited for; matrix products, arithmetic and copies ran while one was open for 3% of the time, Pallas kernels for 0%

profile of v8, /device:TPU:1, one launch (start us, length us, event | category | flops | bytes accessed | tf_op | source)
XLA Modules:
  0.0 305.0 jit_solution(13081669253468299125)
XLA Ops:
  6.5 0.0 copy-start
  6.5 0.0 all-gather.3.cloned.1.call-start
  6.5 2.5 copy.38
  9.0 0.0 all-gather.3.cloned.1.call-update
  9.1 0.1 copy.37
  9.2 1.2 tile.2
  10.4 19.2 %all-to-all-start = ((bf16[16,128,256]{1,2,0:T(8,128)(2,1)}), bf16[16,128,256]{1,2,0:T(8,128)(2,1)S(1)}, u32[]{:S(2)}, u32[]{:S(2)}) async-start(bf16[16,128,256]{1,2,0:T(8,128)(2,1)} %tile.2), calls=%async_computation | async-start | bytes 2097152 | tf_op jit(solution)/shard_map/all_to_all | solution.py:25
  29.6 1.0 constant_dynamic-slice_fusion.5
  30.7 0.1 dynamic-slice_negate_fusion
  30.8 0.7 copy.45
  31.5 0.1 copy.53
  31.5 0.1 copy.42
  31.6 0.0 copy-done.8
  31.6 0.6 dynamic_slice.15
  32.3 0.6 broadcast_subtract_fusion
  32.9 0.6 iota_compare_fusion.2
  33.5 0.7 convert_multiply_fusion
  34.1 46.2 %all-to-all-done = bf16[16,128,256]{1,2,0:T(8,128)(2,1)S(1)} async-done(((bf16[16,128,256]{1,2,0:T(8,128)(2,1)}), bf16[16,128,256]{1,2,0:T(8,128)(2,1)S(1)}, u32[]{:S(2)}, u32[]{:S(2)}) %all-to-all-start) | async-done | bytes 1048608 | tf_op jit(solution)/shard_map/all_to_all | solution.py:25
  80.4 116.5 %all-gather.3.cloned.1.call-done = bf16[4096,3,256]{0,2,1:T(8,128)(2,1)} async-done(((bf16[512,3,256]{0,2,1:T(8,128)(2,1)}), bf16[4096,3,256]{0,2,1:T(8,128)(2,1)}) %all-gather.3.cloned.1.call-update) | async-done | bytes 6291472 | tf_op jit(solution)/shard_map/all_gather | solution.py:26
  196.9 5.0 %convolution_convert_fusion = bf16[128,768]{1,0:T(8,128)(2,1)S(1)} fusion(bf16[128,4096]{0,1:T(8,128)(2,1)S(1)} %bitcast.67, bf16[4096,768]{0,1:T(8,128)(2,1)} %bitcast.66), kind=kOutput, calls=%fused_computation.3 | convolution fusion | flops 805404672 | bytes 7536640 | tf_op jit(solution)/shard_map/dot_general | solution.py:27
  201.9 0.2 copy.39
  202.1 0.7 copy.40
  202.7 7.3 %all-to-all-start.1 = ((bf16[8,128,3,32]{1,3,2,0:T(8,128)(2,1)}), bf16[8,128,3,32]{1,3,2,0:T(8,128)(2,1)S(1)}, u32[]{:S(2)}, u32[]{:S(2)}) async-start(bf16[8,128,3,32]{1,3,2,0:T(8,128)(2,1)} %copy.40), calls=%async_computation.1 | async-start | bytes 393216 | tf_op jit(solution)/shard_map/all_to_all | solution.py:33
  210.0 0.0 all-gather.5.cloned.1.call-start
  210.1 0.0 copy-done.7
  210.1 0.4 fusion.20
  210.6 3.6 %fusion = f32[64,64,32]{1,2,0:T(8,128)S(1)} fusion(f32[32,64,1]{1,0,2:T(8,128)S(1)} %bitcast.77, s32[64,64]{1,0:T(8,128)S(1)} %iota_subtract_fusion), kind=kOutput, calls=%fused_computation.2 | convolution fusion | flops 100925440 | bytes 548864 | tf_op jit(solution)/shard_map/tsk,kc->tsc/dot_general | solution.py:61
  214.2 6.9 %all-to-all-done.1 = bf16[8,128,3,32]{1,3,2,0:T(8,128)(2,1)S(1)} async-done(((bf16[8,128,3,32]{1,3,2,0:T(8,128)(2,1)}), bf16[8,128,3,32]{1,3,2,0:T(8,128)(2,1)S(1)}, u32[]{:S(2)}, u32[]{:S(2)}) %all-to-all-start.1) | async-done | bytes 196640 | tf_op jit(solution)/shard_map/all_to_all | solution.py:33
  221.1 0.8 fusion.11
  221.9 0.7 copy.63
  222.6 0.1 mul.195
  222.7 2.9 fusion.2
  225.6 1.3 convolution_bitcast_fusion
  226.9 0.2 copy.44
  227.1 1.5 multiply_reduce_fusion
  228.6 0.2 copy.46
  228.7 1.5 fusion.1
  230.2 0.1 reshape.179
  230.4 0.1 fusion.21
  230.5 17.5 %all_to_all.41 = bf16[8,128,32]{1,2,0:T(8,128)(2,1)S(1)} all-to-all(bf16[8,128,32]{1,2,0:T(8,128)(2,1)S(1)} %fusion.21), channel_id=1, replica_groups=mesh['dp'=4,'seq'=8,'zhi'=2,'inner'=8] {'seq'}, dimensions={0} | all-to-all | bytes 131072 | tf_op jit(solution)/shard_map/all_to_all | solution.py:77
  248.1 8.6 %collective-permute-start = (bf16[128,256]{0,1:T(8,128)(2,1)S(1)}, bf16[128,256]{0,1:T(8,128)(2,1)S(1)}, u32[]{:S(2)}, u32[]{:S(2)}) collective-permute-start(bf16[128,256]{0,1:T(8,128)(2,1)S(1)} %bitcast.74), channel_id=1, source_target_pairs={{0,8},{8,0},{1,9},{9,1},{2,10},{10,2},{3,11},{11,3},{4,12},{12,4},... | collective-permute-start | bytes 196616 | tf_op jit(solution)/shard_map/ppermute | solution.py:78
  256.6 5.9 %collective-permute-done = bf16[128,256]{0,1:T(8,128)(2,1)S(1)} collective-permute-done((bf16[128,256]{0,1:T(8,128)(2,1)S(1)}, bf16[128,256]{0,1:T(8,128)(2,1)S(1)}, u32[]{:S(2)}, u32[]{:S(2)}) %collective-permute-start) | collective-permute-done | bytes 65568 | tf_op jit(solution)/shard_map/ppermute | solution.py:78
  262.6 0.1 copy.50
  262.7 0.1 copy.51
  262.8 0.7 maximum_select_fusion
  263.5 0.0 all-gather.5.cloned.1.call-update
  263.5 32.2 %all-gather.5.cloned.1.call-done = bf16[128,2,8,256]{0,3,2,1:T(8,128)(2,1)} async-done(((bf16[128,2,1,256]{0,3,2,1:T(8,128)(2,1)}), bf16[128,2,8,256]{0,3,2,1:T(8,128)(2,1)}) %all-gather.5.cloned.1.call-update) | async-done | bytes 1048592 | tf_op jit(solution)/shard_map/all_gather | solution.py:80
  295.7 2.4 convolution_convert_fusion.1
  (25 shorter events, 0.1 us)
Async XLA Ops:
  6.5 289.2 %copy-start = (bf16[4096,256]{1,0:T(8,128)(2,1)S(1)}, bf16[4096,256]{1,0:T(8,128)(2,1)}, u32[]{:S(2)}) copy-start(bf16[4096,256]{1,0:T(8,128)(2,1)} %param.13) | copy-start | bytes 6291460
  6.5 2.5 copy-start.3
  6.5 190.3 %all-gather.3.cloned.1.call-start = ((), (), s32[]{:S(2)}) async-start(), calls=%async_computation.3 | async-start | bytes 7077888 | tf_op jit(solution)/shard_map/all_gather | solution.py:26
  9.0 21.6 %copy-start.4 = (f32[16,256]{1,0:T(8,128)S(1)}, f32[16,256]{1,0:T(8,128)}, u32[]{:S(2)}) copy-start(f32[16,256]{1,0:T(8,128)} %param.10) | copy-start | bytes 49156
  9.0 21.6 %copy-start.5 = (f32[16,256]{1,0:T(8,128)S(1)}, f32[16,256]{1,0:T(8,128)}, u32[]{:S(2)}) copy-start(f32[16,256]{1,0:T(8,128)} %param.11) | copy-start | bytes 49156
  9.0 22.6 %copy-start.8 = (f32[256]{0:T(256)S(1)}, f32[256]{0:T(256)}, u32[]{:S(2)}) copy-start(f32[256]{0:T(256)} %param.12) | copy-start | bytes 3076
  10.4 70.0 %all-to-all-start = ((bf16[16,128,256]{1,2,0:T(8,128)(2,1)}), bf16[16,128,256]{1,2,0:T(8,128)(2,1)S(1)}, u32[]{:S(2)}, u32[]{:S(2)}) async-start(bf16[16,128,256]{1,2,0:T(8,128)(2,1)} %tile.2), calls=%async_computation | async-start | bytes 2097152 | tf_op jit(solution)/shard_map/all_to_all | solution.py:25
  30.8 2.1 copy-start.2
  32.3 177.8 %copy-start.7 = (f32[64]{0:T(128)}, f32[64]{0:T(128)S(1)}, u32[]{:S(2)}) copy-start(f32[64]{0:T(128)S(1)} %iota_convert_fusion) | copy-start | bytes 772
  202.7 18.3 %all-to-all-start.1 = ((bf16[8,128,3,32]{1,3,2,0:T(8,128)(2,1)}), bf16[8,128,3,32]{1,3,2,0:T(8,128)(2,1)S(1)}, u32[]{:S(2)}, u32[]{:S(2)}) async-start(bf16[8,128,3,32]{1,3,2,0:T(8,128)(2,1)} %copy.40), calls=%async_computation.1 | async-start | bytes 393216 | tf_op jit(solution)/shard_map/all_to_all | solution.py:33
  210.0 85.7 %all-gather.5.cloned.1.call-start = ((), (), s32[]{:S(2)}) async-start(), calls=%async_computation.4 | async-start | bytes 1179648 | tf_op jit(solution)/shard_map/all_gather | solution.py:80
  225.6 4.8 %copy-start.1 = (f32[4,8,8,128]{3,2,1,0:T(8,128)S(1)}, f32[4,8,8,128]{3,2,1,0:T(8,128)}, u32[]{:S(2)}) copy-start(f32[4,8,8,128]{3,2,1,0:T(8,128)} %copy.63) | copy-start | bytes 393220
  225.6 4.8 %copy-start.6 = (f32[32]{0:T(128)S(1)}, f32[32]{0:T(128)}, u32[]{:S(2)}) copy-start(f32[32]{0:T(128)} %dynamic_slice.15) | copy-start | bytes 388
  248.1 14.5 %collective-permute-start = (bf16[128,256]{0,1:T(8,128)(2,1)S(1)}, bf16[128,256]{0,1:T(8,128)(2,1)S(1)}, u32[]{:S(2)}, u32[]{:S(2)}) collective-permute-start(bf16[128,256]{0,1:T(8,128)(2,1)S(1)} %bitcast.74), channel_id=1, source_target_pairs={{0,8},{8,0},{1,9},{9,1},{2,10},{10,2},{3,11},{11,3},{4,12},{12,4},... | collective-permute-start | bytes 196616 | tf_op jit(solution)/shard_map/ppermute | solution.py:78
Sparse Core Ops, SparseCore 0:
  9.4 187.3 all-gather.2
  263.6 32.0 all-gather.4

commit v9 on v6

--- a/solution.py
+++ b/solution.py
@@ -35,12 +35,14 @@
     half_of = lane % halves
     doubled = jnp.concatenate([in_weight, in_weight], axis=0)
     weight_rows = lax.dynamic_slice_in_dim(doubled, half_of * fcols, rows_here, axis=0)
-    weight_rows = weight_rows.reshape(rows_here, branches, seq_n, sub)
+    weight_rows = weight_rows.reshape(rows_here, branches, seq_n, sub).transpose(0, 1, 3, 2)
     partial = jnp.einsum(
-        "td,djgc->gtjc", rows_of_feats, weight_rows, preferred_element_type=jnp.float32
+        "djcg,td->jcgt", weight_rows, rows_of_feats, preferred_element_type=jnp.float32
     )
-    summed = lax.psum_scatter(partial.reshape(seq_n * length, -1), "seq", scatter_dimension=0, tiled=True)
-    summed = summed.reshape(length, branches, sub)
+    summed = lax.psum_scatter(
+        partial.reshape(branches * sub, seq_n * length), "seq", scatter_dimension=1, tiled=True
+    )
+    summed = summed.T.reshape(length, branches, sub)
     projected = lax.reduce_precision(summed, exponent_bits=8, mantissa_bits=7)
 
     taps = lax.dynamic_slice_in_dim(short_taps, place * sub, sub, axis=2)

time: 278 us -> 275 us (0.989)
  no operation moved by 1% of the time
where the time goes in v9:
time: 275 us
  waiting for transfers between devices  161 us (59%)
  blocking collectives  48.5 us (18%)
  starting transfers between devices  20.8 us (8%)
  matrix products  14.3 us (5%)
  between operations  13.7 us (5%)
  local copies, waits for them, and re-layouts  9.55 us (3%)
  other arithmetic  7 us (3%)
    reduce_scatter x1, waiting for transfers between devices, body(): lax.psum_scatter(partial.reshape(branches * sub, seq_n * length), 'seq',...  123 us
    all_gather x1, waiting for transfers between devices, body(): whole = lax.all_gather(pair, 'inner', axis=2, tiled=False)  35.6 us
    all_to_all x1, blocking collectives, body(): my_columns = lax.all_to_all(copies, 'seq', 0, 0, tiled=True)  35.6 us
    all_to_all x1, blocking collectives, body(): gated = lax.all_to_all(gated, 'seq', 0, 1, tiled=True)  12.9 us
    ppermute x1, starting transfers between devices, body(): lax.ppermute(gated, 'zhi', [(z, outer_n - 1 - z) for z in range(outer_n)])  11.1 us
    ppermute x1, starting transfers between devices, body(): second = lax.ppermute(first, 'inner', swap)  8.9 us
  transfers between devices with their start and end apart: 5, of which 3 were waited for; matrix products, arithmetic and copies ran while one was open for 4% of the time, Pallas kernels for 0%

profile of v9, /device:TPU:1, one launch (start us, length us, event | category | flops | bytes accessed | tf_op | source)
XLA Modules:
  0.0 274.7 jit_solution(14867437080278610218)
XLA Ops:
  6.5 0.0 copy-start
  6.5 0.0 reduce-scatter.2.cloned.1.call-start
  6.5 1.0 tile.2
  7.6 35.6 %all_to_all.25 = bf16[8,128,256]{2,1,0:T(8,128)(2,1)S(1)} all-to-all(bf16[8,128,256]{2,1,0:T(8,128)(2,1)S(1)} %tile.2), channel_id=1, replica_groups=mesh['dp'=4,'seq'=8,'zhi'=2,'inner'=8] {'seq'}, dimensions={0} | all-to-all | bytes 1048576 | tf_op jit(solution)/shard_map/all_to_all | solution.py:25
  43.1 0.7 collective-permute-start
  43.8 0.0 collective-permute-done
  43.8 8.9 %collective-permute-start.1 = (bf16[1024,256]{1,0:T(8,128)(2,1)S(1)}, bf16[1024,256]{1,0:T(8,128)(2,1)}, u32[]{:S(2)}, u32[]{:S(2)}) collective-permute-start(bf16[1024,256]{1,0:T(8,128)(2,1)S(1)} %collective-permute-done), channel_id=1, source_target_pairs={{0,1},{1,0},{2,3},{3,2},{4,5},{5,4},{6,7},{7,6},{8,9},{9,8},{10,11... | collective-permute-start | bytes 1572872 | tf_op jit(solution)/shard_map/ppermute | solution.py:33
  52.8 1.4 copy.42
  54.2 0.3 fusion.8
  54.5 0.0 collective-permute-done.1
  54.5 2.1 fusion.2
  56.7 3.8 %copy.64 = f32[12,8,8,1024]{3,1,2,0:T(8,128)} copy(f32[12,8,8,1024]{3,2,1,0:T(8,128)S(1)} %bitcast.77) | data formatting | bytes 6291456
  60.5 0.0 reduce-scatter.2.cloned.1.call-update
  60.5 0.0 all-gather.2.cloned.1.call-start
  60.6 1.1 constant_dynamic-slice_fusion.5
  61.7 0.1 dynamic-slice_negate_fusion
  61.8 0.1 copy.45
  61.8 0.7 copy.48
  62.5 0.1 copy.55
  62.6 0.6 dynamic_slice.19
  63.2 0.6 broadcast_subtract_fusion
  63.8 0.6 iota_compare_fusion.2
  64.4 0.7 convert_multiply_fusion
  65.0 0.4 fusion.26
  65.5 3.6 %fusion = f32[64,64,32]{1,2,0:T(8,128)S(1)} fusion(f32[32,64,1]{1,0,2:T(8,128)S(1)} %bitcast.87, s32[64,64]{1,0:T(8,128)S(1)} %iota_subtract_fusion), kind=kOutput, calls=%fused_computation.2 | convolution fusion | flops 100925440 | bytes 548864 | tf_op jit(solution)/shard_map/tsk,kc->tsc/dot_general | solution.py:73
  69.1 122.6 %reduce-scatter.2.cloned.1.call-done = f32[96,1024]{1,0:T(8,128)} async-done(((f32[96,8192]{1,0:T(8,128)}), f32[96,1024]{1,0:T(8,128)}) %reduce-scatter.2.cloned.1.call-update) | async-done | bytes 393232 | tf_op jit(solution)/shard_map/reduce_scatter | solution.py:42
  191.7 1.0 reduce_precision.9
  192.8 0.8 fusion.17
  193.6 0.7 slice_bitcast_fusion
  194.3 0.1 mul.203
  194.4 2.9 %fusion.5 = f32[32,16,64]{2,1,0:T(8,128)} fusion(f32[16,64,32]{1,0,2:T(8,128)S(1)} %mul.203, f32[64,64,32]{1,2,0:T(8,128)S(1)} %fusion), kind=kOutput, calls=%fused_computation.13 | convolution fusion | flops 25165824 | bytes 786432 | tf_op jit(solution)/shard_map/tsc,bsc->btc/dot_general | solution.py:74
  197.3 1.3 convolution_bitcast_fusion
  198.6 0.2 copy.47
  198.8 1.5 multiply_reduce_fusion
  200.2 0.2 copy.49
  200.4 1.5 fusion.1
  201.9 0.1 reshape.173
  202.1 0.1 fusion.29
  202.2 12.9 %all_to_all.26 = bf16[8,128,32]{1,2,0:T(8,128)(2,1)S(1)} all-to-all(bf16[8,128,32]{1,2,0:T(8,128)(2,1)S(1)} %copy.50), channel_id=1, replica_groups=mesh['dp'=4,'seq'=8,'zhi'=2,'inner'=8] {'seq'}, dimensions={0} | all-to-all | bytes 131072 | tf_op jit(solution)/shard_map/all_to_all | solution.py:89
  215.1 11.1 %collective-permute-start.2 = (bf16[128,256]{0,1:T(8,128)(2,1)S(1)}, bf16[128,256]{0,1:T(8,128)(2,1)S(1)}, u32[]{:S(2)}, u32[]{:S(2)}) collective-permute-start(bf16[128,256]{0,1:T(8,128)(2,1)S(1)} %bitcast.84), channel_id=1, source_target_pairs={{0,8},{8,0},{1,9},{9,1},{2,10},{10,2},{3,11},{11,3},{4,12},{12,4},... | collective-permute-start | bytes 196616 | tf_op jit(solution)/shard_map/ppermute | solution.py:90
  226.3 2.6 collective-permute-done.2
  228.8 0.1 copy.51
  228.9 0.1 copy.52
  229.1 0.7 maximum_select_fusion
  229.7 0.0 all-gather.2.cloned.1.call-update
  229.8 35.6 %all-gather.2.cloned.1.call-done = bf16[128,2,8,256]{0,3,2,1:T(8,128)(2,1)} async-done(((bf16[128,2,1,256]{0,3,2,1:T(8,128)(2,1)}), bf16[128,2,8,256]{0,3,2,1:T(8,128)(2,1)}) %all-gather.2.cloned.1.call-update) | async-done | bytes 1048592 | tf_op jit(solution)/shard_map/all_gather | solution.py:92
  265.4 0.0 copy-done
  265.4 2.4 convolution_convert_fusion
  (24 shorter events, 0.1 us)
Async XLA Ops:
  6.5 258.9 %copy-start = (bf16[4096,256]{1,0:T(8,128)(2,1)S(1)}, bf16[4096,256]{1,0:T(8,128)(2,1)}, u32[]{:S(2)}) copy-start(bf16[4096,256]{1,0:T(8,128)(2,1)} %param.13) | copy-start | bytes 6291460
  6.5 185.2 %reduce-scatter.2.cloned.1.call-start = ((), (), s32[]{:S(2)}) async-start(), calls=%async_computation.3 | async-start | bytes 3538944 | tf_op jit(solution)/shard_map/reduce_scatter | solution.py:42
  43.1 0.7 collective-permute-start
  43.8 10.7 %collective-permute-start.1 = (bf16[1024,256]{1,0:T(8,128)(2,1)S(1)}, bf16[1024,256]{1,0:T(8,128)(2,1)}, u32[]{:S(2)}, u32[]{:S(2)}) collective-permute-start(bf16[1024,256]{1,0:T(8,128)(2,1)S(1)} %collective-permute-done), channel_id=1, source_target_pairs={{0,1},{1,0},{2,3},{3,2},{4,5},{5,4},{6,7},{7,6},{8,9},{9,8},{10,11... | collective-permute-start | bytes 1572872 | tf_op jit(solution)/shard_map/ppermute | solution.py:33
  60.5 1.2 copy-start.3
  60.5 1.2 copy-start.4
  60.5 2.1 copy-start.7
  60.5 204.9 %all-gather.2.cloned.1.call-start = ((), (), s32[]{:S(2)}) async-start(), calls=%async_computation.4 | async-start | bytes 1179648 | tf_op jit(solution)/shard_map/all_gather | solution.py:92
  61.8 3.7 %copy-start.2 = (f32[16,32]{1,0:T(8,128)}, f32[16,32]{1,0:T(8,128)S(1)}, u32[]{:S(2)}) copy-start(f32[16,32]{1,0:T(8,128)S(1)} %get-tuple-element.14) | copy-start | bytes 6148
  63.2 2.3 copy-start.6
  197.3 4.7 %copy-start.1 = (f32[4,8,8,128]{3,1,2,0:T(8,128)S(1)}, f32[4,8,8,128]{3,1,2,0:T(8,128)}, u32[]{:S(2)}) copy-start(f32[4,8,8,128]{3,1,2,0:T(8,128)} %get-tuple-element.5) | copy-start | bytes 393220
  197.3 4.8 %copy-start.5 = (f32[32]{0:T(128)S(1)}, f32[32]{0:T(128)}, u32[]{:S(2)}) copy-start(f32[32]{0:T(128)} %dynamic_slice.19) | copy-start | bytes 388
  215.1 13.7 %collective-permute-start.2 = (bf16[128,256]{0,1:T(8,128)(2,1)S(1)}, bf16[128,256]{0,1:T(8,128)(2,1)S(1)}, u32[]{:S(2)}, u32[]{:S(2)}) collective-permute-start(bf16[128,256]{0,1:T(8,128)(2,1)S(1)} %bitcast.84), channel_id=1, source_target_pairs={{0,8},{8,0},{1,9},{9,1},{2,10},{10,2},{3,11},{11,3},{4,12},{12,4},... | collective-permute-start | bytes 196616 | tf_op jit(solution)/shard_map/ppermute | solution.py:90
Sparse Core Ops, SparseCore 0:
  60.6 131.0 reduce-scatter.1
  229.9 35.4 all-gather.1

commit v10 on v9

--- a/solution.py
+++ b/solution.py
@@ -35,14 +35,14 @@
     half_of = lane % halves
     doubled = jnp.concatenate([in_weight, in_weight], axis=0)
     weight_rows = lax.dynamic_slice_in_dim(doubled, half_of * fcols, rows_here, axis=0)
-    weight_rows = weight_rows.reshape(rows_here, branches, seq_n, sub).transpose(0, 1, 3, 2)
+    weight_rows = weight_rows.reshape(rows_here, branches, seq_n, sub).transpose(0, 2, 1, 3)
     partial = jnp.einsum(
-        "djcg,td->jcgt", weight_rows, rows_of_feats, preferred_element_type=jnp.float32
+        "dgjc,td->gjct", weight_rows, rows_of_feats, preferred_element_type=jnp.float32
     )
     summed = lax.psum_scatter(
-        partial.reshape(branches * sub, seq_n * length), "seq", scatter_dimension=1, tiled=True
+        partial.reshape(seq_n, branches * sub, length), "seq", scatter_dimension=0, tiled=True
     )
-    summed = summed.T.reshape(length, branches, sub)
+    summed = summed.reshape(branches * sub, length).T.reshape(length, branches, sub)
     projected = lax.reduce_precision(summed, exponent_bits=8, mantissa_bits=7)
 
     taps = lax.dynamic_slice_in_dim(short_taps, place * sub, sub, axis=2)

time: 275 us -> 273 us (level)
  local copies, waits for them, and re-layouts: 9.55 us -> 5.73 us
    unnamed x24 -> x23, local copies, waits for them, and re-layouts: 5.34 us -> 1.51 us
where the time goes in v10:
time: 273 us; the launch traced here: 272 us
  waiting for transfers between devices  161 us (59%)
  blocking collectives  48.5 us (18%)
  starting transfers between devices  20.7 us (8%)
  matrix products  15.9 us (6%)
  between operations  13.7 us (5%)
  other arithmetic  7 us (3%)
  local copies, waits for them, and re-layouts  5.73 us (2%)
    reduce_scatter x1, waiting for transfers between devices, body(): lax.psum_scatter(partial.reshape(seq_n, branches * sub, length), 'seq', s...  123 us
    all_gather x1, waiting for transfers between devices, body(): whole = lax.all_gather(pair, 'inner', axis=2, tiled=False)  35.6 us
    all_to_all x1, blocking collectives, body(): my_columns = lax.all_to_all(copies, 'seq', 0, 0, tiled=True)  35.6 us
    all_to_all x1, blocking collectives, body(): gated = lax.all_to_all(gated, 'seq', 0, 1, tiled=True)  13 us
    ppermute x1, starting transfers between devices, body(): lax.ppermute(gated, 'zhi', [(z, outer_n - 1 - z) for z in range(outer_n)])  11.1 us
    ppermute x1, starting transfers between devices, body(): second = lax.ppermute(first, 'inner', swap)  8.9 us
  transfers between devices with their start and end apart: 5, of which 3 were waited for; matrix products, arithmetic and copies ran while one was open for 4% of the time, Pallas kernels for 0%

profile of v10, /device:TPU:1, one launch (start us, length us, event | category | flops | bytes accessed | tf_op | source)
XLA Modules:
  0.0 272.4 jit_solution(3323801127070424967)
XLA Ops:
  6.5 0.0 copy-start
  6.5 0.0 reduce-scatter.2.cloned.1.call-start
  6.5 1.0 tile.2
  7.6 35.6 %all_to_all.25 = bf16[8,128,256]{2,1,0:T(8,128)(2,1)S(1)} all-to-all(bf16[8,128,256]{2,1,0:T(8,128)(2,1)S(1)} %tile.2), channel_id=1, replica_groups=mesh['dp'=4,'seq'=8,'zhi'=2,'inner'=8] {'seq'}, dimensions={0} | all-to-all | bytes 1048576 | tf_op jit(solution)/shard_map/all_to_all | solution.py:25
  43.1 0.7 collective-permute-start
  43.8 0.0 collective-permute-done
  43.8 8.9 %collective-permute-start.1 = (bf16[1024,256]{1,0:T(8,128)(2,1)S(1)}, bf16[1024,256]{1,0:T(8,128)(2,1)}, u32[]{:S(2)}, u32[]{:S(2)}) collective-permute-start(bf16[1024,256]{1,0:T(8,128)(2,1)S(1)} %collective-permute-done), channel_id=1, source_target_pairs={{0,1},{1,0},{2,3},{3,2},{4,5},{5,4},{6,7},{7,6},{8,9},{9,8},{10,11... | collective-permute-start | bytes 1572872 | tf_op jit(solution)/shard_map/ppermute | solution.py:33
  52.8 1.4 copy.42
  54.2 0.3 fusion.8
  54.5 0.0 collective-permute-done.1
  54.5 3.7 %fusion.2 = f32[8,3,32,1024]{3,2,1,0:T(8,128)} fusion(bf16[1024,256]{1,0:T(8,128)(2,1)} %collective-permute-done.1, bf16[1024,256]{1,0:T(8,128)(2,1)S(1)} %collective-permute-done, bf16[512,3,8,32]{0,3,2,1:T(8,128)(2,1)S(1)} %bitcast.77), kind=kOutput, calls=%fused_computation.10 | convolution fusion | flops 807403520 | bytes 4980736 | tf_op jit(solution)/shard_map/dgjc,td->gjct/dot_general | solution.py:39
  58.2 0.0 reduce-scatter.2.cloned.1.call-update
  58.2 0.0 all-gather.2.cloned.1.call-start
  58.3 1.1 constant_dynamic-slice_fusion.5
  59.4 0.0 copy-done.3
  59.4 0.0 copy-done.4
  59.4 0.1 dynamic-slice_negate_fusion
  59.5 0.1 copy.45
  59.6 0.7 copy.48
  60.2 0.1 copy.55
  60.3 0.6 dynamic_slice.19
  60.9 0.6 broadcast_subtract_fusion
  61.5 0.6 iota_compare_fusion.2
  62.1 0.7 convert_multiply_fusion
  62.8 0.4 fusion.26
  63.2 3.6 %fusion = f32[64,64,32]{1,2,0:T(8,128)S(1)} fusion(f32[32,64,1]{1,0,2:T(8,128)S(1)} %bitcast.86, s32[64,64]{1,0:T(8,128)S(1)} %iota_subtract_fusion), kind=kOutput, calls=%fused_computation.2 | convolution fusion | flops 100925440 | bytes 548864 | tf_op jit(solution)/shard_map/tsk,kc->tsc/dot_general | solution.py:73
  66.8 122.6 %reduce-scatter.2.cloned.1.call-done = f32[1,96,1024]{2,1,0:T(8,128)} async-done(((f32[8,96,1024]{2,1,0:T(8,128)}), f32[1,96,1024]{2,1,0:T(8,128)}) %reduce-scatter.2.cloned.1.call-update) | async-done | bytes 393232 | tf_op jit(solution)/shard_map/reduce_scatter | solution.py:42
  189.5 1.0 reduce_precision.12
  190.5 0.8 fusion.17
  191.3 0.7 slice_bitcast_fusion
  192.0 0.1 mul.203
  192.1 2.9 %fusion.5 = f32[32,16,64]{2,1,0:T(8,128)} fusion(f32[16,64,32]{1,0,2:T(8,128)S(1)} %mul.203, f32[64,64,32]{1,2,0:T(8,128)S(1)} %fusion), kind=kOutput, calls=%fused_computation.13 | convolution fusion | flops 25165824 | bytes 786432 | tf_op jit(solution)/shard_map/tsc,bsc->btc/dot_general | solution.py:74
  195.0 1.3 convolution_bitcast_fusion
  196.3 0.2 copy.47
  196.5 1.5 multiply_reduce_fusion
  198.0 0.2 copy.49
  198.1 1.5 fusion.1
  199.6 0.1 reshape.175
  199.8 0.1 fusion.29
  199.9 13.0 %all_to_all.26 = bf16[8,128,32]{1,2,0:T(8,128)(2,1)S(1)} all-to-all(bf16[8,128,32]{1,2,0:T(8,128)(2,1)S(1)} %copy.50), channel_id=1, replica_groups=mesh['dp'=4,'seq'=8,'zhi'=2,'inner'=8] {'seq'}, dimensions={0} | all-to-all | bytes 131072 | tf_op jit(solution)/shard_map/all_to_all | solution.py:89
  212.9 11.1 %collective-permute-start.2 = (bf16[128,256]{0,1:T(8,128)(2,1)S(1)}, bf16[128,256]{0,1:T(8,128)(2,1)S(1)}, u32[]{:S(2)}, u32[]{:S(2)}) collective-permute-start(bf16[128,256]{0,1:T(8,128)(2,1)S(1)} %bitcast.83), channel_id=1, source_target_pairs={{0,8},{8,0},{1,9},{9,1},{2,10},{10,2},{3,11},{11,3},{4,12},{12,4},... | collective-permute-start | bytes 196616 | tf_op jit(solution)/shard_map/ppermute | solution.py:90
  224.0 2.6 collective-permute-done.2
  226.6 0.1 copy.51
  226.7 0.1 copy.52
  226.8 0.7 maximum_select_fusion
  227.5 0.0 all-gather.2.cloned.1.call-update
  227.5 35.6 %all-gather.2.cloned.1.call-done = bf16[128,2,8,256]{0,3,2,1:T(8,128)(2,1)} async-done(((bf16[128,2,1,256]{0,3,2,1:T(8,128)(2,1)}), bf16[128,2,8,256]{0,3,2,1:T(8,128)(2,1)}) %all-gather.2.cloned.1.call-update) | async-done | bytes 1048592 | tf_op jit(solution)/shard_map/all_gather | solution.py:92
  263.1 2.4 convolution_convert_fusion
  (23 shorter events, 0.1 us)
Async XLA Ops:
  6.5 256.6 %copy-start = (bf16[4096,256]{1,0:T(8,128)(2,1)S(1)}, bf16[4096,256]{1,0:T(8,128)(2,1)}, u32[]{:S(2)}) copy-start(bf16[4096,256]{1,0:T(8,128)(2,1)} %param.13) | copy-start | bytes 6291460
  6.5 182.9 %reduce-scatter.2.cloned.1.call-start = ((), (), s32[]{:S(2)}) async-start(), calls=%async_computation.3 | async-start | bytes 3538944 | tf_op jit(solution)/shard_map/reduce_scatter | solution.py:42
  43.1 0.7 collective-permute-start
  43.8 10.7 %collective-permute-start.1 = (bf16[1024,256]{1,0:T(8,128)(2,1)S(1)}, bf16[1024,256]{1,0:T(8,128)(2,1)}, u32[]{:S(2)}, u32[]{:S(2)}) collective-permute-start(bf16[1024,256]{1,0:T(8,128)(2,1)S(1)} %collective-permute-done), channel_id=1, source_target_pairs={{0,1},{1,0},{2,3},{3,2},{4,5},{5,4},{6,7},{7,6},{8,9},{9,8},{10,11... | collective-permute-start | bytes 1572872 | tf_op jit(solution)/shard_map/ppermute | solution.py:33
  58.2 1.2 copy-start.3
  58.2 1.2 copy-start.4
  58.2 2.1 copy-start.7
  58.2 204.9 %all-gather.2.cloned.1.call-start = ((), (), s32[]{:S(2)}) async-start(), calls=%async_computation.4 | async-start | bytes 1179648 | tf_op jit(solution)/shard_map/all_gather | solution.py:92
  59.5 3.7 %copy-start.2 = (f32[16,32]{1,0:T(8,128)}, f32[16,32]{1,0:T(8,128)S(1)}, u32[]{:S(2)}) copy-start(f32[16,32]{1,0:T(8,128)S(1)} %get-tuple-element.14) | copy-start | bytes 6148
  60.9 2.3 copy-start.6
  195.0 4.7 %copy-start.1 = (f32[4,8,8,128]{3,1,2,0:T(8,128)S(1)}, f32[4,8,8,128]{3,1,2,0:T(8,128)}, u32[]{:S(2)}) copy-start(f32[4,8,8,128]{3,1,2,0:T(8,128)} %get-tuple-element.5) | copy-start | bytes 393220
  195.0 4.8 %copy-start.5 = (f32[32]{0:T(128)S(1)}, f32[32]{0:T(128)}, u32[]{:S(2)}) copy-start(f32[32]{0:T(128)} %dynamic_slice.19) | copy-start | bytes 388
  212.9 13.7 %collective-permute-start.2 = (bf16[128,256]{0,1:T(8,128)(2,1)S(1)}, bf16[128,256]{0,1:T(8,128)(2,1)S(1)}, u32[]{:S(2)}, u32[]{:S(2)}) collective-permute-start(bf16[128,256]{0,1:T(8,128)(2,1)S(1)} %bitcast.83), channel_id=1, source_target_pairs={{0,8},{8,0},{1,9},{9,1},{2,10},{10,2},{3,11},{11,3},{4,12},{12,4},... | collective-permute-start | bytes 196616 | tf_op jit(solution)/shard_map/ppermute | solution.py:90
Sparse Core Ops, SparseCore 0:
  58.4 131.0 reduce-scatter.1
  227.7 35.4 all-gather.1

commit v11 on v10

--- a/solution.py
+++ b/solution.py
@@ -86,9 +86,12 @@
     outer = jnp.einsum("mic,bmc->bic", amplitude[:, None, :] * falloff, starts, precision=precise)
     conv = (inner + outer).reshape(length, sub)
     gated = (short[:, 0, :] * (conv + skip[None, :] * product)).astype(jnp.bfloat16)
-    gated = lax.all_to_all(gated, "seq", 0, 1, tiled=True)
-    opposite = lax.ppermute(gated, "zhi", [(z, outer_n - 1 - z) for z in range(outer_n)])
-    pair = jnp.where(far == 0, jnp.stack([gated, opposite], 1), jnp.stack([opposite, gated], 1))
+    outgoing = jnp.broadcast_to(
+        gated.reshape(seq_n, 1, tok_rows, sub), (seq_n, outer_n, tok_rows, sub)
+    ).reshape(seq_n * outer_n * tok_rows, sub)
+    incoming = lax.all_to_all(outgoing, ("seq", "zhi"), 0, 0, tiled=True)
+    pair = incoming.reshape(seq_n, outer_n, tok_rows, sub).transpose(2, 1, 0, 3)
+    pair = pair.reshape(tok_rows, outer_n, seq_n * sub)
     whole = lax.all_gather(pair, "inner", axis=2, tiled=False)
     mixed = jnp.dot(
         whole.reshape(tok_rows, ten_n * channels),

time: 273 us -> 257 us (0.941)
  waiting for transfers between devices: 161 us -> 149 us
  starting transfers between devices: 20.7 us -> 9.63 us
  blocking collectives: 48.5 us -> 54.5 us
    ppermute x1 -> x0, starting transfers between devices: 11.1 us -> none  [body(): lax.ppermute(gated, 'zhi', [(z, outer_n - 1 - z) for z in range(outer_n)])]
    all_gather x1, waiting for transfers between devices: 35.6 us -> 26.7 us  [body(): whole = lax.all_gather(pair, 'inner', axis=2, tiled=False)]
    all_to_all x1, blocking collectives: 13 us -> 18.9 us  [body(): incoming = lax.all_to_all(outgoing, ('seq', 'zhi'), 0, 0, tiled=True)]
  transfers between devices with their start and end apart: 5 -> 4, of which waited for: 3 -> 2; matrix products, arithmetic and copies ran while one was open for 4% -> 4% of each run, Pallas kernels for 0% -> 0%
where the time goes in v11:
time: 257 us; the launch traced here: 256 us
  waiting for transfers between devices  149 us (58%)
  blocking collectives  54.5 us (21%)
  matrix products  14.7 us (6%)
  between operations  13.7 us (5%)
  starting transfers between devices  9.63 us (4%)
  local copies, waits for them, and re-layouts  7.99 us (3%)
  other arithmetic  6.34 us (2%)
    reduce_scatter x1, waiting for transfers between devices, body(): lax.psum_scatter(partial.reshape(seq_n, branches * sub, length), 'seq', s...  123 us
    all_to_all x1, blocking collectives, body(): my_columns = lax.all_to_all(copies, 'seq', 0, 0, tiled=True)  35.6 us
    all_gather x1, waiting for transfers between devices, body(): whole = lax.all_gather(pair, 'inner', axis=2, tiled=False)  26.7 us
    all_to_all x1, blocking collectives, body(): incoming = lax.all_to_all(outgoing, ('seq', 'zhi'), 0, 0, tiled=True)  18.9 us
    ppermute x1, starting transfers between devices, body(): second = lax.ppermute(first, 'inner', swap)  8.9 us
  transfers between devices with their start and end apart: 4, of which 2 were waited for; matrix products, arithmetic and copies ran while one was open for 4% of the time, Pallas kernels for 0%

profile of v11, /device:TPU:1, one launch (start us, length us, event | category | flops | bytes accessed | tf_op | source)
XLA Modules:
  0.0 256.0 jit_solution(15534398769435689275)
XLA Ops:
  6.5 0.0 copy-start
  6.5 0.0 reduce-scatter.2.cloned.1.call-start
  6.5 1.0 tile.2
  7.6 35.6 %all_to_all.18 = bf16[8,128,256]{2,1,0:T(8,128)(2,1)S(1)} all-to-all(bf16[8,128,256]{2,1,0:T(8,128)(2,1)S(1)} %tile.2), channel_id=1, replica_groups=mesh['dp'=4,'seq'=8,'zhi'=2,'inner'=8] {'seq'}, dimensions={0} | all-to-all | bytes 1048576 | tf_op jit(solution)/shard_map/all_to_all | solution.py:25
  43.1 0.7 collective-permute-start
  43.8 0.0 collective-permute-done
  43.8 8.9 %collective-permute-start.1 = (bf16[1024,256]{1,0:T(8,128)(2,1)S(1)}, bf16[1024,256]{1,0:T(8,128)(2,1)}, u32[]{:S(2)}, u32[]{:S(2)}) collective-permute-start(bf16[1024,256]{1,0:T(8,128)(2,1)S(1)} %collective-permute-done), channel_id=1, source_target_pairs={{0,1},{1,0},{2,3},{3,2},{4,5},{5,4},{6,7},{7,6},{8,9},{9,8},{10,11... | collective-permute-start | bytes 1572872 | tf_op jit(solution)/shard_map/ppermute | solution.py:33
  52.8 1.4 copy.38
  54.2 0.3 fusion.8
  54.5 0.0 collective-permute-done.1
  54.5 3.7 %fusion.2 = f32[8,3,32,1024]{3,2,1,0:T(8,128)} fusion(bf16[1024,256]{1,0:T(8,128)(2,1)} %collective-permute-done.1, bf16[1024,256]{1,0:T(8,128)(2,1)S(1)} %collective-permute-done, bf16[512,3,8,32]{0,3,2,1:T(8,128)(2,1)S(1)} %bitcast.77), kind=kOutput, calls=%fused_computation.10 | convolution fusion | flops 807403520 | bytes 4980736 | tf_op jit(solution)/shard_map/dgjc,td->gjct/dot_general | solution.py:39
  58.2 0.0 reduce-scatter.2.cloned.1.call-update
  58.3 0.0 all-gather.2.cloned.1.call-start
  58.3 1.1 constant_dynamic-slice_fusion.5
  59.4 0.0 copy-done.3
  59.4 0.0 copy-done.4
  59.4 0.1 dynamic-slice_negate_fusion
  59.5 0.1 copy.41
  59.6 0.7 copy.44
  60.3 0.1 copy.51
  60.3 0.0 copy-done.7
  60.3 0.6 dynamic_slice.19
  60.9 0.6 broadcast_subtract_fusion
  61.5 0.6 iota_compare_fusion.2
  62.2 0.7 convert_multiply_fusion
  62.8 0.4 fusion.26
  63.3 3.6 %fusion = f32[64,64,32]{1,2,0:T(8,128)S(1)} fusion(f32[32,64,1]{1,0,2:T(8,128)S(1)} %bitcast.85, s32[64,64]{1,0:T(8,128)S(1)} %iota_subtract_fusion), kind=kOutput, calls=%fused_computation.2 | convolution fusion | flops 100925440 | bytes 548864 | tf_op jit(solution)/shard_map/tsk,kc->tsc/dot_general | solution.py:73
  66.9 122.6 %reduce-scatter.2.cloned.1.call-done = f32[1,96,1024]{2,1,0:T(8,128)} async-done(((f32[8,96,1024]{2,1,0:T(8,128)}), f32[1,96,1024]{2,1,0:T(8,128)}) %reduce-scatter.2.cloned.1.call-update) | async-done | bytes 393232 | tf_op jit(solution)/shard_map/reduce_scatter | solution.py:42
  189.5 1.0 reduce_precision.12
  190.5 0.0 copy-done.6
  190.5 0.8 fusion.17
  191.3 0.7 slice_bitcast_fusion
  192.0 0.1 mul.212
  192.1 2.9 %fusion.5 = f32[32,16,64]{2,1,0:T(8,128)} fusion(f32[16,64,32]{1,0,2:T(8,128)S(1)} %mul.212, f32[64,64,32]{1,2,0:T(8,128)S(1)} %fusion), kind=kOutput, calls=%fused_computation.13 | convolution fusion | flops 25165824 | bytes 786432 | tf_op jit(solution)/shard_map/tsc,bsc->btc/dot_general | solution.py:74
  195.0 1.3 convolution_bitcast_fusion
  196.3 0.2 copy.43
  196.5 1.5 multiply_reduce_fusion
  198.0 0.2 copy.45
  198.1 1.5 fusion.1
  199.6 0.1 reshape.138
  199.8 0.0 copy-done.5
  199.8 0.1 fusion.29
  200.0 18.9 %all_to_all.19 = bf16[16,128,32]{1,2,0:T(8,128)(2,1)S(1)} all-to-all(bf16[16,128,32]{1,2,0:T(8,128)(2,1)S(1)} %bitcast.81), channel_id=1, replica_groups=mesh['dp'=4,'seq'=8,'zhi'=2,'inner'=8] {'seq','zhi'}, dimensions={0} | all-to-all | bytes 262144 | tf_op jit(solution)/shard_map/all_to_all | solution.py:92
  218.9 0.8 copy.48
  219.6 0.0 all-gather.2.cloned.1.call-update
  219.7 26.7 %all-gather.2.cloned.1.call-done = bf16[128,2,8,256]{3,0,1,2:T(8,128)(2,1)} async-done(((bf16[128,2,1,256]{3,0,1,2:T(8,128)(2,1)}), bf16[128,2,8,256]{3,0,1,2:T(8,128)(2,1)}) %all-gather.2.cloned.1.call-update) | async-done | bytes 1048592 | tf_op jit(solution)/shard_map/all_gather | solution.py:95
  246.4 1.6 copy.49
  248.0 1.2 convolution_convert_fusion
  (22 shorter events, 0.1 us)
Async XLA Ops:
  6.5 241.4 %copy-start = (bf16[4096,256]{1,0:T(8,128)(2,1)S(1)}, bf16[4096,256]{1,0:T(8,128)(2,1)}, u32[]{:S(2)}) copy-start(bf16[4096,256]{1,0:T(8,128)(2,1)} %param.13) | copy-start | bytes 6291460
  6.5 182.9 %reduce-scatter.2.cloned.1.call-start = ((), (), s32[]{:S(2)}) async-start(), calls=%async_computation.3 | async-start | bytes 3538944 | tf_op jit(solution)/shard_map/reduce_scatter | solution.py:42
  43.1 0.7 collective-permute-start
  43.8 10.7 %collective-permute-start.1 = (bf16[1024,256]{1,0:T(8,128)(2,1)S(1)}, bf16[1024,256]{1,0:T(8,128)(2,1)}, u32[]{:S(2)}, u32[]{:S(2)}) collective-permute-start(bf16[1024,256]{1,0:T(8,128)(2,1)S(1)} %collective-permute-done), channel_id=1, source_target_pairs={{0,1},{1,0},{2,3},{3,2},{4,5},{5,4},{6,7},{7,6},{8,9},{9,8},{10,11... | collective-permute-start | bytes 1572872 | tf_op jit(solution)/shard_map/ppermute | solution.py:33
  58.2 1.2 copy-start.3
  58.2 1.2 copy-start.4
  58.2 2.1 copy-start.7
  58.3 188.1 %all-gather.2.cloned.1.call-start = ((), (), s32[]{:S(2)}) async-start(), calls=%async_computation.4 | async-start | bytes 1179648 | tf_op jit(solution)/shard_map/all_gather | solution.py:95
  59.5 3.8 %copy-start.2 = (f32[16,32]{1,0:T(8,128)}, f32[16,32]{1,0:T(8,128)S(1)}, u32[]{:S(2)}) copy-start(f32[16,32]{1,0:T(8,128)S(1)} %get-tuple-element.14) | copy-start | bytes 6148
  60.9 129.6 %copy-start.6 = (f32[64]{0:T(128)}, f32[64]{0:T(128)S(1)}, u32[]{:S(2)}) copy-start(f32[64]{0:T(128)S(1)} %iota_convert_fusion) | copy-start | bytes 772
  195.0 4.7 %copy-start.1 = (f32[4,8,8,128]{3,1,2,0:T(8,128)S(1)}, f32[4,8,8,128]{3,1,2,0:T(8,128)}, u32[]{:S(2)}) copy-start(f32[4,8,8,128]{3,1,2,0:T(8,128)} %get-tuple-element.5) | copy-start | bytes 393220
  195.0 4.8 %copy-start.5 = (f32[32]{0:T(128)S(1)}, f32[32]{0:T(128)}, u32[]{:S(2)}) copy-start(f32[32]{0:T(128)} %dynamic_slice.19) | copy-start | bytes 388
Sparse Core Ops, SparseCore 0:
  58.4 131.0 reduce-scatter.1
  219.8 26.5 all-gather.1

commit v12 on v11

--- a/solution.py
+++ b/solution.py
@@ -21,21 +21,20 @@
     sub = channels // seq_n
     length = tok_rows * seq_n
     taps_count = short_taps.shape[1]
-    copies = jnp.tile(features, (seq_n, 1))
-    my_columns = lax.all_to_all(copies, "seq", 0, 0, tiled=True)
-    across = []
+    flip = []
     for s in range(seq_n):
-        for a in range(seq_n):
-            for b in range(halves):
-                across.append((a * ten_n + s * halves + b, s * ten_n + a * halves + b))
-    first = lax.ppermute(my_columns, ("seq", "zhi", "inner"), across)
-    swap = [(k, k + 1 - 2 * (k % 2)) for k in range(inner_n)]
-    second = lax.ppermute(first, "inner", swap)
-    rows_of_feats = jnp.concatenate([first, second], axis=1)
-    half_of = lane % halves
-    doubled = jnp.concatenate([in_weight, in_weight], axis=0)
-    weight_rows = lax.dynamic_slice_in_dim(doubled, half_of * fcols, rows_here, axis=0)
-    weight_rows = weight_rows.reshape(rows_here, branches, seq_n, sub).transpose(0, 2, 1, 3)
+        for c in range(seq_n):
+            for e in range(halves):
+                flip.append((s * ten_n + c * halves + e, c * ten_n + s * halves + e))
+    flipped = lax.ppermute(features, ("seq", "zhi", "inner"), flip)
+    copies = jnp.tile(flipped, (ten_n, 1))
+    gathered = lax.all_to_all(copies, ("zhi", "inner"), 0, 1, tiled=True)
+    rows_of_feats = (
+        gathered.reshape(tok_rows, seq_n, halves * fcols)
+        .transpose(1, 0, 2)
+        .reshape(length, rows_here)
+    )
+    weight_rows = in_weight.reshape(rows_here, branches, seq_n, sub).transpose(0, 2, 1, 3)
     partial = jnp.einsum(
         "dgjc,td->gjct", weight_rows, rows_of_feats, preferred_element_type=jnp.float32
     )

time: 257 us -> 246 us (0.957)
  blocking collectives: 54.5 us -> 18.9 us
  starting transfers between devices: 9.63 us -> 32.7 us
  local copies, waits for them, and re-layouts: 7.99 us -> 13.8 us
  waiting for transfers between devices: 149 us -> 146 us
    reduce_scatter x1, waiting for transfers between devices: 123 us -> 84.3 us  [body(): lax.psum_scatter(partial.reshape(seq_n, branches * sub, length), 'seq', s...]
    all_to_all x1 -> x0, blocking collectives: 35.6 us -> none  [body(): my_columns = lax.all_to_all(copies, 'seq', 0, 0, tiled=True)]
    all_to_all x0 -> x1, waiting for transfers between devices: none -> 34.7 us  [body(): gathered = lax.all_to_all(copies, ('zhi', 'inner'), 0, 1, tiled=True)]
    all_to_all x0 -> x1, starting transfers between devices: none -> 31 us  [body(): gathered = lax.all_to_all(copies, ('zhi', 'inner'), 0, 1, tiled=True)]
    ppermute x2 -> x1, starting transfers between devices: 9.59 us -> 1.62 us  [body(): flipped = lax.ppermute(features, ('seq', 'zhi', 'inner'), flip)]
  transfers between devices with their start and end apart: 4 -> 4, of which waited for: 2 -> 3; matrix products, arithmetic and copies ran while one was open for 4% -> 5% of each run, Pallas kernels for 0% -> 0%
where the time goes in v12:
time: 246 us; the launch traced here: 245 us
  waiting for transfers between devices  146 us (59%)
  starting transfers between devices  32.7 us (13%)
  blocking collectives  18.9 us (8%)
  matrix products  14.7 us (6%)
  local copies, waits for them, and re-layouts  13.8 us (6%)
  between operations  13.6 us (6%)
  other arithmetic  5.96 us (2%)
    reduce_scatter x1, waiting for transfers between devices, body(): lax.psum_scatter(partial.reshape(seq_n, branches * sub, length), 'seq', s...  84.3 us
    all_to_all x1, waiting for transfers between devices, body(): gathered = lax.all_to_all(copies, ('zhi', 'inner'), 0, 1, tiled=True)  34.7 us
    all_to_all x1, starting transfers between devices, body(): gathered = lax.all_to_all(copies, ('zhi', 'inner'), 0, 1, tiled=True)  31 us
    all_gather x1, waiting for transfers between devices, body(): whole = lax.all_gather(pair, 'inner', axis=2, tiled=False)  26.7 us
    all_to_all x1, blocking collectives, body(): incoming = lax.all_to_all(outgoing, ('seq', 'zhi'), 0, 0, tiled=True)  18.9 us
  transfers between devices with their start and end apart: 4, of which 3 were waited for; matrix products, arithmetic and copies ran while one was open for 5% of the time, Pallas kernels for 0%

profile of v12, /device:TPU:1, one launch (start us, length us, event | category | flops | bytes accessed | tf_op | source)
XLA Modules:
  0.0 245.4 jit_solution(10444796863998754003)
XLA Ops:
  6.5 0.0 copy-start
  6.5 1.6 collective-permute-start
  8.2 0.0 collective-permute-done
  8.2 0.1 copy.43
  8.3 1.2 tile.2
  9.5 31.0 %all-to-all-start = ((bf16[16,128,256]{1,2,0:T(8,128)(2,1)}), bf16[16,128,256]{1,2,0:T(8,128)(2,1)S(1)}, u32[]{:S(2)}, u32[]{:S(2)}) async-start(bf16[16,128,256]{1,2,0:T(8,128)(2,1)} %tile.2), calls=%async_computation | async-start | bytes 2097152 | tf_op jit(solution)/shard_map/all_to_all | solution.py:31
  40.5 0.0 reduce-scatter.2.cloned.1.call-start
  40.5 2.3 copy.41
  42.9 2.1 copy.42
  45.0 34.7 %all-to-all-done = bf16[16,128,256]{1,2,0:T(8,128)(2,1)S(1)} async-done(((bf16[16,128,256]{1,2,0:T(8,128)(2,1)}), bf16[16,128,256]{1,2,0:T(8,128)(2,1)S(1)}, u32[]{:S(2)}, u32[]{:S(2)}) %all-to-all-start) | async-done | bytes 1048608 | tf_op jit(solution)/shard_map/all_to_all | solution.py:31
  79.7 1.0 copy-done.1
  80.7 1.5 copy.44
  82.1 3.8 %fusion.31 = f32[8,96,1024]{2,1,0:T(8,128)} fusion(bf16[8,96,512]{2,1,0:T(8,128)(2,1)} %bitcast.81, bf16[1024,512,1]{1,0,2:T(8,128)(2,1)S(1)} %bitcast.78), kind=kOutput, calls=%fused_computation.68 | convolution fusion | flops 805306368 | bytes 4980736 | tf_op jit(solution)/shard_map/dgjc,td->gjct/dot_general | solution.py:38
  85.9 0.0 reduce-scatter.2.cloned.1.call-update
  86.0 0.0 all-gather.2.cloned.1.call-start
  86.0 1.1 constant_dynamic-slice_fusion.5
  87.1 0.0 copy-done.4
  87.1 0.0 copy-done.5
  87.1 0.1 dynamic-slice_negate_fusion
  87.2 0.7 copy.48
  87.9 0.1 copy.54
  88.0 0.1 copy.45
  88.0 0.6 dynamic_slice.15
  88.7 0.5 broadcast_subtract_fusion
  89.2 0.6 iota_compare_fusion.2
  89.9 0.7 convert_multiply_fusion
  90.5 0.4 fusion.20
  91.0 3.6 %fusion = f32[64,64,32]{1,2,0:T(8,128)S(1)} fusion(f32[32,64,1]{1,0,2:T(8,128)S(1)} %bitcast.89, s32[64,64]{1,0:T(8,128)S(1)} %iota_subtract_fusion), kind=kOutput, calls=%fused_computation.2 | convolution fusion | flops 100925440 | bytes 548864 | tf_op jit(solution)/shard_map/tsk,kc->tsc/dot_general | solution.py:72
  94.6 84.3 %reduce-scatter.2.cloned.1.call-done = f32[1,96,1024]{2,1,0:T(8,128)} async-done(((f32[8,96,1024]{2,1,0:T(8,128)}), f32[1,96,1024]{2,1,0:T(8,128)}) %reduce-scatter.2.cloned.1.call-update) | async-done | bytes 393232 | tf_op jit(solution)/shard_map/reduce_scatter | solution.py:41
  178.8 1.0 reduce_precision.12
  179.9 0.8 fusion.11
  180.7 0.7 slice_bitcast_fusion
  181.4 0.1 mul.204
  181.5 2.9 %fusion.2 = f32[32,16,64]{2,1,0:T(8,128)} fusion(f32[16,64,32]{1,0,2:T(8,128)S(1)} %mul.204, f32[64,64,32]{1,2,0:T(8,128)S(1)} %fusion), kind=kOutput, calls=%fused_computation.7 | convolution fusion | flops 25165824 | bytes 786432 | tf_op jit(solution)/shard_map/tsc,bsc->btc/dot_general | solution.py:73
  184.4 1.3 convolution_bitcast_fusion
  185.7 0.2 copy.47
  185.8 1.5 multiply_reduce_fusion
  187.3 0.2 copy.49
  187.5 1.5 fusion.1
  189.0 0.1 reshape.146
  189.1 0.0 copy-done.2
  189.2 0.1 fusion.23
  189.3 18.9 %all_to_all.22 = bf16[16,128,32]{1,2,0:T(8,128)(2,1)S(1)} all-to-all(bf16[16,128,32]{1,2,0:T(8,128)(2,1)S(1)} %bitcast.85), channel_id=1, replica_groups=mesh['dp'=4,'seq'=8,'zhi'=2,'inner'=8] {'seq','zhi'}, dimensions={0} | all-to-all | bytes 262144 | tf_op jit(solution)/shard_map/all_to_all | solution.py:91
  208.2 0.8 copy.52
  209.0 0.0 all-gather.2.cloned.1.call-update
  209.0 26.7 %all-gather.2.cloned.1.call-done = bf16[128,2,8,256]{3,0,1,2:T(8,128)(2,1)} async-done(((bf16[128,2,1,256]{3,0,1,2:T(8,128)(2,1)}), bf16[128,2,8,256]{3,0,1,2:T(8,128)(2,1)}) %all-gather.2.cloned.1.call-update) | async-done | bytes 1048592 | tf_op jit(solution)/shard_map/all_gather | solution.py:94
  235.7 1.6 copy.53
  237.3 1.2 convolution_convert_fusion
  (25 shorter events, 0.1 us)
Async XLA Ops:
  6.5 230.8 %copy-start = (bf16[4096,256]{1,0:T(8,128)(2,1)S(1)}, bf16[4096,256]{1,0:T(8,128)(2,1)}, u32[]{:S(2)}) copy-start(bf16[4096,256]{1,0:T(8,128)(2,1)} %param.13) | copy-start | bytes 6291460
  6.5 1.6 collective-permute-start
  9.5 70.2 %all-to-all-start = ((bf16[16,128,256]{1,2,0:T(8,128)(2,1)}), bf16[16,128,256]{1,2,0:T(8,128)(2,1)S(1)}, u32[]{:S(2)}, u32[]{:S(2)}) async-start(bf16[16,128,256]{1,2,0:T(8,128)(2,1)} %tile.2), calls=%async_computation | async-start | bytes 2097152 | tf_op jit(solution)/shard_map/all_to_all | solution.py:31
  40.5 138.3 %reduce-scatter.2.cloned.1.call-start = ((), (), s32[]{:S(2)}) async-start(), calls=%async_computation.3 | async-start | bytes 3538944 | tf_op jit(solution)/shard_map/reduce_scatter | solution.py:41
  79.7 1.0 copy-start.1
  85.9 1.2 copy-start.4
  85.9 1.2 copy-start.5
  85.9 2.1 copy-start.8
  86.0 149.7 %all-gather.2.cloned.1.call-start = ((), (), s32[]{:S(2)}) async-start(), calls=%async_computation.4 | async-start | bytes 1179648 | tf_op jit(solution)/shard_map/all_gather | solution.py:94
  87.2 3.8 %copy-start.3 = (f32[16,32]{1,0:T(8,128)}, f32[16,32]{1,0:T(8,128)S(1)}, u32[]{:S(2)}) copy-start(f32[16,32]{1,0:T(8,128)S(1)} %get-tuple-element.14) | copy-start | bytes 6148
  88.7 92.7 %copy-start.7 = (f32[64]{0:T(128)}, f32[64]{0:T(128)S(1)}, u32[]{:S(2)}) copy-start(f32[64]{0:T(128)S(1)} %iota_convert_fusion) | copy-start | bytes 772
  184.4 4.7 %copy-start.2 = (f32[4,8,8,128]{3,1,2,0:T(8,128)S(1)}, f32[4,8,8,128]{3,1,2,0:T(8,128)}, u32[]{:S(2)}) copy-start(f32[4,8,8,128]{3,1,2,0:T(8,128)} %get-tuple-element.5) | copy-start | bytes 393220
  184.4 4.8 %copy-start.6 = (f32[32]{0:T(128)S(1)}, f32[32]{0:T(128)}, u32[]{:S(2)}) copy-start(f32[32]{0:T(128)} %dynamic_slice.15) | copy-start | bytes 388
Sparse Core Ops, SparseCore 0:
  86.1 92.7 reduce-scatter.1
  209.2 26.4 all-gather.1

commit v13 on v12

--- a/solution.py
+++ b/solution.py
@@ -21,17 +21,24 @@
     sub = channels // seq_n
     length = tok_rows * seq_n
     taps_count = short_taps.shape[1]
-    flip = []
+    y_n = inner_n // halves
+
+    def mirror(c):
+        return (outer_n - 1 - c // y_n) * y_n + c % y_n
+
+    flip, flip_far = [], []
     for s in range(seq_n):
         for c in range(seq_n):
             for e in range(halves):
                 flip.append((s * ten_n + c * halves + e, c * ten_n + s * halves + e))
-    flipped = lax.ppermute(features, ("seq", "zhi", "inner"), flip)
-    copies = jnp.tile(flipped, (ten_n, 1))
-    gathered = lax.all_to_all(copies, ("zhi", "inner"), 0, 1, tiled=True)
+                flip_far.append((s * ten_n + c * halves + e, c * ten_n + mirror(s) * halves + e))
+    near = lax.ppermute(features, ("seq", "zhi", "inner"), flip)
+    away = lax.ppermute(features, ("seq", "zhi", "inner"), flip_far)
+    pair = jnp.where(far == 0, jnp.stack([near, away]), jnp.stack([away, near]))
+    gathered = lax.all_gather(pair, "inner", axis=0, tiled=False)
     rows_of_feats = (
-        gathered.reshape(tok_rows, seq_n, halves * fcols)
-        .transpose(1, 0, 2)
+        gathered.reshape(y_n, halves, outer_n, tok_rows, fcols)
+        .transpose(2, 0, 3, 1, 4)
         .reshape(length, rows_here)
     )
     weight_rows = in_weight.reshape(rows_here, branches, seq_n, sub).transpose(0, 2, 1, 3)

time: 246 us -> 224 us (0.911)
  starting transfers between devices: 32.7 us -> 18 us
  waiting for transfers between devices: 146 us -> 141 us
    all_to_all x1 -> x0, waiting for transfers between devices: 34.7 us -> none  [body(): gathered = lax.all_to_all(copies, ('zhi', 'inner'), 0, 1, tiled=True)]
    all_gather x0 -> x1, waiting for transfers between devices: none -> 34.6 us  [body(): gathered = lax.all_gather(pair, 'inner', axis=0, tiled=False)]
    all_to_all x1 -> x0, starting transfers between devices: 31 us -> none  [body(): gathered = lax.all_to_all(copies, ('zhi', 'inner'), 0, 1, tiled=True)]
    ppermute x1 -> x2, starting transfers between devices: 1.62 us -> 17.9 us  [the longest x1 16.4 us: body(): away = lax.ppermute(features, ('seq', 'zhi', 'inner'), flip_far)]
    reduce_scatter x1, waiting for transfers between devices: 84.3 us -> 75.2 us  [body(): lax.psum_scatter(partial.reshape(seq_n, branches * sub, length), 'seq', s...]
    ppermute x1 -> x2, waiting for transfers between devices: 0.01 us -> 4.29 us  [the longest x1 4.29 us: body(): away = lax.ppermute(features, ('seq', 'zhi', 'inner'), flip_far)]
    dot_general x1 -> x0, matrix products: 3.79 us -> none  [body(): jnp.einsum('dgjc,td->gjct', weight_rows, rows_of_feats, preferred_element...]
    unnamed x0 -> x1, matrix products: none -> 2.65 us
  transfers between devices with their start and end apart: 4 -> 5, of which waited for: 3 -> 4; matrix products, arithmetic and copies ran while one was open for 5% -> 5% of each run, Pallas kernels for 0% -> 0%
where the time goes in v13:
time: 224 us; the launch traced here: 223 us
  waiting for transfers between devices  141 us (63%)
  blocking collectives  18.9 us (8%)
  starting transfers between devices  18 us (8%)
  matrix products  13.6 us (6%)
  between operations  13.3 us (6%)
  local copies, waits for them, and re-layouts  11.7 us (5%)
  other arithmetic  6.65 us (3%)
    reduce_scatter x1, waiting for transfers between devices, body(): lax.psum_scatter(partial.reshape(seq_n, branches * sub, length), 'seq', s...  75.2 us
    all_gather x1, waiting for transfers between devices, body(): gathered = lax.all_gather(pair, 'inner', axis=0, tiled=False)  34.6 us
    all_gather x1, waiting for transfers between devices, body(): whole = lax.all_gather(pair, 'inner', axis=2, tiled=False)  26.7 us
    all_to_all x1, blocking collectives, body(): incoming = lax.all_to_all(outgoing, ('seq', 'zhi'), 0, 0, tiled=True)  18.9 us
    ppermute x1, starting transfers between devices, body(): away = lax.ppermute(features, ('seq', 'zhi', 'inner'), flip_far)  16.4 us
  transfers between devices with their start and end apart: 5, of which 4 were waited for; matrix products, arithmetic and copies ran while one was open for 5% of the time, Pallas kernels for 0%

profile of v13, /device:TPU:1, one launch (start us, length us, event | category | flops | bytes accessed | tf_op | source)
XLA Modules:
  0.0 223.0 jit_solution(11507558309396324006)
XLA Ops:
  6.5 0.0 copy-start
  6.5 0.0 all-gather.3.cloned.1.call-start
  6.5 16.4 %collective-permute-start.1 = (bf16[128,256]{1,0:T(8,128)(2,1)}, bf16[128,256]{1,0:T(8,128)(2,1)S(1)}, u32[]{:S(2)}, u32[]{:S(2)}) collective-permute-start(bf16[128,256]{1,0:T(8,128)(2,1)} %param.7), channel_id=1, source_target_pairs={{0,8},{1,9},{2,24},{3,25},{4,40},{5,41},{6,56},{7,57},{8,72},{9,73... | collective-permute-start | bytes 196616 | tf_op jit(solution)/shard_map/ppermute | solution.py:36
  22.9 1.5 collective-permute-start
  24.4 4.3 %collective-permute-done.1 = bf16[128,256]{1,0:T(8,128)(2,1)S(1)} collective-permute-done((bf16[128,256]{1,0:T(8,128)(2,1)}, bf16[128,256]{1,0:T(8,128)(2,1)S(1)}, u32[]{:S(2)}, u32[]{:S(2)}) %collective-permute-start.1) | collective-permute-done | bytes 65568 | tf_op jit(solution)/shard_map/ppermute | solution.py:36
  28.7 0.0 collective-permute-done
  28.7 0.7 maximum_select_fusion
  29.4 0.0 all-gather.3.cloned.1.call-update
  29.4 0.0 reduce-scatter.2.cloned.1.call-start
  29.5 2.3 %copy.41 = bf16[512,3,256]{0,2,1:T(8,128)(2,1)} copy(bf16[512,3,256]{2,0,1:T(8,128)(2,1)} %param.8) | data formatting | bytes 1572864 | tf_op args[1]
  31.8 1.2 copy.42
  33.0 34.6 %all-gather.3.cloned.1.call-done = bf16[8,2,128,256]{3,2,1,0:T(8,128)(2,1)} async-done(((bf16[1,2,128,256]{3,2,1,0:T(8,128)(2,1)}), bf16[8,2,128,256]{3,2,1,0:T(8,128)(2,1)}) %all-gather.3.cloned.1.call-update) | async-done | bytes 1048592 | tf_op jit(solution)/shard_map/all_gather | solution.py:38
  67.6 2.3 %copy.40 = bf16[4,2,2,128,256]{4,1,3,0,2:T(2,128)(2,1)S(1)} copy(bf16[4,2,2,128,256]{4,3,2,1,0:T(8,128)(2,1)} %bitcast.90) | data formatting | bytes 2097152 | tf_op jit(solution)/shard_map/reshape | solution.py:40
  69.9 0.2 copy.61
  70.2 2.7 %fusion.31 = f32[1024,768]{0,1} fusion(bf16[1024,512]{1,0:T(8,128)(2,1)S(1)} %bitcast.83, bf16[512,768]{0,1:T(8,128)(2,1)S(1)} %bitcast.86), kind=kOutput, calls=%fused_computation.69 | convolution fusion | flops 805306368 | bytes 4980736
  72.8 0.0 reduce-scatter.2.cloned.1.call-update
  72.9 0.0 all-gather.5.cloned.1.call-start
  72.9 1.1 constant_dynamic-slice_fusion.5
  74.0 0.0 copy-done.3
  74.0 0.1 dynamic-slice_negate_fusion
  74.1 0.7 copy.46
  74.8 0.1 copy.52
  74.9 0.1 copy.43
  74.9 0.7 dynamic_slice.15
  75.6 0.5 broadcast_subtract_fusion
  76.2 0.6 iota_compare_fusion.2
  76.8 0.7 convert_multiply_fusion
  77.5 0.4 fusion.20
  77.9 3.6 %fusion = f32[64,64,32]{1,2,0:T(8,128)S(1)} fusion(f32[32,64,1]{1,0,2:T(8,128)S(1)} %bitcast.97, s32[64,64]{1,0:T(8,128)S(1)} %iota_subtract_fusion), kind=kOutput, calls=%fused_computation.2 | convolution fusion | flops 100925440 | bytes 548864 | tf_op jit(solution)/shard_map/tsk,kc->tsc/dot_general | solution.py:79
  81.5 75.2 %reduce-scatter.2.cloned.1.call-done = f32[1,96,1024]{2,1,0:T(8,128)} async-done(((f32[8,96,1024]{2,1,0:T(8,128)}), f32[1,96,1024]{2,1,0:T(8,128)}) %reduce-scatter.2.cloned.1.call-update) | async-done | bytes 393232 | tf_op jit(solution)/shard_map/reduce_scatter | solution.py:48
  156.8 1.0 reduce_precision.12
  157.8 0.8 fusion.11
  158.6 0.7 slice_bitcast_fusion
  159.3 0.1 mul.204
  159.4 2.9 %fusion.2 = f32[32,16,64]{2,1,0:T(8,128)} fusion(f32[16,64,32]{1,0,2:T(8,128)S(1)} %mul.204, f32[64,64,32]{1,2,0:T(8,128)S(1)} %fusion), kind=kOutput, calls=%fused_computation.7 | convolution fusion | flops 25165824 | bytes 786432 | tf_op jit(solution)/shard_map/tsc,bsc->btc/dot_general | solution.py:80
  162.3 1.3 convolution_bitcast_fusion
  163.6 0.2 copy.45
  163.7 1.5 multiply_reduce_fusion
  165.2 0.2 copy.47
  165.4 1.5 fusion.1
  166.9 0.1 reshape.198
  167.1 0.1 fusion.23
  167.2 18.9 %all_to_all.9 = bf16[16,128,32]{1,2,0:T(8,128)(2,1)S(1)} all-to-all(bf16[16,128,32]{1,2,0:T(8,128)(2,1)S(1)} %bitcast.91), channel_id=1, replica_groups=mesh['dp'=4,'seq'=8,'zhi'=2,'inner'=8] {'seq','zhi'}, dimensions={0} | all-to-all | bytes 262144 | tf_op jit(solution)/shard_map/all_to_all | solution.py:98
  186.1 0.8 copy.50
  186.9 0.0 all-gather.5.cloned.1.call-update
  186.9 26.7 %all-gather.5.cloned.1.call-done = bf16[128,2,8,256]{3,0,1,2:T(8,128)(2,1)} async-done(((bf16[128,2,1,256]{3,0,1,2:T(8,128)(2,1)}), bf16[128,2,8,256]{3,0,1,2:T(8,128)(2,1)}) %all-gather.5.cloned.1.call-update) | async-done | bytes 1048592 | tf_op jit(solution)/shard_map/all_gather | solution.py:101
  213.6 1.6 copy.51
  215.3 1.2 convolution_convert_fusion
  (26 shorter events, 0.1 us)
Async XLA Ops:
  6.5 208.7 %copy-start = (bf16[4096,256]{1,0:T(8,128)(2,1)S(1)}, bf16[4096,256]{1,0:T(8,128)(2,1)}, u32[]{:S(2)}) copy-start(bf16[4096,256]{1,0:T(8,128)(2,1)} %param.13) | copy-start | bytes 6291460
  6.5 61.1 %all-gather.3.cloned.1.call-start = ((), (), s32[]{:S(2)}) async-start(), calls=%async_computation.2 | async-start | bytes 1179648 | tf_op jit(solution)/shard_map/all_gather | solution.py:38
  6.5 22.2 %collective-permute-start.1 = (bf16[128,256]{1,0:T(8,128)(2,1)}, bf16[128,256]{1,0:T(8,128)(2,1)S(1)}, u32[]{:S(2)}, u32[]{:S(2)}) collective-permute-start(bf16[128,256]{1,0:T(8,128)(2,1)} %param.7), channel_id=1, source_target_pairs={{0,8},{1,9},{2,24},{3,25},{4,40},{5,41},{6,56},{7,57},{8,72},{9,73... | collective-permute-start | bytes 196616 | tf_op jit(solution)/shard_map/ppermute | solution.py:36
  22.9 5.8 %collective-permute-start = (bf16[128,256]{1,0:T(8,128)(2,1)}, bf16[128,256]{1,0:T(8,128)(2,1)S(1)}, u32[]{:S(2)}, u32[]{:S(2)}) collective-permute-start(bf16[128,256]{1,0:T(8,128)(2,1)} %param.7), channel_id=1, source_target_pairs={{0,0},{1,1},{2,16},{3,17},{4,32},{5,33},{6,48},{7,49},{8,64},{9,65... | collective-permute-start | bytes 196616 | tf_op jit(solution)/shard_map/ppermute | solution.py:35
  29.4 127.3 %reduce-scatter.2.cloned.1.call-start = ((), (), s32[]{:S(2)}) async-start(), calls=%async_computation.3 | async-start | bytes 3538944 | tf_op jit(solution)/shard_map/reduce_scatter | solution.py:48
  72.8 1.2 copy-start.3
  72.8 1.2 copy-start.4
  72.8 2.1 copy-start.7
  72.9 140.7 %all-gather.5.cloned.1.call-start = ((), (), s32[]{:S(2)}) async-start(), calls=%async_computation.4 | async-start | bytes 1179648 | tf_op jit(solution)/shard_map/all_gather | solution.py:101
  74.1 3.8 %copy-start.2 = (f32[16,32]{1,0:T(8,128)}, f32[16,32]{1,0:T(8,128)S(1)}, u32[]{:S(2)}) copy-start(f32[16,32]{1,0:T(8,128)S(1)} %get-tuple-element.14) | copy-start | bytes 6148
  75.6 82.2 %copy-start.6 = (f32[64]{0:T(128)}, f32[64]{0:T(128)S(1)}, u32[]{:S(2)}) copy-start(f32[64]{0:T(128)S(1)} %iota_convert_fusion) | copy-start | bytes 772
  162.3 4.7 %copy-start.1 = (f32[4,8,8,128]{3,1,2,0:T(8,128)S(1)}, f32[4,8,8,128]{3,1,2,0:T(8,128)}, u32[]{:S(2)}) copy-start(f32[4,8,8,128]{3,1,2,0:T(8,128)} %get-tuple-element.5) | copy-start | bytes 393220
  162.3 4.8 %copy-start.5 = (f32[32]{0:T(128)S(1)}, f32[32]{0:T(128)}, u32[]{:S(2)}) copy-start(f32[32]{0:T(128)} %dynamic_slice.15) | copy-start | bytes 388
Sparse Core Ops, SparseCore 0:
  29.5 38.0 all-gather.2
  73.0 83.7 reduce-scatter.1
  187.0 26.5 all-gather.4

commit v14 on v12

--- a/solution.py
+++ b/solution.py
@@ -21,19 +21,21 @@
     sub = channels // seq_n
     length = tok_rows * seq_n
     taps_count = short_taps.shape[1]
-    flip = []
+    routes = [[], []]
     for s in range(seq_n):
         for c in range(seq_n):
             for e in range(halves):
-                flip.append((s * ten_n + c * halves + e, c * ten_n + s * halves + e))
-    flipped = lax.ppermute(features, ("seq", "zhi", "inner"), flip)
-    copies = jnp.tile(flipped, (ten_n, 1))
-    gathered = lax.all_to_all(copies, ("zhi", "inner"), 0, 1, tiled=True)
-    rows_of_feats = (
-        gathered.reshape(tok_rows, seq_n, halves * fcols)
-        .transpose(1, 0, 2)
-        .reshape(length, rows_here)
-    )
+                for h in range(outer_n):
+                    src_id = s * ten_n + c * halves + e
+                    dst_id = c * ten_n + h * inner_n + s
+                    routes[(e + h) % 2].append((src_id, dst_id))
+    first = lax.ppermute(features, ("seq", "zhi", "inner"), routes[0])
+    second = lax.ppermute(features, ("seq", "zhi", "inner"), routes[1])
+    col_lo = jnp.where(far == 0, first, second)
+    col_hi = jnp.where(far == 0, second, first)
+    pair = jnp.concatenate([col_lo, col_hi], axis=1)
+    gathered = lax.all_gather(pair, "inner", axis=0, tiled=True)
+    rows_of_feats = gathered.reshape(length, rows_here)
     weight_rows = in_weight.reshape(rows_here, branches, seq_n, sub).transpose(0, 2, 1, 3)
     partial = jnp.einsum(
         "dgjc,td->gjct", weight_rows, rows_of_feats, preferred_element_type=jnp.float32

time: 246 us -> 220 us (0.89)
  starting transfers between devices: 32.7 us -> 19 us
  waiting for transfers between devices: 146 us -> 138 us
  local copies, waits for them, and re-layouts: 13.8 us -> 9.03 us
    all_to_all x1 -> x0, waiting for transfers between devices: 34.7 us -> none  [body(): gathered = lax.all_to_all(copies, ('zhi', 'inner'), 0, 1, tiled=True)]
    all_gather x0 -> x1, waiting for transfers between devices: none -> 31.7 us  [body(): gathered = lax.all_gather(pair, 'inner', axis=0, tiled=True)]
    all_to_all x1 -> x0, starting transfers between devices: 31 us -> none  [body(): gathered = lax.all_to_all(copies, ('zhi', 'inner'), 0, 1, tiled=True)]
    ppermute x1 -> x2, starting transfers between devices: 1.62 us -> 18.9 us  [the longest x1 17 us: body(): first = lax.ppermute(features, ('seq', 'zhi', 'inner'), routes[0])]
    reduce_scatter x1, waiting for transfers between devices: 84.3 us -> 75.3 us  [body(): lax.psum_scatter(partial.reshape(seq_n, branches * sub, length), 'seq', s...]
    unnamed x0 -> x1, matrix products: none -> 3.89 us
    ppermute x1 -> x2, waiting for transfers between devices: 0.01 us -> 3.83 us  [the longest x1 3.41 us: body(): second = lax.ppermute(features, ('seq', 'zhi', 'inner'), routes[1])]
    dot_general x1 -> x0, matrix products: 3.79 us -> none  [body(): jnp.einsum('dgjc,td->gjct', weight_rows, rows_of_feats, preferred_element...]
  transfers between devices with their start and end apart: 4 -> 5, of which waited for: 3 -> 5; matrix products, arithmetic and copies ran while one was open for 5% -> 5% of each run, Pallas kernels for 0% -> 0%
where the time goes in v14:
time: 220 us; the launch traced here: 219 us
  waiting for transfers between devices  138 us (63%)
  starting transfers between devices  19 us (9%)
  blocking collectives  18.9 us (9%)
  matrix products  14.8 us (7%)
  between operations  13.4 us (6%)
  local copies, waits for them, and re-layouts  9.03 us (4%)
  other arithmetic  6.65 us (3%)
    reduce_scatter x1, waiting for transfers between devices, body(): lax.psum_scatter(partial.reshape(seq_n, branches * sub, length), 'seq', s...  75.3 us
    all_gather x1, waiting for transfers between devices, body(): gathered = lax.all_gather(pair, 'inner', axis=0, tiled=True)  31.7 us
    all_gather x1, waiting for transfers between devices, body(): whole = lax.all_gather(pair, 'inner', axis=2, tiled=False)  26.7 us
    all_to_all x1, blocking collectives, body(): incoming = lax.all_to_all(outgoing, ('seq', 'zhi'), 0, 0, tiled=True)  18.9 us
    ppermute x1, starting transfers between devices, body(): first = lax.ppermute(features, ('seq', 'zhi', 'inner'), routes[0])  17 us
  transfers between devices with their start and end apart: 5, of which 5 were waited for; matrix products, arithmetic and copies ran while one was open for 5% of the time, Pallas kernels for 0%

profile of v14, /device:TPU:1, one launch (start us, length us, event | category | flops | bytes accessed | tf_op | source)
XLA Modules:
  0.0 219.3 jit_solution(17063175377069945098)
XLA Ops:
  6.5 0.0 copy-start
  6.5 0.0 all-gather.3.cloned.1.call-start
  6.5 17.0 %collective-permute-start = (bf16[128,256]{1,0:T(8,128)(2,1)}, bf16[128,256]{1,0:T(8,128)(2,1)S(1)}, u32[]{:S(2)}, u32[]{:S(2)}) collective-permute-start(bf16[128,256]{1,0:T(8,128)(2,1)} %param.7), channel_id=1, source_target_pairs={{0,0},{1,8},{2,16},{3,24},{4,32},{5,40},{6,48},{7,56},{8,64},{9,72... | collective-permute-start | bytes 196616 | tf_op jit(solution)/shard_map/ppermute | solution.py:32
  23.5 1.9 collective-permute-start.1
  25.4 0.4 collective-permute-done
  25.8 3.4 %collective-permute-done.1 = bf16[128,256]{1,0:T(8,128)(2,1)S(1)} collective-permute-done((bf16[128,256]{1,0:T(8,128)(2,1)}, bf16[128,256]{1,0:T(8,128)(2,1)S(1)}, u32[]{:S(2)}, u32[]{:S(2)}) %collective-permute-start.1) | collective-permute-done | bytes 65568 | tf_op jit(solution)/shard_map/ppermute | solution.py:33
  29.3 0.7 pad_maximum_fusion
  29.9 0.0 all-gather.3.cloned.1.call-update
  30.0 0.0 reduce-scatter.2.cloned.1.call-start
  30.0 2.3 %copy.36 = bf16[512,3,256]{0,2,1:T(8,128)(2,1)} copy(bf16[512,3,256]{2,0,1:T(8,128)(2,1)} %param.8) | data formatting | bytes 1572864 | tf_op args[1]
  32.3 1.2 copy.37
  33.5 31.7 %all-gather.3.cloned.1.call-done = bf16[1024,512]{1,0:T(8,128)(2,1)} async-done(((bf16[128,512]{1,0:T(8,128)(2,1)}), bf16[1024,512]{1,0:T(8,128)(2,1)}) %all-gather.3.cloned.1.call-update) | async-done | bytes 1048592 | tf_op jit(solution)/shard_map/all_gather | solution.py:37
  65.2 3.9 %fusion.31 = f32[1024,768]{0,1} fusion(bf16[1024,512]{1,0:T(8,128)(2,1)} %all-gather.3.cloned.1.call-done, bf16[512,768]{0,1:T(8,128)(2,1)S(1)} %bitcast.77), kind=kOutput, calls=%fused_computation.71 | convolution fusion | flops 805306368 | bytes 4980736
  69.1 0.0 reduce-scatter.2.cloned.1.call-update
  69.1 0.0 all-gather.5.cloned.1.call-start
  69.2 1.1 constant_dynamic-slice_fusion.5
  70.3 0.0 copy-done.3
  70.3 0.0 copy-done.4
  70.3 0.1 dynamic-slice_negate_fusion
  70.4 0.7 copy.41
  71.1 0.1 copy.47
  71.1 0.1 copy.38
  71.2 0.0 copy-done.7
  71.2 0.6 dynamic_slice.15
  71.8 0.5 broadcast_subtract_fusion
  72.4 0.6 iota_compare_fusion.2
  73.0 0.7 convert_multiply_fusion
  73.7 0.4 fusion.20
  74.1 3.6 %fusion = f32[64,64,32]{1,2,0:T(8,128)S(1)} fusion(f32[32,64,1]{1,0,2:T(8,128)S(1)} %bitcast.85, s32[64,64]{1,0:T(8,128)S(1)} %iota_subtract_fusion), kind=kOutput, calls=%fused_computation.2 | convolution fusion | flops 100925440 | bytes 548864 | tf_op jit(solution)/shard_map/tsk,kc->tsc/dot_general | solution.py:74
  77.7 75.3 %reduce-scatter.2.cloned.1.call-done = f32[1,96,1024]{2,1,0:T(8,128)} async-done(((f32[8,96,1024]{2,1,0:T(8,128)}), f32[1,96,1024]{2,1,0:T(8,128)}) %reduce-scatter.2.cloned.1.call-update) | async-done | bytes 393232 | tf_op jit(solution)/shard_map/reduce_scatter | solution.py:43
  153.0 1.0 reduce_precision.12
  154.1 0.8 fusion.11
  154.9 0.7 slice_bitcast_fusion
  155.6 0.1 mul.204
  155.7 2.9 %fusion.2 = f32[32,16,64]{2,1,0:T(8,128)} fusion(f32[16,64,32]{1,0,2:T(8,128)S(1)} %mul.204, f32[64,64,32]{1,2,0:T(8,128)S(1)} %fusion), kind=kOutput, calls=%fused_computation.7 | convolution fusion | flops 25165824 | bytes 786432 | tf_op jit(solution)/shard_map/tsc,bsc->btc/dot_general | solution.py:75
  158.6 1.3 convolution_bitcast_fusion
  159.9 0.2 copy.40
  160.0 1.5 multiply_reduce_fusion
  161.5 0.2 copy.42
  161.7 1.5 fusion.1
  163.1 0.1 reshape.131
  163.3 0.1 fusion.23
  163.5 18.9 %all_to_all.9 = bf16[16,128,32]{1,2,0:T(8,128)(2,1)S(1)} all-to-all(bf16[16,128,32]{1,2,0:T(8,128)(2,1)S(1)} %bitcast.81), channel_id=1, replica_groups=mesh['dp'=4,'seq'=8,'zhi'=2,'inner'=8] {'seq','zhi'}, dimensions={0} | all-to-all | bytes 262144 | tf_op jit(solution)/shard_map/all_to_all | solution.py:93
  182.4 0.8 copy.45
  183.2 0.0 all-gather.5.cloned.1.call-update
  183.2 26.7 %all-gather.5.cloned.1.call-done = bf16[128,2,8,256]{3,0,1,2:T(8,128)(2,1)} async-done(((bf16[128,2,1,256]{3,0,1,2:T(8,128)(2,1)}), bf16[128,2,8,256]{3,0,1,2:T(8,128)(2,1)}) %all-gather.5.cloned.1.call-update) | async-done | bytes 1048592 | tf_op jit(solution)/shard_map/all_gather | solution.py:96
  209.9 1.6 copy.46
  211.5 1.2 convolution_convert_fusion
  (25 shorter events, 0.2 us)
Async XLA Ops:
  6.5 205.0 %copy-start = (bf16[4096,256]{1,0:T(8,128)(2,1)S(1)}, bf16[4096,256]{1,0:T(8,128)(2,1)}, u32[]{:S(2)}) copy-start(bf16[4096,256]{1,0:T(8,128)(2,1)} %param.13) | copy-start | bytes 6291460
  6.5 58.7 %all-gather.3.cloned.1.call-start = ((), (), s32[]{:S(2)}) async-start(), calls=%async_computation.2 | async-start | bytes 1179648 | tf_op jit(solution)/shard_map/all_gather | solution.py:37
  6.5 19.3 %collective-permute-start = (bf16[128,256]{1,0:T(8,128)(2,1)}, bf16[128,256]{1,0:T(8,128)(2,1)S(1)}, u32[]{:S(2)}, u32[]{:S(2)}) collective-permute-start(bf16[128,256]{1,0:T(8,128)(2,1)} %param.7), channel_id=1, source_target_pairs={{0,0},{1,8},{2,16},{3,24},{4,32},{5,40},{6,48},{7,56},{8,64},{9,72... | collective-permute-start | bytes 196616 | tf_op jit(solution)/shard_map/ppermute | solution.py:32
  23.5 5.8 %collective-permute-start.1 = (bf16[128,256]{1,0:T(8,128)(2,1)}, bf16[128,256]{1,0:T(8,128)(2,1)S(1)}, u32[]{:S(2)}, u32[]{:S(2)}) collective-permute-start(bf16[128,256]{1,0:T(8,128)(2,1)} %param.7), channel_id=1, source_target_pairs={{0,8},{1,0},{2,24},{3,16},{4,40},{5,32},{6,56},{7,48},{8,72},{9,64... | collective-permute-start | bytes 196616 | tf_op jit(solution)/shard_map/ppermute | solution.py:33
  30.0 123.1 %reduce-scatter.2.cloned.1.call-start = ((), (), s32[]{:S(2)}) async-start(), calls=%async_computation.3 | async-start | bytes 3538944 | tf_op jit(solution)/shard_map/reduce_scatter | solution.py:43
  69.1 1.2 copy-start.3
  69.1 1.2 copy-start.4
  69.1 2.1 copy-start.7
  69.1 140.7 %all-gather.5.cloned.1.call-start = ((), (), s32[]{:S(2)}) async-start(), calls=%async_computation.4 | async-start | bytes 1179648 | tf_op jit(solution)/shard_map/all_gather | solution.py:96
  70.4 3.7 %copy-start.2 = (f32[16,32]{1,0:T(8,128)}, f32[16,32]{1,0:T(8,128)S(1)}, u32[]{:S(2)}) copy-start(f32[16,32]{1,0:T(8,128)S(1)} %get-tuple-element.16) | copy-start | bytes 6148
  71.8 82.2 %copy-start.6 = (f32[64]{0:T(128)}, f32[64]{0:T(128)S(1)}, u32[]{:S(2)}) copy-start(f32[64]{0:T(128)S(1)} %iota_convert_fusion) | copy-start | bytes 772
  158.6 4.7 %copy-start.1 = (f32[4,8,8,128]{3,1,2,0:T(8,128)S(1)}, f32[4,8,8,128]{3,1,2,0:T(8,128)}, u32[]{:S(2)}) copy-start(f32[4,8,8,128]{3,1,2,0:T(8,128)} %get-tuple-element.5) | copy-start | bytes 393220
  158.6 4.8 %copy-start.5 = (f32[32]{0:T(128)S(1)}, f32[32]{0:T(128)}, u32[]{:S(2)}) copy-start(f32[32]{0:T(128)} %dynamic_slice.15) | copy-start | bytes 388
Sparse Core Ops, SparseCore 0:
  30.1 35.0 all-gather.2
  69.3 83.7 reduce-scatter.1
  183.3 26.5 all-gather.4

commit v15 on v14

--- a/solution.py
+++ b/solution.py
@@ -92,13 +92,14 @@
     ).reshape(seq_n * outer_n * tok_rows, sub)
     incoming = lax.all_to_all(outgoing, ("seq", "zhi"), 0, 0, tiled=True)
     pair = incoming.reshape(seq_n, outer_n, tok_rows, sub).transpose(2, 1, 0, 3)
-    pair = pair.reshape(tok_rows, outer_n, seq_n * sub)
-    whole = lax.all_gather(pair, "inner", axis=2, tiled=False)
-    mixed = jnp.dot(
-        whole.reshape(tok_rows, ten_n * channels),
-        out_weight,
-        preferred_element_type=jnp.float32,
+    pair = pair.reshape(tok_rows, outer_n * seq_n * sub)
+    whole = lax.all_gather(pair, "inner", axis=1, tiled=True)
+    weight_out = (
+        out_weight.reshape(outer_n, inner_n, channels, -1)
+        .transpose(1, 0, 2, 3)
+        .reshape(ten_n * channels, -1)
     )
+    mixed = jnp.dot(whole, weight_out, preferred_element_type=jnp.float32)
     return mixed.astype(jnp.bfloat16)
 
 

time: 220 us -> 215 us (0.977)
  local copies, waits for them, and re-layouts: 9.03 us -> 5.86 us
  other arithmetic: 6.65 us -> 3.57 us
  waiting for transfers between devices: 138 us -> 141 us
    reduce_scatter x1, waiting for transfers between devices: 75.3 us -> 78.1 us  [body(): lax.psum_scatter(partial.reshape(seq_n, branches * sub, length), 'seq', s...]
  transfers between devices with their start and end apart: 5 -> 5, of which waited for: 5 -> 5; matrix products, arithmetic and copies ran while one was open for 5% -> 4% of each run, Pallas kernels for 0% -> 0%
where the time goes in v15:
time: 215 us
  waiting for transfers between devices  141 us (66%)
  blocking collectives  18.9 us (9%)
  starting transfers between devices  18.8 us (9%)
  matrix products  13.7 us (6%)
  between operations  13.3 us (6%)
  local copies, waits for them, and re-layouts  5.86 us (3%)
  other arithmetic  3.57 us (2%)
    reduce_scatter x1, waiting for transfers between devices, body(): lax.psum_scatter(partial.reshape(seq_n, branches * sub, length), 'seq', s...  78.1 us
    all_gather x1, waiting for transfers between devices, body(): gathered = lax.all_gather(pair, 'inner', axis=0, tiled=True)  33.7 us
    all_gather x1, waiting for transfers between devices, body(): whole = lax.all_gather(pair, 'inner', axis=1, tiled=True)  25 us
    all_to_all x1, blocking collectives, body(): incoming = lax.all_to_all(outgoing, ('seq', 'zhi'), 0, 0, tiled=True)  18.9 us
    ppermute x1, starting transfers between devices, body(): first = lax.ppermute(features, ('seq', 'zhi', 'inner'), routes[0])  16.8 us
  transfers between devices with their start and end apart: 5, of which 5 were waited for; matrix products, arithmetic and copies ran while one was open for 4% of the time, Pallas kernels for 0%

profile of v15, /device:TPU:1, one launch (start us, length us, event | category | flops | bytes accessed | tf_op | source)
XLA Modules:
  0.0 214.9 jit_solution(1021885329795554757)
XLA Ops:
  6.5 0.0 all-gather.3.cloned.1.call-start
  6.5 16.8 %collective-permute-start = (bf16[128,256]{1,0:T(8,128)(2,1)}, bf16[128,256]{1,0:T(8,128)(2,1)S(1)}, u32[]{:S(2)}, u32[]{:S(2)}) collective-permute-start(bf16[128,256]{1,0:T(8,128)(2,1)} %param.7), channel_id=1, source_target_pairs={{0,0},{1,8},{2,16},{3,24},{4,32},{5,40},{6,48},{7,56},{8,64},{9,72... | collective-permute-start | bytes 196616 | tf_op jit(solution)/shard_map/ppermute | solution.py:32
  23.4 1.9 collective-permute-start.1
  25.3 0.4 collective-permute-done
  25.7 3.4 %collective-permute-done.1 = bf16[128,256]{1,0:T(8,128)(2,1)S(1)} collective-permute-done((bf16[128,256]{1,0:T(8,128)(2,1)}, bf16[128,256]{1,0:T(8,128)(2,1)S(1)}, u32[]{:S(2)}, u32[]{:S(2)}) %collective-permute-start.1) | collective-permute-done | bytes 65568 | tf_op jit(solution)/shard_map/ppermute | solution.py:33
  29.1 0.7 pad_maximum_fusion
  29.8 0.0 all-gather.3.cloned.1.call-update
  29.8 0.0 reduce-scatter.2.cloned.1.call-start
  29.9 1.4 copy.26
  31.3 0.1 copy.27
  31.4 33.7 %all-gather.3.cloned.1.call-done = bf16[1024,512]{1,0:T(8,128)(2,1)} async-done(((bf16[128,512]{1,0:T(8,128)(2,1)}), bf16[1024,512]{1,0:T(8,128)(2,1)}) %all-gather.3.cloned.1.call-update) | async-done | bytes 1048592 | tf_op jit(solution)/shard_map/all_gather | solution.py:37
  65.1 3.9 %fusion.31 = f32[1024,768]{0,1} fusion(bf16[1024,512]{1,0:T(8,128)(2,1)} %all-gather.3.cloned.1.call-done, bf16[512,768]{0,1:T(8,128)(2,1)S(1)} %bitcast.80), kind=kOutput, calls=%fused_computation.71 | convolution fusion | flops 805306368 | bytes 4980736
  69.0 0.0 copy-start
  69.0 0.0 copy-start.1
  69.0 0.0 copy-start.2
  69.0 0.0 reduce-scatter.2.cloned.1.call-update
  69.0 0.0 all-gather.5.cloned.1.call-start
  69.1 1.1 constant_dynamic-slice_fusion.5
  70.1 0.0 copy-done
  70.1 0.0 copy-done.1
  70.2 0.1 dynamic-slice_negate_fusion
  70.2 0.1 copy.31
  70.3 0.1 copy.36
  70.4 0.1 copy.28
  70.5 0.0 copy-done.2
  70.5 0.1 dynamic_slice.15
  70.6 0.1 convert_multiply_fusion
  70.7 0.4 fusion.20
  71.2 3.6 %fusion = f32[64,64,32]{1,2,0:T(8,128)S(1)} fusion(f32[32,64,1]{1,0,2:T(8,128)S(1)} %bitcast.89, s32[64,64]{1,0:T(8,128)S(1)} %iota_subtract_fusion), kind=kOutput, calls=%fused_computation.2 | convolution fusion | flops 100925440 | bytes 548864 | tf_op jit(solution)/shard_map/tsk,kc->tsc/dot_general | solution.py:74
  74.8 78.1 %reduce-scatter.2.cloned.1.call-done = f32[1,96,1024]{2,1,0:T(8,128)} async-done(((f32[8,96,1024]{2,1,0:T(8,128)}), f32[1,96,1024]{2,1,0:T(8,128)}) %reduce-scatter.2.cloned.1.call-update) | async-done | bytes 393232 | tf_op jit(solution)/shard_map/reduce_scatter | solution.py:43
  152.9 1.0 reduce_precision.12
  153.9 0.8 fusion.11
  154.8 0.1 mul.204
  154.9 2.2 %fusion.2 = f32[32,16,64]{2,1,0:T(8,128)S(1)} fusion(f32[16,64,32]{1,0,2:T(8,128)S(1)} %mul.204, f32[64,64,32]{1,2,0:T(8,128)S(1)} %fusion), kind=kOutput, calls=%fused_computation.7 | convolution fusion | flops 25165824 | bytes 786432 | tf_op jit(solution)/shard_map/tsc,bsc->btc/dot_general | solution.py:75
  157.1 0.6 convolution_bitcast_fusion
  157.7 0.2 copy.30
  157.9 0.7 multiply_reduce_fusion
  158.6 0.2 copy.32
  158.8 0.5 fusion.1
  159.3 0.1 reshape.137
  159.5 0.1 fusion.23
  159.6 18.9 %all_to_all.9 = bf16[16,128,32]{1,2,0:T(8,128)(2,1)S(1)} all-to-all(bf16[16,128,32]{1,2,0:T(8,128)(2,1)S(1)} %bitcast.86), channel_id=1, replica_groups=mesh['dp'=4,'seq'=8,'zhi'=2,'inner'=8] {'seq','zhi'}, dimensions={0} | all-to-all | bytes 262144 | tf_op jit(solution)/shard_map/all_to_all | solution.py:93
  178.5 0.7 copy.34
  179.2 0.0 all-gather.5.cloned.1.call-update
  179.2 1.7 copy.35
  180.9 25.0 %all-gather.5.cloned.1.call-done = bf16[128,4096]{0,1:T(8,128)(2,1)} async-done(((bf16[128,512]{0,1:T(8,128)(2,1)}), bf16[128,4096]{0,1:T(8,128)(2,1)}) %all-gather.5.cloned.1.call-update) | async-done | bytes 1048592 | tf_op jit(solution)/shard_map/all_gather | solution.py:96
  205.9 2.4 %convolution_convert_fusion = bf16[128,256]{1,0:T(8,128)(2,1)} fusion(bf16[128,4096]{0,1:T(8,128)(2,1)} %all-gather.5.cloned.1.call-done, bf16[4096,256]{1,0:T(8,128)(2,1)S(1)} %bitcast.79), kind=kOutput, calls=%fused_computation.6 | convolution fusion | flops 268468224 | bytes 3211264 | tf_op jit(solution)/shard_map/dot_general | solution.py:102
  (15 shorter events, 0.2 us)
Async XLA Ops:
  6.5 58.6 %all-gather.3.cloned.1.call-start = ((), (), s32[]{:S(2)}) async-start(), calls=%async_computation.2 | async-start | bytes 1179648 | tf_op jit(solution)/shard_map/all_gather | solution.py:37
  6.5 19.2 %collective-permute-start = (bf16[128,256]{1,0:T(8,128)(2,1)}, bf16[128,256]{1,0:T(8,128)(2,1)S(1)}, u32[]{:S(2)}, u32[]{:S(2)}) collective-permute-start(bf16[128,256]{1,0:T(8,128)(2,1)} %param.7), channel_id=1, source_target_pairs={{0,0},{1,8},{2,16},{3,24},{4,32},{5,40},{6,48},{7,56},{8,64},{9,72... | collective-permute-start | bytes 196616 | tf_op jit(solution)/shard_map/ppermute | solution.py:32
  23.4 5.8 %collective-permute-start.1 = (bf16[128,256]{1,0:T(8,128)(2,1)}, bf16[128,256]{1,0:T(8,128)(2,1)S(1)}, u32[]{:S(2)}, u32[]{:S(2)}) collective-permute-start(bf16[128,256]{1,0:T(8,128)(2,1)} %param.7), channel_id=1, source_target_pairs={{0,8},{1,0},{2,24},{3,16},{4,40},{5,32},{6,56},{7,48},{8,72},{9,64... | collective-permute-start | bytes 196616 | tf_op jit(solution)/shard_map/ppermute | solution.py:33
  29.8 123.1 %reduce-scatter.2.cloned.1.call-start = ((), (), s32[]{:S(2)}) async-start(), calls=%async_computation.3 | async-start | bytes 3538944 | tf_op jit(solution)/shard_map/reduce_scatter | solution.py:43
  69.0 1.2 copy-start
  69.0 1.2 copy-start.1
  69.0 1.5 copy-start.2
  69.0 136.9 %all-gather.5.cloned.1.call-start = ((), (), s32[]{:S(2)}) async-start(), calls=%async_computation.4 | async-start | bytes 1179648 | tf_op jit(solution)/shard_map/all_gather | solution.py:96
Sparse Core Ops, SparseCore 0:
  30.0 35.0 all-gather.2
  69.1 83.7 reduce-scatter.1
  179.3 26.5 all-gather.4

commit v16 on v15

--- a/solution.py
+++ b/solution.py
@@ -43,7 +43,7 @@
     summed = lax.psum_scatter(
         partial.reshape(seq_n, branches * sub, length), "seq", scatter_dimension=0, tiled=True
     )
-    summed = summed.reshape(branches * sub, length).T.reshape(length, branches, sub)
+    summed = summed.reshape(branches, sub, length)
     projected = lax.reduce_precision(summed, exponent_bits=8, mantissa_bits=7)
 
     taps = lax.dynamic_slice_in_dim(short_taps, place * sub, sub, axis=2)
@@ -53,40 +53,40 @@
 
     rim_rows = taps_count - 1
     extended = jnp.concatenate(
-        [jnp.zeros((rim_rows, branches, sub), jnp.float32), projected], axis=0
+        [jnp.zeros((branches, sub, rim_rows), jnp.float32), projected], axis=2
     )
-    short = jnp.zeros((length, branches, sub), jnp.float32)
+    short = jnp.zeros((branches, sub, length), jnp.float32)
     for offset_lag in range(taps_count):
         short = (
             short
-            + taps[:, offset_lag, :][None]
-            * extended[rim_rows - offset_lag : rim_rows - offset_lag + length]
+            + taps[:, offset_lag, :][:, :, None]
+            * extended[:, :, rim_rows - offset_lag : rim_rows - offset_lag + length]
         )
-    product = short[:, 1, :] * short[:, 2, :]
+    product = short[1] * short[2]
     blocks = length // block_len
-    pieces = product.reshape(blocks, block_len, sub)
+    pieces = product.reshape(sub, blocks, block_len)
     amplitude = resid * jnp.sqrt(2.0 * decay)
     offsets = jnp.arange(block_len).astype(jnp.float32)
-    falloff = jnp.exp(-decay[:, None, :] * offsets[None, :, None])
-    kernel = jnp.einsum("mc,mtc->tc", amplitude, falloff, precision=precise)
+    falloff = jnp.exp(-decay[:, :, None] * offsets[None, None, :])
+    kernel = jnp.einsum("mc,mct->ct", amplitude, falloff, precision=precise)
     lag_grid = jnp.arange(block_len)[:, None] - jnp.arange(block_len)[None, :]
     select = (lag_grid[:, :, None] == jnp.arange(block_len)[None, None, :]).astype(jnp.float32)
-    toeplitz = jnp.einsum("tsk,kc->tsc", select, kernel, precision=precise)
-    inner = jnp.einsum("tsc,bsc->btc", toeplitz, pieces, precision=precise)
-    toward_end = jnp.exp(-decay[:, None, :] * (block_len - offsets)[None, :, None])
-    block_sums = jnp.einsum("msc,bsc->bmc", toward_end, pieces, precision=precise)
+    toeplitz = jnp.einsum("tsk,ck->cts", select, kernel, precision=precise)
+    inner = jnp.einsum("cts,cbs->cbt", toeplitz, pieces, precision=precise)
+    toward_end = jnp.exp(-decay[:, :, None] * (block_len - offsets)[None, None, :])
+    block_sums = jnp.einsum("mcs,cbs->mcb", toward_end, pieces, precision=precise)
     later = jnp.arange(blocks)[:, None]
     earlier = jnp.arange(blocks)[None, :]
     distance = jnp.maximum(later - 1 - earlier, 0).astype(jnp.float32)
     carry = jnp.where(
-        (earlier < later)[:, :, None, None],
-        jnp.exp(-decay[None, None] * (block_len * distance)[:, :, None, None]),
+        (earlier < later)[None, None],
+        jnp.exp(-decay[:, :, None, None] * (block_len * distance)[None, None]),
         0.0,
     )
-    starts = jnp.sum(carry * block_sums[None], axis=1)
-    outer = jnp.einsum("mic,bmc->bic", amplitude[:, None, :] * falloff, starts, precision=precise)
-    conv = (inner + outer).reshape(length, sub)
-    gated = (short[:, 0, :] * (conv + skip[None, :] * product)).astype(jnp.bfloat16)
+    starts = jnp.sum(carry * block_sums[:, :, None, :], axis=3)
+    outer = jnp.einsum("mct,mcb->cbt", amplitude[:, :, None] * falloff, starts, precision=precise)
+    conv = (inner + outer).reshape(sub, length)
+    gated = (short[0] * (conv + skip[:, None] * product)).astype(jnp.bfloat16).T
     outgoing = jnp.broadcast_to(
         gated.reshape(seq_n, 1, tok_rows, sub), (seq_n, outer_n, tok_rows, sub)
     ).reshape(seq_n * outer_n * tok_rows, sub)

time: 215 us -> 216 us (level)
  no operation moved by 1% of the time
where the time goes in v16:
time: 216 us; the launch traced here: 215 us
  waiting for transfers between devices  141 us (65%)
  blocking collectives  18.9 us (9%)
  starting transfers between devices  18.8 us (9%)
  matrix products  13.7 us (6%)
  between operations  13.3 us (6%)
  local copies, waits for them, and re-layouts  5.85 us (3%)
  other arithmetic  4.07 us (2%)
    reduce_scatter x1, waiting for transfers between devices, body(): lax.psum_scatter(partial.reshape(seq_n, branches * sub, length), 'seq', s...  78.2 us
    all_gather x1, waiting for transfers between devices, body(): gathered = lax.all_gather(pair, 'inner', axis=0, tiled=True)  33.7 us
    all_gather x1, waiting for transfers between devices, body(): whole = lax.all_gather(pair, 'inner', axis=1, tiled=True)  25 us
    all_to_all x1, blocking collectives, body(): incoming = lax.all_to_all(outgoing, ('seq', 'zhi'), 0, 0, tiled=True)  18.9 us
    ppermute x1, starting transfers between devices, body(): first = lax.ppermute(features, ('seq', 'zhi', 'inner'), routes[0])  16.8 us
  transfers between devices with their start and end apart: 5, of which 5 were waited for; matrix products, arithmetic and copies ran while one was open for 4% of the time, Pallas kernels for 0%

profile of v16, /device:TPU:1, one launch (start us, length us, event | category | flops | bytes accessed | tf_op | source)
XLA Modules:
  0.0 215.3 jit_solution(7890694241632446451)
XLA Ops:
  6.5 0.0 all-gather.3.cloned.1.call-start
  6.5 16.8 %collective-permute-start = (bf16[128,256]{1,0:T(8,128)(2,1)}, bf16[128,256]{1,0:T(8,128)(2,1)S(1)}, u32[]{:S(2)}, u32[]{:S(2)}) collective-permute-start(bf16[128,256]{1,0:T(8,128)(2,1)} %param.7), channel_id=1, source_target_pairs={{0,0},{1,8},{2,16},{3,24},{4,32},{5,40},{6,48},{7,56},{8,64},{9,72... | collective-permute-start | bytes 196616 | tf_op jit(solution)/shard_map/ppermute | solution.py:32
  23.4 1.9 collective-permute-start.1
  25.3 0.4 collective-permute-done
  25.7 3.4 %collective-permute-done.1 = bf16[128,256]{1,0:T(8,128)(2,1)S(1)} collective-permute-done((bf16[128,256]{1,0:T(8,128)(2,1)}, bf16[128,256]{1,0:T(8,128)(2,1)S(1)}, u32[]{:S(2)}, u32[]{:S(2)}) %collective-permute-start.1) | collective-permute-done | bytes 65568 | tf_op jit(solution)/shard_map/ppermute | solution.py:33
  29.1 0.7 pad_maximum_fusion
  29.8 0.0 all-gather.3.cloned.1.call-update
  29.8 0.0 reduce-scatter.2.cloned.1.call-start
  29.9 1.4 copy.26
  31.3 0.1 copy.27
  31.4 33.7 %all-gather.3.cloned.1.call-done = bf16[1024,512]{1,0:T(8,128)(2,1)} async-done(((bf16[128,512]{1,0:T(8,128)(2,1)}), bf16[1024,512]{1,0:T(8,128)(2,1)}) %all-gather.3.cloned.1.call-update) | async-done | bytes 1048592 | tf_op jit(solution)/shard_map/all_gather | solution.py:37
  65.1 3.9 %fusion.31 = f32[1024,768]{0,1} fusion(bf16[1024,512]{1,0:T(8,128)(2,1)} %all-gather.3.cloned.1.call-done, bf16[512,768]{0,1:T(8,128)(2,1)S(1)} %bitcast.75), kind=kOutput, calls=%fused_computation.72 | convolution fusion | flops 805306368 | bytes 4980736
  69.0 0.0 copy-start
  69.0 0.0 copy-start.1
  69.0 0.0 copy-start.2
  69.0 0.0 reduce-scatter.2.cloned.1.call-update
  69.0 0.0 all-gather.5.cloned.1.call-start
  69.0 1.1 constant_dynamic-slice_fusion.5
  70.1 0.0 copy-done
  70.1 0.0 copy-done.1
  70.1 0.1 dynamic-slice_negate_fusion
  70.2 0.1 copy.31
  70.3 0.1 copy.36
  70.4 0.1 copy.28
  70.5 0.0 copy-done.2
  70.5 0.1 dynamic_slice.15
  70.6 0.1 convert_multiply_fusion
  70.7 0.4 fusion.19
  71.1 3.6 %fusion = f32[32,64,64]{2,0,1:T(8,128)S(1)} fusion(f32[32,64,1]{1,0,2:T(8,128)S(1)} %bitcast.83, s32[64,64]{1,0:T(8,128)S(1)} %iota_subtract_fusion), kind=kOutput, calls=%fused_computation.2 | convolution fusion | flops 100925440 | bytes 548864 | tf_op jit(solution)/shard_map/tsk,ck->cts/dot_general | solution.py:74
  74.7 78.2 %reduce-scatter.2.cloned.1.call-done = f32[1,96,1024]{2,1,0:T(8,128)} async-done(((f32[8,96,1024]{2,1,0:T(8,128)}), f32[1,96,1024]{2,1,0:T(8,128)}) %reduce-scatter.2.cloned.1.call-update) | async-done | bytes 393232 | tf_op jit(solution)/shard_map/reduce_scatter | solution.py:43
  152.9 1.0 reduce_precision.6
  153.9 0.8 fusion.10
  154.7 0.1 mul.192
  154.8 2.2 %fusion.1 = f32[32,16,64]{2,1,0:T(8,128)S(1)} fusion(f32[32,16,64]{2,1,0:T(8,128)S(1)} %mul.192, f32[32,64,64]{2,0,1:T(8,128)S(1)} %fusion), kind=kOutput, calls=%fused_computation.6 | convolution fusion | flops 25165824 | bytes 786432 | tf_op jit(solution)/shard_map/cts,cbs->cbt/dot_general | solution.py:75
  157.1 0.6 convolution_bitcast_fusion
  157.7 0.2 copy.30
  157.9 1.3 multiply_reduce_fusion
  159.1 0.2 copy.32
  159.3 0.5 convolution_add_fusion
  159.8 0.1 reshape.109
  160.0 0.1 copy_bitcast_fusion
  160.1 18.9 %all_to_all.9 = bf16[16,128,32]{1,2,0:T(8,128)(2,1)S(1)} all-to-all(bf16[16,128,32]{1,2,0:T(8,128)(2,1)S(1)} %bitcast.80), channel_id=1, replica_groups=mesh['dp'=4,'seq'=8,'zhi'=2,'inner'=8] {'seq','zhi'}, dimensions={0} | all-to-all | bytes 262144 | tf_op jit(solution)/shard_map/all_to_all | solution.py:93
  179.0 0.7 copy.34
  179.6 0.0 all-gather.5.cloned.1.call-update
  179.6 1.7 copy.35
  181.4 25.0 %all-gather.5.cloned.1.call-done = bf16[128,4096]{0,1:T(8,128)(2,1)} async-done(((bf16[128,512]{0,1:T(8,128)(2,1)}), bf16[128,4096]{0,1:T(8,128)(2,1)}) %all-gather.5.cloned.1.call-update) | async-done | bytes 1048592 | tf_op jit(solution)/shard_map/all_gather | solution.py:96
  206.4 2.4 %convolution_convert_fusion = bf16[128,256]{1,0:T(8,128)(2,1)} fusion(bf16[128,4096]{0,1:T(8,128)(2,1)} %all-gather.5.cloned.1.call-done, bf16[4096,256]{1,0:T(8,128)(2,1)S(1)} %bitcast.74), kind=kOutput, calls=%fused_computation.5 | convolution fusion | flops 268468224 | bytes 3211264 | tf_op jit(solution)/shard_map/dot_general | solution.py:102
  (12 shorter events, 0.1 us)
Async XLA Ops:
  6.5 58.6 %all-gather.3.cloned.1.call-start = ((), (), s32[]{:S(2)}) async-start(), calls=%async_computation.2 | async-start | bytes 1179648 | tf_op jit(solution)/shard_map/all_gather | solution.py:37
  6.5 19.2 %collective-permute-start = (bf16[128,256]{1,0:T(8,128)(2,1)}, bf16[128,256]{1,0:T(8,128)(2,1)S(1)}, u32[]{:S(2)}, u32[]{:S(2)}) collective-permute-start(bf16[128,256]{1,0:T(8,128)(2,1)} %param.7), channel_id=1, source_target_pairs={{0,0},{1,8},{2,16},{3,24},{4,32},{5,40},{6,48},{7,56},{8,64},{9,72... | collective-permute-start | bytes 196616 | tf_op jit(solution)/shard_map/ppermute | solution.py:32
  23.4 5.8 %collective-permute-start.1 = (bf16[128,256]{1,0:T(8,128)(2,1)}, bf16[128,256]{1,0:T(8,128)(2,1)S(1)}, u32[]{:S(2)}, u32[]{:S(2)}) collective-permute-start(bf16[128,256]{1,0:T(8,128)(2,1)} %param.7), channel_id=1, source_target_pairs={{0,8},{1,0},{2,24},{3,16},{4,40},{5,32},{6,56},{7,48},{8,72},{9,64... | collective-permute-start | bytes 196616 | tf_op jit(solution)/shard_map/ppermute | solution.py:33
  29.8 123.0 %reduce-scatter.2.cloned.1.call-start = ((), (), s32[]{:S(2)}) async-start(), calls=%async_computation.3 | async-start | bytes 3538944 | tf_op jit(solution)/shard_map/reduce_scatter | solution.py:43
  69.0 1.2 copy-start
  69.0 1.2 copy-start.1
  69.0 1.5 copy-start.2
  69.0 137.4 %all-gather.5.cloned.1.call-start = ((), (), s32[]{:S(2)}) async-start(), calls=%async_computation.4 | async-start | bytes 1179648 | tf_op jit(solution)/shard_map/all_gather | solution.py:96
Sparse Core Ops, SparseCore 0:
  30.0 35.0 all-gather.2
  69.1 83.7 reduce-scatter.1
  179.8 26.5 all-gather.4

commit v17 on v16

--- a/solution.py
+++ b/solution.py
@@ -34,7 +34,7 @@
     col_lo = jnp.where(far == 0, first, second)
     col_hi = jnp.where(far == 0, second, first)
     pair = jnp.concatenate([col_lo, col_hi], axis=1)
-    gathered = lax.all_gather(pair, "inner", axis=0, tiled=True)
+    gathered = lax.all_to_all(jnp.tile(pair, (inner_n, 1)), "inner", 0, 0, tiled=True)
     rows_of_feats = gathered.reshape(length, rows_here)
     weight_rows = in_weight.reshape(rows_here, branches, seq_n, sub).transpose(0, 2, 1, 3)
     partial = jnp.einsum(

time: 216 us -> 203 us (0.940)
  waiting for transfers between devices: 141 us -> 117 us
  starting transfers between devices: 18.8 us -> 30.5 us
    all_gather x1 -> x0, waiting for transfers between devices: 33.7 us -> none  [body(): gathered = lax.all_gather(pair, 'inner', axis=0, tiled=True)]
    all_to_all x0 -> x1, waiting for transfers between devices: none -> 14.7 us  [body(): lax.all_to_all(jnp.tile(pair, (inner_n, 1)), 'inner', 0, 0, tiled=True)]
    all_to_all x0 -> x1, starting transfers between devices: none -> 11.6 us  [body(): lax.all_to_all(jnp.tile(pair, (inner_n, 1)), 'inner', 0, 0, tiled=True)]
    reduce_scatter x1, waiting for transfers between devices: 78.2 us -> 74 us  [body(): lax.psum_scatter(partial.reshape(seq_n, branches * sub, length), 'seq', s...]
where the time goes in v17:
time: 203 us; the launch traced here: 202 us
  waiting for transfers between devices  117 us (58%)
  starting transfers between devices  30.5 us (15%)
  blocking collectives  18.9 us (9%)
  between operations  13.6 us (7%)
  matrix products  12.4 us (6%)
  local copies, waits for them, and re-layouts  5.79 us (3%)
  other arithmetic  3.42 us (2%)
    reduce_scatter x1, waiting for transfers between devices, body(): lax.psum_scatter(partial.reshape(seq_n, branches * sub, length), 'seq', s...  74 us
    all_gather x1, waiting for transfers between devices, body(): whole = lax.all_gather(pair, 'inner', axis=1, tiled=True)  24.9 us
    all_to_all x1, blocking collectives, body(): incoming = lax.all_to_all(outgoing, ('seq', 'zhi'), 0, 0, tiled=True)  18.9 us
    ppermute x1, starting transfers between devices, body(): first = lax.ppermute(features, ('seq', 'zhi', 'inner'), routes[0])  17 us
    all_to_all x1, waiting for transfers between devices, body(): lax.all_to_all(jnp.tile(pair, (inner_n, 1)), 'inner', 0, 0, tiled=True)  14.7 us
    all_to_all x1, starting transfers between devices, body(): lax.all_to_all(jnp.tile(pair, (inner_n, 1)), 'inner', 0, 0, tiled=True)  11.6 us
  transfers between devices with their start and end apart: 5, of which 5 were waited for; matrix products, arithmetic and copies ran while one was open for 4% of the time, Pallas kernels for 0%

profile of v17, /device:TPU:1, one launch (start us, length us, event | category | flops | bytes accessed | tf_op | source)
XLA Modules:
  0.0 202.1 jit_solution(540886353213286925)
XLA Ops:
  6.5 0.0 copy-start
  6.5 17.0 %collective-permute-start = (bf16[128,256]{1,0:T(8,128)(2,1)}, bf16[128,256]{1,0:T(8,128)(2,1)S(1)}, u32[]{:S(2)}, u32[]{:S(2)}) collective-permute-start(bf16[128,256]{1,0:T(8,128)(2,1)} %param.7), channel_id=1, source_target_pairs={{0,0},{1,8},{2,16},{3,24},{4,32},{5,40},{6,48},{7,56},{8,64},{9,72... | collective-permute-start | bytes 196616 | tf_op jit(solution)/shard_map/ppermute | solution.py:32
  23.5 1.9 collective-permute-start.1
  25.4 0.4 collective-permute-done
  25.8 3.4 %collective-permute-done.1 = bf16[128,256]{1,0:T(8,128)(2,1)S(1)} collective-permute-done((bf16[128,256]{1,0:T(8,128)(2,1)}, bf16[128,256]{1,0:T(8,128)(2,1)S(1)}, u32[]{:S(2)}, u32[]{:S(2)}) %collective-permute-start.1) | collective-permute-done | bytes 65568 | tf_op jit(solution)/shard_map/ppermute | solution.py:33
  29.3 1.1 tile.2
  30.4 11.6 %all-to-all-start = ((bf16[8,128,512]{2,1,0:T(8,128)(2,1)}), bf16[8,128,512]{2,1,0:T(8,128)(2,1)S(1)}, u32[]{:S(2)}, u32[]{:S(2)}) async-start(bf16[8,128,512]{2,1,0:T(8,128)(2,1)} %tile.2), calls=%async_computation | async-start | bytes 2097152 | tf_op jit(solution)/shard_map/all_to_all | solution.py:37
  42.0 0.0 reduce-scatter.2.cloned.1.call-start
  42.0 0.0 copy-done
  42.0 0.3 copy.26
  42.3 0.1 copy.27
  42.3 14.7 %all-to-all-done = bf16[8,128,512]{2,1,0:T(8,128)(2,1)S(1)} async-done(((bf16[8,128,512]{2,1,0:T(8,128)(2,1)}), bf16[8,128,512]{2,1,0:T(8,128)(2,1)S(1)}, u32[]{:S(2)}, u32[]{:S(2)}) %all-to-all-start) | async-done | bytes 1048608 | tf_op jit(solution)/shard_map/all_to_all | solution.py:37
  57.1 2.6 %fusion.31 = f32[1024,768]{0,1} fusion(bf16[1024,512]{1,0:T(8,128)(2,1)S(1)} %bitcast.76, bf16[512,768]{0,1:T(8,128)(2,1)S(1)} %bitcast.77), kind=kOutput, calls=%fused_computation.72 | convolution fusion | flops 805306368 | bytes 4980736
  59.7 0.0 copy-start.1
  59.7 0.0 copy-start.2
  59.7 0.0 copy-start.3
  59.7 0.0 reduce-scatter.2.cloned.1.call-update
  59.7 0.0 all-gather.2.cloned.1.call-start
  59.8 1.1 constant_dynamic-slice_fusion.5
  60.9 0.0 copy-done.1
  60.9 0.0 copy-done.2
  60.9 0.1 dynamic-slice_negate_fusion
  61.0 0.1 copy.31
  61.1 0.1 copy.36
  61.1 0.1 copy.28
  61.2 0.0 copy-done.3
  61.2 0.1 dynamic_slice.15
  61.4 0.1 convert_multiply_fusion
  61.4 0.4 fusion.19
  61.9 3.6 %fusion = f32[32,64,64]{2,0,1:T(8,128)S(1)} fusion(f32[32,64,1]{1,0,2:T(8,128)S(1)} %bitcast.85, s32[64,64]{1,0:T(8,128)S(1)} %iota_subtract_fusion), kind=kOutput, calls=%fused_computation.2 | convolution fusion | flops 100925440 | bytes 548864 | tf_op jit(solution)/shard_map/tsk,ck->cts/dot_general | solution.py:74
  65.5 74.0 %reduce-scatter.2.cloned.1.call-done = f32[1,96,1024]{2,1,0:T(8,128)} async-done(((f32[8,96,1024]{2,1,0:T(8,128)}), f32[1,96,1024]{2,1,0:T(8,128)}) %reduce-scatter.2.cloned.1.call-update) | async-done | bytes 393232 | tf_op jit(solution)/shard_map/reduce_scatter | solution.py:43
  139.4 1.0 reduce_precision.6
  140.5 0.8 fusion.10
  141.3 0.1 mul.192
  141.4 2.2 %fusion.1 = f32[32,16,64]{2,1,0:T(8,128)S(1)} fusion(f32[32,16,64]{2,1,0:T(8,128)S(1)} %mul.192, f32[32,64,64]{2,0,1:T(8,128)S(1)} %fusion), kind=kOutput, calls=%fused_computation.6 | convolution fusion | flops 25165824 | bytes 786432 | tf_op jit(solution)/shard_map/cts,cbs->cbt/dot_general | solution.py:75
  143.6 0.6 convolution_bitcast_fusion
  144.2 0.2 copy.30
  144.4 1.3 multiply_reduce_fusion
  145.7 0.2 copy.32
  145.9 0.5 convolution_add_fusion
  146.4 0.1 reshape.116
  146.5 0.1 copy_bitcast_fusion
  146.6 18.9 %all_to_all.18 = bf16[16,128,32]{1,2,0:T(8,128)(2,1)S(1)} all-to-all(bf16[16,128,32]{1,2,0:T(8,128)(2,1)S(1)} %bitcast.82), channel_id=1, replica_groups=mesh['dp'=4,'seq'=8,'zhi'=2,'inner'=8] {'seq','zhi'}, dimensions={0} | all-to-all | bytes 262144 | tf_op jit(solution)/shard_map/all_to_all | solution.py:93
  165.5 0.7 copy.34
  166.2 0.0 all-gather.2.cloned.1.call-update
  166.2 1.7 copy.35
  167.9 24.9 %all-gather.2.cloned.1.call-done = bf16[128,4096]{0,1:T(8,128)(2,1)} async-done(((bf16[128,512]{0,1:T(8,128)(2,1)}), bf16[128,4096]{0,1:T(8,128)(2,1)}) %all-gather.2.cloned.1.call-update) | async-done | bytes 1048592 | tf_op jit(solution)/shard_map/all_gather | solution.py:96
  192.9 2.4 %convolution_convert_fusion = bf16[128,256]{1,0:T(8,128)(2,1)} fusion(bf16[128,4096]{0,1:T(8,128)(2,1)} %all-gather.2.cloned.1.call-done, bf16[4096,256]{1,0:T(8,128)(2,1)S(1)} %bitcast.75), kind=kOutput, calls=%fused_computation.5 | convolution fusion | flops 268468224 | bytes 3211264 | tf_op jit(solution)/shard_map/dot_general | solution.py:102
  (13 shorter events, 0.1 us)
Async XLA Ops:
  6.5 35.4 %copy-start = (bf16[512,3,256]{2,0,1:T(8,128)(2,1)S(1)}, bf16[512,3,256]{2,0,1:T(8,128)(2,1)}, u32[]{:S(2)}) copy-start(bf16[512,3,256]{2,0,1:T(8,128)(2,1)} %param.8) | copy-start | bytes 2359300
  6.5 19.3 %collective-permute-start = (bf16[128,256]{1,0:T(8,128)(2,1)}, bf16[128,256]{1,0:T(8,128)(2,1)S(1)}, u32[]{:S(2)}, u32[]{:S(2)}) collective-permute-start(bf16[128,256]{1,0:T(8,128)(2,1)} %param.7), channel_id=1, source_target_pairs={{0,0},{1,8},{2,16},{3,24},{4,32},{5,40},{6,48},{7,56},{8,64},{9,72... | collective-permute-start | bytes 196616 | tf_op jit(solution)/shard_map/ppermute | solution.py:32
  23.5 5.8 %collective-permute-start.1 = (bf16[128,256]{1,0:T(8,128)(2,1)}, bf16[128,256]{1,0:T(8,128)(2,1)S(1)}, u32[]{:S(2)}, u32[]{:S(2)}) collective-permute-start(bf16[128,256]{1,0:T(8,128)(2,1)} %param.7), channel_id=1, source_target_pairs={{0,8},{1,0},{2,24},{3,16},{4,40},{5,32},{6,56},{7,48},{8,72},{9,64... | collective-permute-start | bytes 196616 | tf_op jit(solution)/shard_map/ppermute | solution.py:33
  30.4 26.7 %all-to-all-start = ((bf16[8,128,512]{2,1,0:T(8,128)(2,1)}), bf16[8,128,512]{2,1,0:T(8,128)(2,1)S(1)}, u32[]{:S(2)}, u32[]{:S(2)}) async-start(bf16[8,128,512]{2,1,0:T(8,128)(2,1)} %tile.2), calls=%async_computation | async-start | bytes 2097152 | tf_op jit(solution)/shard_map/all_to_all | solution.py:37
  42.0 97.5 %reduce-scatter.2.cloned.1.call-start = ((), (), s32[]{:S(2)}) async-start(), calls=%async_computation.3 | async-start | bytes 3538944 | tf_op jit(solution)/shard_map/reduce_scatter | solution.py:43
  59.7 1.2 copy-start.1
  59.7 1.2 copy-start.2
  59.7 1.5 copy-start.3
  59.7 133.1 %all-gather.2.cloned.1.call-start = ((), (), s32[]{:S(2)}) async-start(), calls=%async_computation.4 | async-start | bytes 1179648 | tf_op jit(solution)/shard_map/all_gather | solution.py:96
Sparse Core Ops, SparseCore 0:
  59.9 79.5 reduce-scatter.1
  166.3 26.4 all-gather.1

commit v18 on v17

--- a/solution.py
+++ b/solution.py
@@ -93,7 +93,7 @@
     incoming = lax.all_to_all(outgoing, ("seq", "zhi"), 0, 0, tiled=True)
     pair = incoming.reshape(seq_n, outer_n, tok_rows, sub).transpose(2, 1, 0, 3)
     pair = pair.reshape(tok_rows, outer_n * seq_n * sub)
-    whole = lax.all_gather(pair, "inner", axis=1, tiled=True)
+    whole = lax.all_to_all(jnp.tile(pair, (inner_n, 1)), "inner", 0, 1, tiled=True)
     weight_out = (
         out_weight.reshape(outer_n, inner_n, channels, -1)
         .transpose(1, 0, 2, 3)

time: 203 us -> 198 us (0.975)
  waiting for transfers between devices: 117 us -> 106 us
  starting transfers between devices: 30.5 us -> 38.2 us
    all_gather x1 -> x0, waiting for transfers between devices: 24.9 us -> none  [body(): whole = lax.all_gather(pair, 'inner', axis=1, tiled=True)]
    all_to_all x0 -> x1, waiting for transfers between devices: none -> 13.4 us  [body(): lax.all_to_all(jnp.tile(pair, (inner_n, 1)), 'inner', 0, 1, tiled=True)]
    all_to_all x0 -> x1, starting transfers between devices: none -> 7.69 us  [body(): lax.all_to_all(jnp.tile(pair, (inner_n, 1)), 'inner', 0, 1, tiled=True)]
where the time goes in v18:
time: 198 us; the launch traced here: 197 us
  waiting for transfers between devices  106 us (54%)
  starting transfers between devices  38.2 us (19%)
  blocking collectives  18.9 us (10%)
  between operations  13.6 us (7%)
  matrix products  11.2 us (6%)
  local copies, waits for them, and re-layouts  6.24 us (3%)
  other arithmetic  3.42 us (2%)
    reduce_scatter x1, waiting for transfers between devices, body(): lax.psum_scatter(partial.reshape(seq_n, branches * sub, length), 'seq', s...  74 us
    all_to_all x1, blocking collectives, body(): incoming = lax.all_to_all(outgoing, ('seq', 'zhi'), 0, 0, tiled=True)  18.9 us
    ppermute x1, starting transfers between devices, body(): first = lax.ppermute(features, ('seq', 'zhi', 'inner'), routes[0])  17 us
    all_to_all x1, waiting for transfers between devices, body(): lax.all_to_all(jnp.tile(pair, (inner_n, 1)), 'inner', 0, 0, tiled=True)  14.7 us
    all_to_all x1, waiting for transfers between devices, body(): lax.all_to_all(jnp.tile(pair, (inner_n, 1)), 'inner', 0, 1, tiled=True)  13.4 us
    all_to_all x1, starting transfers between devices, body(): lax.all_to_all(jnp.tile(pair, (inner_n, 1)), 'inner', 0, 0, tiled=True)  11.6 us
    all_to_all x1, starting transfers between devices, body(): lax.all_to_all(jnp.tile(pair, (inner_n, 1)), 'inner', 0, 1, tiled=True)  7.69 us
  transfers between devices with their start and end apart: 5, of which 5 were waited for; matrix products, arithmetic and copies ran while one was open for 4% of the time, Pallas kernels for 0%

profile of v18, /device:TPU:1, one launch (start us, length us, event | category | flops | bytes accessed | tf_op | source)
XLA Modules:
  0.0 197.5 jit_solution(10983550434746402909)
XLA Ops:
  6.5 0.0 copy-start
  6.5 17.0 %collective-permute-start = (bf16[128,256]{1,0:T(8,128)(2,1)}, bf16[128,256]{1,0:T(8,128)(2,1)S(1)}, u32[]{:S(2)}, u32[]{:S(2)}) collective-permute-start(bf16[128,256]{1,0:T(8,128)(2,1)} %param.7), channel_id=1, source_target_pairs={{0,0},{1,8},{2,16},{3,24},{4,32},{5,40},{6,48},{7,56},{8,64},{9,72... | collective-permute-start | bytes 196616 | tf_op jit(solution)/shard_map/ppermute | solution.py:32
  23.5 1.9 collective-permute-start.1
  25.4 0.4 collective-permute-done
  25.8 3.4 %collective-permute-done.1 = bf16[128,256]{1,0:T(8,128)(2,1)S(1)} collective-permute-done((bf16[128,256]{1,0:T(8,128)(2,1)}, bf16[128,256]{1,0:T(8,128)(2,1)S(1)}, u32[]{:S(2)}, u32[]{:S(2)}) %collective-permute-start.1) | collective-permute-done | bytes 65568 | tf_op jit(solution)/shard_map/ppermute | solution.py:33
  29.3 1.1 tile.6
  30.4 11.6 %all-to-all-start = ((bf16[8,128,512]{2,1,0:T(8,128)(2,1)}), bf16[8,128,512]{2,1,0:T(8,128)(2,1)S(1)}, u32[]{:S(2)}, u32[]{:S(2)}) async-start(bf16[8,128,512]{2,1,0:T(8,128)(2,1)} %tile.6), calls=%async_computation | async-start | bytes 2097152 | tf_op jit(solution)/shard_map/all_to_all | solution.py:37
  42.0 0.0 reduce-scatter.2.cloned.1.call-start
  42.0 0.0 copy-done
  42.0 0.3 copy.26
  42.3 0.1 copy.27
  42.3 14.7 %all-to-all-done = bf16[8,128,512]{2,1,0:T(8,128)(2,1)S(1)} async-done(((bf16[8,128,512]{2,1,0:T(8,128)(2,1)}), bf16[8,128,512]{2,1,0:T(8,128)(2,1)S(1)}, u32[]{:S(2)}, u32[]{:S(2)}) %all-to-all-start) | async-done | bytes 1048608 | tf_op jit(solution)/shard_map/all_to_all | solution.py:37
  57.1 2.6 %fusion.31 = f32[1024,768]{0,1} fusion(bf16[1024,512]{1,0:T(8,128)(2,1)S(1)} %bitcast.79, bf16[512,768]{0,1:T(8,128)(2,1)S(1)} %bitcast.81), kind=kOutput, calls=%fused_computation.72 | convolution fusion | flops 805306368 | bytes 4980736
  59.7 0.0 copy-start.1
  59.7 0.0 copy-start.2
  59.7 0.0 copy-start.3
  59.7 0.0 reduce-scatter.2.cloned.1.call-update
  59.7 1.1 constant_dynamic-slice_fusion.5
  60.8 0.0 copy-done.1
  60.8 0.0 copy-done.2
  60.8 0.1 dynamic-slice_negate_fusion
  60.9 0.1 copy.31
  61.0 0.1 copy.36
  61.1 0.1 copy.28
  61.1 0.0 copy-done.3
  61.2 0.1 dynamic_slice.15
  61.3 0.1 convert_multiply_fusion
  61.4 0.4 fusion.19
  61.8 3.6 %fusion = f32[32,64,64]{2,0,1:T(8,128)S(1)} fusion(f32[32,64,1]{1,0,2:T(8,128)S(1)} %bitcast.89, s32[64,64]{1,0:T(8,128)S(1)} %iota_subtract_fusion), kind=kOutput, calls=%fused_computation.2 | convolution fusion | flops 100925440 | bytes 548864 | tf_op jit(solution)/shard_map/tsk,ck->cts/dot_general | solution.py:74
  65.4 74.0 %reduce-scatter.2.cloned.1.call-done = f32[1,96,1024]{2,1,0:T(8,128)} async-done(((f32[8,96,1024]{2,1,0:T(8,128)}), f32[1,96,1024]{2,1,0:T(8,128)}) %reduce-scatter.2.cloned.1.call-update) | async-done | bytes 393232 | tf_op jit(solution)/shard_map/reduce_scatter | solution.py:43
  139.4 1.0 reduce_precision.6
  140.5 0.8 fusion.10
  141.3 0.1 mul.192
  141.4 2.2 %fusion.1 = f32[32,16,64]{2,1,0:T(8,128)S(1)} fusion(f32[32,16,64]{2,1,0:T(8,128)S(1)} %mul.192, f32[32,64,64]{2,0,1:T(8,128)S(1)} %fusion), kind=kOutput, calls=%fused_computation.6 | convolution fusion | flops 25165824 | bytes 786432 | tf_op jit(solution)/shard_map/cts,cbs->cbt/dot_general | solution.py:75
  143.6 0.6 convolution_bitcast_fusion
  144.2 0.2 copy.30
  144.4 1.3 multiply_reduce_fusion
  145.7 0.2 copy.32
  145.9 0.5 convolution_add_fusion
  146.4 0.1 reshape.121
  146.5 0.1 copy_bitcast_fusion
  146.6 18.9 %all_to_all.34 = bf16[16,128,32]{1,2,0:T(8,128)(2,1)S(1)} all-to-all(bf16[16,128,32]{1,2,0:T(8,128)(2,1)S(1)} %bitcast.86), channel_id=1, replica_groups=mesh['dp'=4,'seq'=8,'zhi'=2,'inner'=8] {'seq','zhi'}, dimensions={0} | all-to-all | bytes 262144 | tf_op jit(solution)/shard_map/all_to_all | solution.py:93
  165.5 1.1 tile.8
  166.6 7.7 %all-to-all-start.2 = ((bf16[8,128,512]{1,2,0:T(8,128)(2,1)}), bf16[8,128,512]{1,2,0:T(8,128)(2,1)S(1)}, u32[]{:S(2)}, u32[]{:S(2)}) async-start(bf16[8,128,512]{1,2,0:T(8,128)(2,1)} %tile.8), calls=%async_computation.3 | async-start | bytes 2097152 | tf_op jit(solution)/shard_map/all_to_all | solution.py:96
  174.3 1.7 copy.35
  176.1 13.4 %all-to-all-done.2 = bf16[8,128,512]{1,2,0:T(8,128)(2,1)S(1)} async-done(((bf16[8,128,512]{1,2,0:T(8,128)(2,1)}), bf16[8,128,512]{1,2,0:T(8,128)(2,1)S(1)}, u32[]{:S(2)}, u32[]{:S(2)}) %all-to-all-start.2) | async-done | bytes 1048608 | tf_op jit(solution)/shard_map/all_to_all | solution.py:96
  189.4 1.2 convolution_convert_fusion
  (14 shorter events, 0.1 us)
Async XLA Ops:
  6.5 35.4 %copy-start = (bf16[512,3,256]{2,0,1:T(8,128)(2,1)S(1)}, bf16[512,3,256]{2,0,1:T(8,128)(2,1)}, u32[]{:S(2)}) copy-start(bf16[512,3,256]{2,0,1:T(8,128)(2,1)} %param.8) | copy-start | bytes 2359300
  6.5 19.3 %collective-permute-start = (bf16[128,256]{1,0:T(8,128)(2,1)}, bf16[128,256]{1,0:T(8,128)(2,1)S(1)}, u32[]{:S(2)}, u32[]{:S(2)}) collective-permute-start(bf16[128,256]{1,0:T(8,128)(2,1)} %param.7), channel_id=1, source_target_pairs={{0,0},{1,8},{2,16},{3,24},{4,32},{5,40},{6,48},{7,56},{8,64},{9,72... | collective-permute-start | bytes 196616 | tf_op jit(solution)/shard_map/ppermute | solution.py:32
  23.5 5.8 %collective-permute-start.1 = (bf16[128,256]{1,0:T(8,128)(2,1)}, bf16[128,256]{1,0:T(8,128)(2,1)S(1)}, u32[]{:S(2)}, u32[]{:S(2)}) collective-permute-start(bf16[128,256]{1,0:T(8,128)(2,1)} %param.7), channel_id=1, source_target_pairs={{0,8},{1,0},{2,24},{3,16},{4,40},{5,32},{6,56},{7,48},{8,72},{9,64... | collective-permute-start | bytes 196616 | tf_op jit(solution)/shard_map/ppermute | solution.py:33
  30.4 26.7 %all-to-all-start = ((bf16[8,128,512]{2,1,0:T(8,128)(2,1)}), bf16[8,128,512]{2,1,0:T(8,128)(2,1)S(1)}, u32[]{:S(2)}, u32[]{:S(2)}) async-start(bf16[8,128,512]{2,1,0:T(8,128)(2,1)} %tile.6), calls=%async_computation | async-start | bytes 2097152 | tf_op jit(solution)/shard_map/all_to_all | solution.py:37
  42.0 97.5 %reduce-scatter.2.cloned.1.call-start = ((), (), s32[]{:S(2)}) async-start(), calls=%async_computation.4 | async-start | bytes 3538944 | tf_op jit(solution)/shard_map/reduce_scatter | solution.py:43
  59.7 1.1 copy-start.1
  59.7 1.1 copy-start.2
  59.7 1.4 copy-start.3
  166.6 22.8 %all-to-all-start.2 = ((bf16[8,128,512]{1,2,0:T(8,128)(2,1)}), bf16[8,128,512]{1,2,0:T(8,128)(2,1)S(1)}, u32[]{:S(2)}, u32[]{:S(2)}) async-start(bf16[8,128,512]{1,2,0:T(8,128)(2,1)} %tile.8), calls=%async_computation.3 | async-start | bytes 2097152 | tf_op jit(solution)/shard_map/all_to_all | solution.py:96
Sparse Core Ops, SparseCore 0:
  59.9 79.5 reduce-scatter.1

commit v19 on v18

--- a/solution.py
+++ b/solution.py
@@ -44,7 +44,7 @@
         partial.reshape(seq_n, branches * sub, length), "seq", scatter_dimension=0, tiled=True
     )
     summed = summed.reshape(branches, sub, length)
-    projected = lax.reduce_precision(summed, exponent_bits=8, mantissa_bits=7)
+    projected = summed
 
     taps = lax.dynamic_slice_in_dim(short_taps, place * sub, sub, axis=2)
     decay = lax.dynamic_slice_in_dim(decay_rates, place * sub, sub, axis=1)
@@ -52,8 +52,10 @@
     skip = lax.dynamic_slice_in_dim(skip_gain, place * sub, sub, axis=0)
 
     rim_rows = taps_count - 1
-    extended = jnp.concatenate(
-        [jnp.zeros((branches, sub, rim_rows), jnp.float32), projected], axis=2
+    extended = lax.reduce_precision(
+        jnp.concatenate([jnp.zeros((branches, sub, rim_rows), jnp.float32), projected], axis=2),
+        exponent_bits=8,
+        mantissa_bits=7,
     )
     short = jnp.zeros((branches, sub, length), jnp.float32)
     for offset_lag in range(taps_count):

time: 198 us -> 199 us (level)
  no operation moved by 1% of the time
where the time goes in v19:
time: 199 us; the launch traced here: 198 us
  waiting for transfers between devices  106 us (53%)
  starting transfers between devices  38.1 us (19%)
  blocking collectives  18.9 us (9%)
  between operations  13.6 us (7%)
  matrix products  11.2 us (6%)
  local copies, waits for them, and re-layouts  6.24 us (3%)
  other arithmetic  4.36 us (2%)
    reduce_scatter x1, waiting for transfers between devices, body(): lax.psum_scatter(partial.reshape(seq_n, branches * sub, length), 'seq', s...  74 us
    all_to_all x1, blocking collectives, body(): incoming = lax.all_to_all(outgoing, ('seq', 'zhi'), 0, 0, tiled=True)  18.9 us
    ppermute x1, starting transfers between devices, body(): first = lax.ppermute(features, ('seq', 'zhi', 'inner'), routes[0])  17 us
    all_to_all x1, waiting for transfers between devices, body(): lax.all_to_all(jnp.tile(pair, (inner_n, 1)), 'inner', 0, 0, tiled=True)  14.7 us
    all_to_all x1, waiting for transfers between devices, body(): lax.all_to_all(jnp.tile(pair, (inner_n, 1)), 'inner', 0, 1, tiled=True)  13.4 us
    all_to_all x1, starting transfers between devices, body(): lax.all_to_all(jnp.tile(pair, (inner_n, 1)), 'inner', 0, 0, tiled=True)  11.6 us
    all_to_all x1, starting transfers between devices, body(): lax.all_to_all(jnp.tile(pair, (inner_n, 1)), 'inner', 0, 1, tiled=True)  7.68 us
  transfers between devices with their start and end apart: 5, of which 5 were waited for; matrix products, arithmetic and copies ran while one was open for 4% of the time, Pallas kernels for 0%

profile of v19, /device:TPU:1, one launch (start us, length us, event | category | flops | bytes accessed | tf_op | source)
XLA Modules:
  0.0 198.4 jit_solution(156880347162449946)
XLA Ops:
  6.5 0.0 copy-start
  6.5 17.0 %collective-permute-start = (bf16[128,256]{1,0:T(8,128)(2,1)}, bf16[128,256]{1,0:T(8,128)(2,1)S(1)}, u32[]{:S(2)}, u32[]{:S(2)}) collective-permute-start(bf16[128,256]{1,0:T(8,128)(2,1)} %param.7), channel_id=1, source_target_pairs={{0,0},{1,8},{2,16},{3,24},{4,32},{5,40},{6,48},{7,56},{8,64},{9,72... | collective-permute-start | bytes 196616 | tf_op jit(solution)/shard_map/ppermute | solution.py:32
  23.5 1.9 collective-permute-start.1
  25.4 0.4 collective-permute-done
  25.8 3.4 %collective-permute-done.1 = bf16[128,256]{1,0:T(8,128)(2,1)S(1)} collective-permute-done((bf16[128,256]{1,0:T(8,128)(2,1)}, bf16[128,256]{1,0:T(8,128)(2,1)S(1)}, u32[]{:S(2)}, u32[]{:S(2)}) %collective-permute-start.1) | collective-permute-done | bytes 65568 | tf_op jit(solution)/shard_map/ppermute | solution.py:33
  29.3 1.1 tile.6
  30.4 11.6 %all-to-all-start = ((bf16[8,128,512]{2,1,0:T(8,128)(2,1)}), bf16[8,128,512]{2,1,0:T(8,128)(2,1)S(1)}, u32[]{:S(2)}, u32[]{:S(2)}) async-start(bf16[8,128,512]{2,1,0:T(8,128)(2,1)} %tile.6), calls=%async_computation | async-start | bytes 2097152 | tf_op jit(solution)/shard_map/all_to_all | solution.py:37
  42.0 0.0 reduce-scatter.2.cloned.1.call-start
  42.0 0.0 copy-done
  42.0 0.3 copy.26
  42.3 0.1 copy.27
  42.3 14.7 %all-to-all-done = bf16[8,128,512]{2,1,0:T(8,128)(2,1)S(1)} async-done(((bf16[8,128,512]{2,1,0:T(8,128)(2,1)}), bf16[8,128,512]{2,1,0:T(8,128)(2,1)S(1)}, u32[]{:S(2)}, u32[]{:S(2)}) %all-to-all-start) | async-done | bytes 1048608 | tf_op jit(solution)/shard_map/all_to_all | solution.py:37
  57.1 2.6 %fusion.38 = f32[1024,768]{0,1} fusion(bf16[1024,512]{1,0:T(8,128)(2,1)S(1)} %bitcast.79, bf16[512,768]{0,1:T(8,128)(2,1)S(1)} %bitcast.81), kind=kOutput, calls=%fused_computation.80 | convolution fusion | flops 805306368 | bytes 4980736
  59.7 0.0 copy-start.1
  59.7 0.0 copy-start.2
  59.7 0.0 copy-start.3
  59.7 0.0 reduce-scatter.2.cloned.1.call-update
  59.7 1.1 constant_dynamic-slice_fusion.5
  60.8 0.0 copy-done.1
  60.8 0.0 copy-done.2
  60.8 0.1 dynamic-slice_negate_fusion
  60.9 0.1 copy.31
  61.0 0.1 copy.36
  61.1 0.1 copy.28
  61.1 0.0 copy-done.3
  61.2 0.1 dynamic_slice.15
  61.3 0.1 convert_multiply_fusion
  61.4 0.4 fusion.26
  61.8 3.6 %fusion = f32[32,64,64]{2,0,1:T(8,128)S(1)} fusion(f32[32,64,1]{1,0,2:T(8,128)S(1)} %bitcast.89, s32[64,64]{1,0:T(8,128)S(1)} %iota_subtract_fusion), kind=kOutput, calls=%fused_computation.2 | convolution fusion | flops 100925440 | bytes 548864 | tf_op jit(solution)/shard_map/tsk,ck->cts/dot_general | solution.py:76
  65.4 74.0 %reduce-scatter.2.cloned.1.call-done = f32[1,96,1024]{2,1,0:T(8,128)} async-done(((f32[8,96,1024]{2,1,0:T(8,128)}), f32[1,96,1024]{2,1,0:T(8,128)}) %reduce-scatter.2.cloned.1.call-update) | async-done | bytes 393232 | tf_op jit(solution)/shard_map/reduce_scatter | solution.py:43
  139.4 2.8 %fusion.7 = f32[3,32,1024]{2,1,0:T(8,128)S(1)} fusion(f32[3,32,1024]{2,1,0:T(8,128)} %bitcast.87, f32[3,32]{1,0:T(4,128)S(1)} %get-tuple-element.16, f32[3,32]{1,0:T(4,128)S(1)} %get-tuple-element.17, f32[3,32]{1,0:T(4,128)S(1)} %get-tuple-element.18, f32[3,32]{1,0:T(4,128)S(1)} %get-tuple-element.19, f32[3,32]{1,0:T(4,128)S(1)} %get-tuple-element.20, ...), kind=kLoop, calls=%fused_computation.18 | loop fusion | flops 1966080 | bytes 789120 | tf_op jit(solution)/shard_map/add | solution.py:63
  142.2 0.1 mul.192
  142.3 2.2 %fusion.1 = f32[32,16,64]{2,1,0:T(8,128)S(1)} fusion(f32[32,16,64]{2,1,0:T(8,128)S(1)} %mul.192, f32[32,64,64]{2,0,1:T(8,128)S(1)} %fusion), kind=kOutput, calls=%fused_computation.6 | convolution fusion | flops 25165824 | bytes 786432 | tf_op jit(solution)/shard_map/cts,cbs->cbt/dot_general | solution.py:77
  144.5 0.6 convolution_bitcast_fusion
  145.2 0.2 copy.30
  145.3 1.3 multiply_reduce_fusion
  146.6 0.2 copy.32
  146.8 0.5 convolution_add_fusion
  147.3 0.1 reshape.123
  147.4 0.1 copy_bitcast_fusion
  147.6 18.9 %all_to_all.34 = bf16[16,128,32]{1,2,0:T(8,128)(2,1)S(1)} all-to-all(bf16[16,128,32]{1,2,0:T(8,128)(2,1)S(1)} %bitcast.85), channel_id=1, replica_groups=mesh['dp'=4,'seq'=8,'zhi'=2,'inner'=8] {'seq','zhi'}, dimensions={0} | all-to-all | bytes 262144 | tf_op jit(solution)/shard_map/all_to_all | solution.py:95
  166.5 1.1 tile.8
  167.6 7.7 %all-to-all-start.2 = ((bf16[8,128,512]{1,2,0:T(8,128)(2,1)}), bf16[8,128,512]{1,2,0:T(8,128)(2,1)S(1)}, u32[]{:S(2)}, u32[]{:S(2)}) async-start(bf16[8,128,512]{1,2,0:T(8,128)(2,1)} %tile.8), calls=%async_computation.3 | async-start | bytes 2097152 | tf_op jit(solution)/shard_map/all_to_all | solution.py:98
  175.3 1.7 copy.35
  177.0 13.4 %all-to-all-done.2 = bf16[8,128,512]{1,2,0:T(8,128)(2,1)S(1)} async-done(((bf16[8,128,512]{1,2,0:T(8,128)(2,1)}), bf16[8,128,512]{1,2,0:T(8,128)(2,1)S(1)}, u32[]{:S(2)}, u32[]{:S(2)}) %all-to-all-start.2) | async-done | bytes 1048608 | tf_op jit(solution)/shard_map/all_to_all | solution.py:98
  190.4 1.2 convolution_convert_fusion
  (14 shorter events, 0.1 us)
Async XLA Ops:
  6.5 35.4 %copy-start = (bf16[512,3,256]{2,0,1:T(8,128)(2,1)S(1)}, bf16[512,3,256]{2,0,1:T(8,128)(2,1)}, u32[]{:S(2)}) copy-start(bf16[512,3,256]{2,0,1:T(8,128)(2,1)} %param.8) | copy-start | bytes 2359300
  6.5 19.3 %collective-permute-start = (bf16[128,256]{1,0:T(8,128)(2,1)}, bf16[128,256]{1,0:T(8,128)(2,1)S(1)}, u32[]{:S(2)}, u32[]{:S(2)}) collective-permute-start(bf16[128,256]{1,0:T(8,128)(2,1)} %param.7), channel_id=1, source_target_pairs={{0,0},{1,8},{2,16},{3,24},{4,32},{5,40},{6,48},{7,56},{8,64},{9,72... | collective-permute-start | bytes 196616 | tf_op jit(solution)/shard_map/ppermute | solution.py:32
  23.5 5.8 %collective-permute-start.1 = (bf16[128,256]{1,0:T(8,128)(2,1)}, bf16[128,256]{1,0:T(8,128)(2,1)S(1)}, u32[]{:S(2)}, u32[]{:S(2)}) collective-permute-start(bf16[128,256]{1,0:T(8,128)(2,1)} %param.7), channel_id=1, source_target_pairs={{0,8},{1,0},{2,24},{3,16},{4,40},{5,32},{6,56},{7,48},{8,72},{9,64... | collective-permute-start | bytes 196616 | tf_op jit(solution)/shard_map/ppermute | solution.py:33
  30.4 26.7 %all-to-all-start = ((bf16[8,128,512]{2,1,0:T(8,128)(2,1)}), bf16[8,128,512]{2,1,0:T(8,128)(2,1)S(1)}, u32[]{:S(2)}, u32[]{:S(2)}) async-start(bf16[8,128,512]{2,1,0:T(8,128)(2,1)} %tile.6), calls=%async_computation | async-start | bytes 2097152 | tf_op jit(solution)/shard_map/all_to_all | solution.py:37
  42.0 97.5 %reduce-scatter.2.cloned.1.call-start = ((), (), s32[]{:S(2)}) async-start(), calls=%async_computation.4 | async-start | bytes 3538944 | tf_op jit(solution)/shard_map/reduce_scatter | solution.py:43
  59.7 1.1 copy-start.1
  59.7 1.1 copy-start.2
  59.7 1.4 copy-start.3
  167.6 22.8 %all-to-all-start.2 = ((bf16[8,128,512]{1,2,0:T(8,128)(2,1)}), bf16[8,128,512]{1,2,0:T(8,128)(2,1)S(1)}, u32[]{:S(2)}, u32[]{:S(2)}) async-start(bf16[8,128,512]{1,2,0:T(8,128)(2,1)} %tile.8), calls=%async_computation.3 | async-start | bytes 2097152 | tf_op jit(solution)/shard_map/all_to_all | solution.py:98
Sparse Core Ops, SparseCore 0:
  59.9 79.5 reduce-scatter.1
